TPU v7x, 256 devices: a whole 4x4x8 slice. The times are simulated.
256 devices in a mesh: proto: 4 (over y), batch: 64 (over x, z, core).
Axes of the slice: x: 4, y: 4, z: 8, core: 2. Of those that a mesh axis runs over, the one named last changes fastest.
Arguments:
- teacher: bfloat16 [32768, 256], P(('proto', 'batch')), may hold values from -6 to 6
- student: bfloat16 [32768, 256], P(('proto', 'batch')), may hold values from -6 to 6
- prototypes: bfloat16 [32768, 256], P('proto'), may hold values from -6 to 6
Outputs:
- grad_student: float32 [32768, 256], P(('proto', 'batch'))
- grad_protos: float32 [32768, 256], P(('proto', 'batch'))
All inputs are finite; a program needn't handle non-finite values.
Results may differ from a plain program's by a relative error of at most 0.0042.
Values may be sent and summed in bfloat16 or wider, within the bound.
No kernel may reach another device: no remote copies, remote signals or barrier semaphores. Data moves between devices by JAX's collectives and lax.ppermute only.
A program may use at most 192 MiB of HBM per device.

v0:
```python
import math

import jax
import jax.numpy as jnp
from jax import lax
from jax.sharding import PartitionSpec as P

ITERS = 3


teacher_temp = 0.05
student_temp = 0.1


def side_by_side(arrays, axis, dim, along):
    ends, at = ([], 0)
    for a in arrays[:-1]:
        at += a.shape[along]
        ends.append(at)
    both = jnp.concatenate(arrays, axis=along)
    return tuple(jnp.split(lax.all_gather(both, axis, axis=dim, tiled=True), ends, axis=along))


def cut_along(value, dim, length):
    lengths = value.shape
    parts = value.reshape(*lengths[:dim], length, lengths[dim] // length, *lengths[dim + 1 :])
    return jnp.moveaxis(parts, dim, 0)


def summed_on_arrival(value, axis, dim):
    parts = cut_along(value, dim, lax.axis_size(axis))
    arrived = lax.all_to_all(parts, axis, split_axis=0, concat_axis=0, tiled=True)
    return arrived.sum(axis=0)


def laid_out(parts, dim):
    parts = jnp.moveaxis(parts, 0, dim)
    lengths = parts.shape
    return parts.reshape(*lengths[:dim], lengths[dim] * lengths[dim + 1], *lengths[dim + 2 :])


def copy_for_each(value, axis):
    copies = jnp.broadcast_to(value, (lax.axis_size(axis), *value.shape))
    return lax.all_to_all(copies, axis, split_axis=0, concat_axis=0, tiled=True)


def gather_directly(value, axis, dim):
    return laid_out(copy_for_each(value, axis), dim)


def over_copies(value, axis):
    return copy_for_each(value, axis).sum(axis=0)


def gather_turned(arrays, axis, dims):
    turned = [jnp.moveaxis(a, dim, 0) for a, dim in zip(arrays, dims)]
    widths = [t[0].size for t in turned]
    both = jnp.concatenate([t.reshape(-1, w) for t, w in zip(turned, widths)], axis=1)
    out = lax.all_gather(both, axis, axis=0, tiled=True)
    parts = jnp.split(out, [sum(widths[:k]) for k in range(1, len(widths))], axis=1)
    return tuple(
        (
            jnp.moveaxis(b.reshape(-1, *t.shape[1:]), 0, dim)
            for b, t, dim in zip(parts, turned, dims)
        )
    )


def unit_rows(value):
    full = value.astype(jnp.float32)
    return (
        full
        * lax.rsqrt(jnp.mean(full * full, axis=1, keepdims=True) + 1e-06)
        / math.sqrt(value.shape[1])
    )


def against(left, right):
    return lax.dot_general(
        left, right, (((1,), (1,)), ((), ())), preferred_element_type=jnp.float32
    )


def per_device(teacher, student, prototypes):
    n_proto = lax.axis_size("proto")
    n_batch = lax.axis_size("batch")
    own_rows = teacher.shape[0]
    count_all = prototypes.shape[0] * n_proto
    rows_all = own_rows * n_proto * n_batch
    tn = unit_rows(teacher).astype(jnp.bfloat16)
    sn = unit_rows(student).astype(jnp.bfloat16)
    cn = unit_rows(prototypes).astype(jnp.bfloat16)
    tn_group, sn_group = side_by_side((tn, sn), "proto", 0, 1)
    weight = jnp.exp(against(tn_group, cn) / teacher_temp)
    row_scale = jnp.ones((tn_group.shape[0],), jnp.float32)
    col_scale = None
    for step in range(ITERS):
        mass_local = jnp.sum(weight * row_scale[:, None], axis=0)
        share = summed_on_arrival(mass_local, "batch", 0)
        col_scale = gather_directly(1.0 / (count_all * share), "batch", 0)
        sample_local = jnp.sum(weight * col_scale[None, :], axis=1)
        row_scale = 1.0 / (rows_all * over_copies(sample_local, "proto"))
    targets = rows_all * weight * row_scale[:, None] * col_scale[None, :]
    logits = against(sn_group, cn) / student_temp
    logz = jnp.log(over_copies(jnp.sum(jnp.exp(logits), axis=1), "proto"))
    logp = logits - logz[:, None]
    scale = 16.0 * math.sqrt(count_all)
    grads = (scale * (jnp.exp(logp) - targets)).astype(jnp.bfloat16)
    grad_sn = summed_on_arrival(
        jnp.dot(grads, cn, preferred_element_type=jnp.float32) / student_temp, "proto", 0
    )
    _, pull = jax.vjp(unit_rows, student.astype(jnp.float32))
    grad_student = pull(grad_sn)[0]
    mine_rows = prototypes.shape[0] // n_batch
    offset = lax.axis_index("batch") * mine_rows
    c_mine = lax.dynamic_slice_in_dim(cn, offset, mine_rows, 0)
    col_mine = lax.dynamic_slice_in_dim(col_scale, offset, mine_rows, 0)
    all_scale, all_logz = gather_turned((row_scale, logz), "batch", (0, 0))
    t_piece, s_piece = side_by_side((tn_group, sn_group), "batch", 0, 1)
    target = (
        rows_all
        * jnp.exp(against(t_piece, c_mine) / teacher_temp)
        * all_scale[:, None]
        * col_mine[None, :]
    )
    probs = jnp.exp(against(s_piece, c_mine) / student_temp - all_logz[:, None])
    local_grads = (scale * (probs - target)).astype(jnp.bfloat16)
    grad_protos = (
        lax.dot_general(
            local_grads, s_piece, (((0,), (0,)), ((), ())), preferred_element_type=jnp.float32
        )
        / student_temp
    )
    return (grad_student, grad_protos)


def solution(mesh):
    return jax.shard_map(
        per_device,
        mesh=mesh,
        in_specs=(P(("proto", "batch"), None), P(("proto", "batch"), None), P("proto", None)),
        out_specs=(P(("proto", "batch"), None), P(("proto", "batch"), None)),
        check_vma=False,
    )
```

profile of v0, /device:TPU:1, one launch (start us, length us, event | category | flops | bytes accessed | tf_op | source)
XLA Modules:
  0.0 313.6 jit_solution(17253044793922192107)
XLA Ops:
  7.2 0.9 fusion.23
  8.2 1.0 fusion.26
  9.1 1.0 fusion.25
  10.1 13.0 %all_gather.9 = bf16[512,512]{1,0:T(8,128)(2,1)} all-gather(bf16[128,512]{1,0:T(8,128)(2,1)S(1)} %pad_maximum_fusion), channel_id=1, replica_groups=mesh['proto'=4,'batch'=64] {'proto'}, dimensions={0}, use_global_device_ids=true | all-gather | bytes 655360 | tf_op jit(solution)/shard_map/all_gather | solution.py:21
  23.1 3.3 %fusion.12 = f32[8192]{0:T(1024)S(1)} fusion(bf16[8192,256]{1,0:T(8,128)(2,1)} %param.5), kind=kLoop, calls=%fused_computation.24 | loop fusion | flops 6283264 | bytes 4227072 | tf_op jit(solution)/shard_map/reduce_sum | solution.py:73
  26.5 2.9 fusion.14
  29.4 2.0 copy-done
  31.4 8.0 %fusion.45 = (f32[8192]{0:T(1024)S(1)}, f32[512,8192]{1,0:T(8,128)}) fusion(bf16[8192,256]{1,0:T(8,128)(2,1)S(1)} %fusion.14, bf16[512,512]{1,0:T(8,128)(2,1)} %all_gather.9), kind=kOutput, calls=%fused_computation.72 | convolution fusion | flops 2155864064 | bytes 21266432 | tf_op jit(solution)/shard_map/dot_general | solution.py:79
  39.3 23.4 %all_to_all.74 = f32[64,1,128]{2,1,0:T(1,128)S(1)} all-to-all(f32[64,1,128]{2,1,0:T(1,128)S(1)} %bitcast.20), channel_id=1, replica_groups=mesh['proto'=4,'batch'=64] {'batch'}, dimensions={0} | all-to-all | bytes 65536 | tf_op jit(solution)/shard_map/all_to_all | solution.py:32
  62.8 13.4 %all_to_all.75 = f32[64,1,128]{2,1,0:T(1,128)S(1)} all-to-all(f32[64,1,128]{2,1,0:T(1,128)S(1)} %broadcast_in_dim.34), channel_id=1, replica_groups=mesh['proto'=4,'batch'=64] {'batch'}, dimensions={0} | all-to-all | bytes 65536 | tf_op jit(solution)/shard_map/all_to_all | solution.py:44
  76.3 7.3 %multiply_reduce_fusion.4 = f32[512]{0:T(512)S(1)} fusion(f32[512,8192]{1,0:T(8,128)} %get-tuple-element.9, f32[8192]{0:T(1024)S(1)} %bitcast.21), kind=kLoop, calls=%fused_computation.16 | loop fusion | flops 8388096 | bytes 16812032 | tf_op jit(solution)/shard_map/reduce_sum | solution.py:101
  83.5 8.1 %all_to_all.76 = f32[4,1,512]{2,1,0:T(1,128)S(1)} all-to-all(f32[4,1,512]{2,1,0:T(1,128)S(1)} %broadcast_in_dim.35), channel_id=1, replica_groups=mesh['proto'=4,'batch'=64] {'proto'}, dimensions={0} | all-to-all | bytes 16384 | tf_op jit(solution)/shard_map/all_to_all | solution.py:44
  91.7 8.7 %multiply_reduce_fusion.3 = f32[8192]{0:T(1024)S(1)} fusion(f32[512,8192]{1,0:T(8,128)} %get-tuple-element.9, f32[512]{0:T(512)S(1)} %multiply_divide_fusion.2), kind=kLoop, calls=%fused_computation.15 | loop fusion | flops 8380416 | bytes 16812032 | tf_op jit(solution)/shard_map/reduce_sum | solution.py:98
  100.3 15.0 %all_to_all.77 = f32[64,1,128]{2,1,0:T(1,128)S(1)} all-to-all(f32[64,1,128]{2,1,0:T(1,128)S(1)} %bitcast.22), channel_id=1, replica_groups=mesh['proto'=4,'batch'=64] {'batch'}, dimensions={0} | all-to-all | bytes 65536 | tf_op jit(solution)/shard_map/all_to_all | solution.py:32
  115.4 13.6 %all_to_all.78 = f32[64,1,128]{2,1,0:T(1,128)S(1)} all-to-all(f32[64,1,128]{2,1,0:T(1,128)S(1)} %broadcast_in_dim.36), channel_id=1, replica_groups=mesh['proto'=4,'batch'=64] {'batch'}, dimensions={0} | all-to-all | bytes 65536 | tf_op jit(solution)/shard_map/all_to_all | solution.py:44
  129.0 8.3 %multiply_reduce_fusion.2 = f32[512]{0:T(512)S(1)} fusion(f32[512,8192]{1,0:T(8,128)} %get-tuple-element.9, f32[8192]{0:T(1024)S(1)} %bitcast.23), kind=kLoop, calls=%fused_computation.14 | loop fusion | flops 8388096 | bytes 16812032 | tf_op jit(solution)/shard_map/reduce_sum | solution.py:101
  137.3 6.6 %all_to_all.79 = f32[4,1,512]{2,1,0:T(1,128)S(1)} all-to-all(f32[4,1,512]{2,1,0:T(1,128)S(1)} %broadcast_in_dim.37), channel_id=1, replica_groups=mesh['proto'=4,'batch'=64] {'proto'}, dimensions={0} | all-to-all | bytes 16384 | tf_op jit(solution)/shard_map/all_to_all | solution.py:44
  143.9 8.5 %multiply_reduce_fusion.1 = f32[8192]{0:T(1024)S(1)} fusion(f32[512,8192]{1,0:T(8,128)} %get-tuple-element.9, f32[512]{0:T(512)S(1)} %multiply_divide_fusion.1), kind=kLoop, calls=%fused_computation.13 | loop fusion | flops 8380416 | bytes 16812032 | tf_op jit(solution)/shard_map/reduce_sum | solution.py:98
  152.4 14.6 %all_to_all.80 = f32[64,1,128]{2,1,0:T(1,128)S(1)} all-to-all(f32[64,1,128]{2,1,0:T(1,128)S(1)} %bitcast.24), channel_id=1, replica_groups=mesh['proto'=4,'batch'=64] {'batch'}, dimensions={0} | all-to-all | bytes 65536 | tf_op jit(solution)/shard_map/all_to_all | solution.py:32
  167.1 0.6 broadcast_in_dim.38
  167.7 4.6 %all-to-all-start.8 = ((f32[64,1,128]{2,1,0:T(1,128)}), f32[64,1,128]{2,1,0:T(1,128)S(1)}, u32[]{:S(2)}, u32[]{:S(2)}) async-start(f32[64,1,128]{2,1,0:T(1,128)} %broadcast_in_dim.38), calls=%async_computation.8 | async-start | bytes 65536 | tf_op jit(solution)/shard_map/all_to_all | solution.py:44
  172.3 9.3 %exponential_reduce_fusion = (f32[512]{0:T(512)S(1)}, f32[512,8192]{1,0:T(8,128)}) fusion(bf16[8192,256]{1,0:T(8,128)(2,1)} %copy-done, bf16[512,512]{1,0:T(8,128)(2,1)S(1)} %copy-done.1), kind=kOutput, calls=%fused_computation.18 | convolution fusion | flops 2155871744 | bytes 21235712 | tf_op jit(solution)/shard_map/dot_general | solution.py:79
  182.3 3.2 %all-to-all-start = ((f32[4,1,512]{2,1,0:T(1,128)}), f32[4,1,512]{2,1,0:T(1,128)S(1)}, u32[]{:S(2)}, u32[]{:S(2)}) async-start(f32[4,1,512]{2,1,0:T(1,128)} %broadcast_in_dim.16), calls=%async_computation | async-start | bytes 16384 | tf_op jit(solution)/shard_map/all_to_all | solution.py:44
  185.6 7.0 %multiply_reduce_fusion = f32[512]{0:T(512)S(1)} fusion(f32[512,8192]{1,0:T(8,128)} %get-tuple-element.9, f32[8192]{0:T(1024)S(1)} %bitcast.17), kind=kLoop, calls=%fused_computation.12 | loop fusion | flops 8388096 | bytes 16812032 | tf_op jit(solution)/shard_map/reduce_sum | solution.py:101
  193.2 4.2 %all-to-all-start.9 = ((f32[4,1,512]{2,1,0:T(1,128)}), f32[4,1,512]{2,1,0:T(1,128)S(1)}, u32[]{:S(2)}, u32[]{:S(2)}) async-start(f32[4,1,512]{2,1,0:T(1,128)} %broadcast_in_dim.39), calls=%async_computation.9 | async-start | bytes 16384 | tf_op jit(solution)/shard_map/all_to_all | solution.py:44
  197.5 4.1 %all-to-all-done.9 = f32[4,1,512]{2,1,0:T(1,128)S(1)} async-done(((f32[4,1,512]{2,1,0:T(1,128)}), f32[4,1,512]{2,1,0:T(1,128)S(1)}, u32[]{:S(2)}, u32[]{:S(2)}) %all-to-all-start.9) | async-done | bytes 8224 | tf_op jit(solution)/shard_map/all_to_all | solution.py:44
  201.6 15.1 %fusion.16 = f32[512,256]{1,0:T(8,128)} fusion(bf16[8192,256]{1,0:T(8,128)(2,1)} %copy-done, f32[512,8192]{1,0:T(8,128)} %get-tuple-element.9, f32[512,8192]{1,0:T(8,128)} %get-tuple-element.11, f32[512]{0:T(512)S(1)} %get-tuple-element.2, f32[8192]{0:T(1024)S(1)} %bitcast.19, f32[512]{0:T(512)S(1)} %log.14), kind=kOutput, calls=%fused_computation.28 | convolution fusion | flops 2176974848 | bytes 38309888 | tf_op jit(solution)/shard_map/dot_general | solution.py:110
  216.7 3.5 %all-to-all-start.10 = ((f32[4,128,256]{2,1,0:T(8,128)}), f32[4,128,256]{2,1,0:T(8,128)S(1)}, u32[]{:S(2)}, u32[]{:S(2)}) async-start(f32[4,128,256]{2,1,0:T(8,128)} %bitcast.9), calls=%async_computation.10 | async-start | bytes 1048576 | tf_op jit(solution)/shard_map/all_to_all | solution.py:32
  220.2 47.3 %all_gather.11 = f32[32768,2]{0,1:T(2,128)S(1)} all-gather(f32[512,2]{0,1:T(2,128)S(1)} %pad_maximum_fusion.1), channel_id=1, replica_groups=mesh['proto'=4,'batch'=64] {'batch'}, dimensions={0}, use_global_device_ids=true | all-gather | bytes 266240 | tf_op jit(solution)/shard_map/all_gather | solution.py:59
  267.9 0.8 add_add_fusion
  268.6 18.2 %fusion.2 = f32[32768,128]{1,0:T(8,128)} fusion(bf16[32768,512]{1,0:T(8,128)(2,1)} %all-gather.2.cloned.1.call-done, f32[128]{0:T(128)S(1)} %dynamic_slice.7, f32[32768]{0:T(1024)S(1)} %bitcast.29, bf16[8192,256]{1,0:T(8,128)(2,1)} %copy-done, s32[]{:T(128)S(6)} %select_n.4), kind=kOutput, calls=%fused_computation.3 | convolution fusion | flops 2160066560 | bytes 33751556 | tf_op jit(solution)/shard_map/dot_general | solution.py:79
  286.9 19.9 %fusion.17 = f32[128,256]{1,0:T(8,128)} fusion(bf16[32768,512]{1,0:T(8,128)(2,1)} %all-gather.2.cloned.1.call-done, f32[32768,128]{1,0:T(8,128)} %fusion.2, f32[32768]{0:T(1024)S(1)} %bitcast.28, bf16[8192,256]{1,0:T(8,128)(2,1)} %copy-done, s32[]{:T(128)S(6)} %select_n.4), kind=kOutput, calls=%fused_computation.29 | convolution fusion | flops 4315971584 | bytes 50659332 | tf_op jit(solution)/shard_map/dot_general | solution.py:129
  (41 shorter events, 2.1 us)
Async XLA Ops:
  7.2 261.5 %all-gather.2.cloned.1.call-start = ((), (), s32[]{:S(2)}) async-start(), calls=%async_computation.11 | async-start | bytes 34078720 | tf_op jit(solution)/shard_map/all_gather | solution.py:21
  29.4 2.0 copy-start
  129.0 43.4 %copy-start.1 = (bf16[512,512]{1,0:T(8,128)(2,1)S(1)}, bf16[512,512]{1,0:T(8,128)(2,1)}, u32[]{:S(2)}) copy-start(bf16[512,512]{1,0:T(8,128)(2,1)} %all_gather.9) | copy-start | bytes 1572868
  167.7 14.0 %all-to-all-start.8 = ((f32[64,1,128]{2,1,0:T(1,128)}), f32[64,1,128]{2,1,0:T(1,128)S(1)}, u32[]{:S(2)}, u32[]{:S(2)}) async-start(f32[64,1,128]{2,1,0:T(1,128)} %broadcast_in_dim.38), calls=%async_computation.8 | async-start | bytes 65536 | tf_op jit(solution)/shard_map/all_to_all | solution.py:44
  182.3 10.3 %all-to-all-start = ((f32[4,1,512]{2,1,0:T(1,128)}), f32[4,1,512]{2,1,0:T(1,128)S(1)}, u32[]{:S(2)}, u32[]{:S(2)}) async-start(f32[4,1,512]{2,1,0:T(1,128)} %broadcast_in_dim.16), calls=%async_computation | async-start | bytes 16384 | tf_op jit(solution)/shard_map/all_to_all | solution.py:44
  193.2 8.4 %all-to-all-start.9 = ((f32[4,1,512]{2,1,0:T(1,128)}), f32[4,1,512]{2,1,0:T(1,128)S(1)}, u32[]{:S(2)}, u32[]{:S(2)}) async-start(f32[4,1,512]{2,1,0:T(1,128)} %broadcast_in_dim.39), calls=%async_computation.9 | async-start | bytes 16384 | tf_op jit(solution)/shard_map/all_to_all | solution.py:44
  201.6 66.2 %copy-start.2 = (bf16[128,256]{1,0:T(8,128)(2,1)S(1)}, bf16[128,256]{1,0:T(8,128)(2,1)}, u32[]{:S(2)}) copy-start(bf16[128,256]{1,0:T(8,128)(2,1)} %param.4) | copy-start | bytes 196612
  216.7 51.0 %all-to-all-start.10 = ((f32[4,128,256]{2,1,0:T(8,128)}), f32[4,128,256]{2,1,0:T(8,128)S(1)}, u32[]{:S(2)}, u32[]{:S(2)}) async-start(f32[4,128,256]{2,1,0:T(8,128)} %bitcast.9), calls=%async_computation.10 | async-start | bytes 1048576 | tf_op jit(solution)/shard_map/all_to_all | solution.py:32
Sparse Core Ops, SparseCore 0:
  23.3 149.1 all-gather.1
where the time goes:
time: 315 us; the launch traced here: 314 us
  blocking collectives  155 us (49%)
  matrix products  70.6 us (22%)
  other arithmetic  50.2 us (16%)
  starting transfers between devices  15.6 us (5%)
  between operations  14.2 us (5%)
  waiting for transfers between devices  4.11 us (1%)
  local copies, waits for them, and re-layouts  3.97 us (1%)
    all_to_all x3, blocking collectives, summed_on_arrival(): lax.all_to_all(parts, axis, split_axis=0, concat_axis=0, tiled=True)  53 us
    all_gather x1, blocking collectives, gather_turned(): out = lax.all_gather(both, axis, axis=0, tiled=True)  47.3 us
    all_to_all x4, blocking collectives, copy_for_each(): return lax.all_to_all(copies, axis, split_axis=0, concat_axis=0, tiled=True)  41.7 us
    dot_general x3, matrix products, against(): lax.dot_general(left, right, (((1,), (1,)), ((), ())), preferred_element_...  35.5 us
    reduce_sum x3, other arithmetic, per_device(): sample_local = jnp.sum(weight * col_scale[None, :], axis=1)  22.6 us
    dot_general x1, matrix products, per_device(): lax.dot_general(local_grads, s_piece, (((0,), (0,)), ((), ())), preferred...  19.9 us
    reduce_sum x2, other arithmetic, per_device(): mass_local = jnp.sum(weight * row_scale[:, None], axis=0)  17.2 us
    dot_general x1, matrix products, per_device(): jnp.dot(grads, cn, preferred_element_type=jnp.float32) / student_temp  15.1 us
  transfers between devices with their start and end apart: 5, of which 1 were waited for; matrix products, arithmetic and copies ran while one was open for 26% of the time, Pallas kernels for 0%

commit v1 on v0

v1 whole, which is shorter than its diff:
```python
import math

import jax
import jax.numpy as jnp
from jax import lax
from jax.sharding import PartitionSpec as P

ITERS = 3


teacher_temp = 0.05
student_temp = 0.1


def side_by_side(arrays, axis, dim, along):
    ends, at = ([], 0)
    for a in arrays[:-1]:
        at += a.shape[along]
        ends.append(at)
    both = jnp.concatenate(arrays, axis=along)
    return tuple(jnp.split(lax.all_gather(both, axis, axis=dim, tiled=True), ends, axis=along))


def unit_rows(value):
    full = value.astype(jnp.float32)
    return (
        full
        * lax.rsqrt(jnp.mean(full * full, axis=1, keepdims=True) + 1e-06)
        / math.sqrt(value.shape[1])
    )


def against(left, right):
    return lax.dot_general(
        left, right, (((1,), (1,)), ((), ())), preferred_element_type=jnp.float32
    )


def per_device(teacher, student, prototypes):
    n_proto = lax.axis_size("proto")
    n_batch = lax.axis_size("batch")
    own_rows = teacher.shape[0]
    count_all = prototypes.shape[0] * n_proto
    rows_all = own_rows * n_proto * n_batch
    tn = unit_rows(teacher).astype(jnp.bfloat16)
    sn = unit_rows(student).astype(jnp.bfloat16)
    cn = unit_rows(prototypes).astype(jnp.bfloat16)
    tn_group, sn_group = side_by_side((tn, sn), "proto", 0, 1)
    weight = jnp.exp(against(tn_group, cn) / teacher_temp)
    row_scale = jnp.ones((tn_group.shape[0],), jnp.float32)
    col_scale = None
    for step in range(ITERS):
        mass_local = jnp.sum(weight * row_scale[:, None], axis=0)
        col_scale = 1.0 / (count_all * lax.psum(mass_local, "batch"))
        sample_local = jnp.sum(weight * col_scale[None, :], axis=1)
        row_scale = 1.0 / (rows_all * lax.psum(sample_local, "proto"))
    targets = rows_all * weight * row_scale[:, None] * col_scale[None, :]
    logits = against(sn_group, cn) / student_temp
    logz = jnp.log(lax.psum(jnp.sum(jnp.exp(logits), axis=1), "proto"))
    logp = logits - logz[:, None]
    scale = 16.0 * math.sqrt(count_all)
    grads = (scale * (jnp.exp(logp) - targets)).astype(jnp.bfloat16)
    grad_sn = lax.psum_scatter(
        jnp.dot(grads, cn, preferred_element_type=jnp.float32) / student_temp,
        "proto",
        scatter_dimension=0,
        tiled=True,
    )
    _, pull = jax.vjp(unit_rows, student.astype(jnp.float32))
    grad_student = pull(grad_sn)[0]
    proto_partial = (
        lax.dot_general(
            grads, sn_group, (((0,), (0,)), ((), ())), preferred_element_type=jnp.float32
        )
        / student_temp
    )
    grad_protos = lax.psum_scatter(proto_partial, "batch", scatter_dimension=0, tiled=True)
    return (grad_student, grad_protos)


def solution(mesh):
    return jax.shard_map(
        per_device,
        mesh=mesh,
        in_specs=(P(("proto", "batch"), None), P(("proto", "batch"), None), P("proto", None)),
        out_specs=(P(("proto", "batch"), None), P(("proto", "batch"), None)),
        check_vma=False,
    )
```

time: 315 us -> 1050 us (3.33)
  blocking collectives: 155 us -> 778 us
  waiting for transfers between devices: 4.11 us -> 164 us
  matrix products: 70.6 us -> 28.8 us
  starting transfers between devices: 15.6 us -> 0.08 us
    psum x0 -> x6, blocking collectives: none -> 765 us  [the longest x3 745 us: per_device(): col_scale = 1.0 / (count_all * lax.psum(mass_local, 'batch'))]
    reduce_scatter x0 -> x2, waiting for transfers between devices: none -> 164 us  [the longest x1 152 us: per_device(): lax.psum_scatter(proto_partial, 'batch', scatter_dimension=0, tiled=True)]
    all_to_all x7 -> x0, blocking collectives: 94.7 us -> none  [the longest x3 53 us: summed_on_arrival(): lax.all_to_all(parts, axis, split_axis=0, concat_axis=0, tiled=True)]
    all_gather x1 -> x0, blocking collectives: 47.3 us -> none  [gather_turned(): out = lax.all_gather(both, axis, axis=0, tiled=True)]
    dot_general x3 -> x2, matrix products: 35.5 us -> 16.5 us  [against(): lax.dot_general(left, right, (((1,), (1,)), ((), ())), preferred_element_...]
    all_to_all x4 -> x0, starting transfers between devices: 15.5 us -> none  [the longest x3 12.1 us: copy_for_each(): return lax.all_to_all(copies, axis, split_axis=0, concat_axis=0, tiled=True)]
    dot_general x1, matrix products: 15.1 us -> 3.31 us  [per_device(): jnp.dot(grads, cn, preferred_element_type=jnp.float32) / student_temp]
    dot_general x1, matrix products: 19.9 us -> 9 us  [per_device(): lax.dot_general(grads, sn_group, (((0,), (0,)), ((), ())), preferred_elem...]
  transfers between devices with their start and end apart: 5 -> 2, of which waited for: 1 -> 2; matrix products, arithmetic and copies ran while one was open for 26% -> 1% of each run, Pallas kernels for 0% -> 0%
where the time goes in v1:
time: 1050 us
  blocking collectives  778 us (74%)
  waiting for transfers between devices  164 us (16%)
  other arithmetic  59.4 us (6%)
  matrix products  28.8 us (3%)
  between operations  14.2 us (1%)
    psum x3, blocking collectives, per_device(): col_scale = 1.0 / (count_all * lax.psum(mass_local, 'batch'))  745 us
    reduce_scatter x1, waiting for transfers between devices, per_device(): lax.psum_scatter(proto_partial, 'batch', scatter_dimension=0, tiled=True)  152 us
    reduce_sum x3, other arithmetic, per_device(): sample_local = jnp.sum(weight * col_scale[None, :], axis=1)  21.5 us
  transfers between devices with their start and end apart: 2, of which 2 were waited for; matrix products, arithmetic and copies ran while one was open for 1% of the time, Pallas kernels for 0%

profile of v1, /device:TPU:1, one launch (start us, length us, event | category | flops | bytes accessed | tf_op | source)
XLA Modules:
  0.0 1047.4 jit_solution(5188379753464744590)
XLA Ops:
  7.2 0.0 reduce-scatter.3.cloned.1.call-start
  7.2 0.9 fusion.10
  8.2 1.0 fusion.7
  9.1 3.4 fusion
  12.5 1.0 fusion.9
  13.5 12.6 %all_gather.3 = bf16[512,512]{1,0:T(8,128)(2,1)S(1)} all-gather(bf16[128,512]{1,0:T(8,128)(2,1)S(1)} %pad_maximum_fusion), channel_id=1, replica_groups=mesh['proto'=4,'batch'=64] {'proto'}, dimensions={0}, use_global_device_ids=true | all-gather | bytes 655360 | tf_op jit(solution)/shard_map/all_gather | solution.py:21
  26.1 9.4 exponential_reduce_fusion
  35.5 0.0 copy-done.1
  35.5 7.1 fusion.18
  42.6 248.6 %psum.50 = f32[8192]{0:T(1024)S(1)} all-reduce(f32[8192]{0:T(1024)S(1)} %get-tuple-element.6), channel_id=1, replica_groups=mesh['proto'=4,'batch'=64] {'batch'}, use_global_device_ids=true, to_apply=%region_6.0 | all-reduce | flops 8192 | bytes 65536 | tf_op jit(solution)/shard_map/psum | solution.py:54
  291.2 7.3 multiply_reduce_fusion.4
  298.5 6.9 psum.51
  305.3 8.3 multiply_reduce_fusion.3
  313.6 248.2 %psum.52 = f32[8192]{0:T(1024)S(1)} all-reduce(f32[8192]{0:T(1024)S(1)} %multiply_reduce_fusion.3), channel_id=1, replica_groups=mesh['proto'=4,'batch'=64] {'batch'}, use_global_device_ids=true, to_apply=%region_10.0 | all-reduce | flops 8192 | bytes 65536 | tf_op jit(solution)/shard_map/psum | solution.py:54
  561.8 7.3 multiply_reduce_fusion.2
  569.1 6.8 psum.53
  575.9 8.3 multiply_reduce_fusion.1
  584.2 248.2 %psum.54 = f32[8192]{0:T(1024)S(1)} all-reduce(f32[8192]{0:T(1024)S(1)} %multiply_reduce_fusion.1), channel_id=1, replica_groups=mesh['proto'=4,'batch'=64] {'batch'}, use_global_device_ids=true, to_apply=%region_14.0 | all-reduce | flops 8192 | bytes 65536 | tf_op jit(solution)/shard_map/psum | solution.py:54
  832.3 7.0 multiply_reduce_fusion
  839.3 6.9 all-reduce
  846.2 12.3 %multiply_convert_fusion = bf16[512,8192]{1,0:T(8,128)(2,1)S(1)} fusion(f32[512,8192]{1,0:T(8,128)} %get-tuple-element.7, f32[512,8192]{1,0:T(8,128)} %get-tuple-element.9, f32[512]{0:T(512)S(1)} %divide_multiply_fusion, f32[8192]{0:T(1024)S(1)} %multiply_divide_fusion, f32[512]{0:T(512)S(1)} %log.3), kind=kLoop, calls=%fused_computation | loop fusion | flops 29360128 | bytes 41979904 | tf_op jit(solution)/shard_map/convert_element_type | solution.py:62
  858.5 3.2 copy-done
  861.7 0.0 copy-done.2
  861.7 3.3 convolution_multiply_fusion.1
  865.0 0.0 reduce-scatter.3.cloned.1.call-update
  865.1 0.0 reduce-scatter.5.cloned.1.call-start
  865.1 9.0 convolution_multiply_fusion
  874.1 0.0 reduce-scatter.5.cloned.1.call-update
  874.1 11.5 %reduce-scatter.3.cloned.1.call-done = f32[128,256]{1,0:T(8,128)} async-done(((f32[512,256]{1,0:T(8,128)}), f32[128,256]{1,0:T(8,128)}) %reduce-scatter.3.cloned.1.call-update) | async-done | bytes 131088 | tf_op jit(solution)/shard_map/reduce_scatter | solution.py:63
  885.6 1.0 fusion.13
  886.7 1.7 add_add_fusion
  888.3 152.2 %reduce-scatter.5.cloned.1.call-done = f32[128,256]{1,0:T(8,128)} async-done(((f32[8192,256]{1,0:T(8,128)}), f32[128,256]{1,0:T(8,128)}) %reduce-scatter.5.cloned.1.call-update) | async-done | bytes 131088 | tf_op jit(solution)/shard_map/reduce_scatter | solution.py:77
  (17 shorter events, 0.1 us)
Async XLA Ops:
  7.2 878.5 %reduce-scatter.3.cloned.1.call-start = ((), (), s32[]{:S(2)}) async-start(), calls=%async_computation.2 | async-start | bytes 655360 | tf_op jit(solution)/shard_map/reduce_scatter | solution.py:63
  26.1 9.4 copy-start.1
  846.2 15.5 %copy-start.2 = (bf16[8192,256]{1,0:T(8,128)(2,1)S(1)}, bf16[8192,256]{1,0:T(8,128)(2,1)}, u32[]{:S(2)}) copy-start(bf16[8192,256]{1,0:T(8,128)(2,1)} %param.5) | copy-start | bytes 12582916
  858.5 3.2 copy-start
  865.1 175.5 %reduce-scatter.5.cloned.1.call-start = ((), (), s32[]{:S(2)}) async-start(), calls=%async_computation.3 | async-start | bytes 8519680 | tf_op jit(solution)/shard_map/reduce_scatter | solution.py:77
  874.1 11.5 %copy-start.3 = (bf16[128,256]{1,0:T(8,128)(2,1)S(1)}, bf16[128,256]{1,0:T(8,128)(2,1)}, u32[]{:S(2)}) copy-start(bf16[128,256]{1,0:T(8,128)(2,1)} %param.4) | copy-start | bytes 196612
Sparse Core Ops, SparseCore 0:
  865.2 20.4 reduce-scatter.2
  890.4 150.0 reduce-scatter.4

commit v2 on v0

--- a/solution.py
+++ b/solution.py
@@ -115,7 +115,8 @@
     offset = lax.axis_index("batch") * mine_rows
     c_mine = lax.dynamic_slice_in_dim(cn, offset, mine_rows, 0)
     col_mine = lax.dynamic_slice_in_dim(col_scale, offset, mine_rows, 0)
-    all_scale, all_logz = gather_turned((row_scale, logz), "batch", (0, 0))
+    both = gather_directly(jnp.stack([row_scale, logz], axis=1), "batch", 0)
+    all_scale, all_logz = both[:, 0], both[:, 1]
     t_piece, s_piece = side_by_side((tn_group, sn_group), "batch", 0, 1)
     target = (
         rows_all

time: 315 us -> 300 us (0.952)
  blocking collectives: 155 us -> 108 us
  waiting for transfers between devices: 4.11 us -> 22.1 us
  starting transfers between devices: 15.6 us -> 29.3 us
    all_gather x1 -> x0, blocking collectives: 47.3 us -> none  [gather_turned(): out = lax.all_gather(both, axis, axis=0, tiled=True)]
    all_to_all x3 -> x4, starting transfers between devices: 12.1 us -> 25.8 us  [copy_for_each(): return lax.all_to_all(copies, axis, split_axis=0, concat_axis=0, tiled=True)]
    all_to_all x3 -> x4, waiting for transfers between devices: 4.08 us -> 15.2 us  [copy_for_each(): return lax.all_to_all(copies, axis, split_axis=0, concat_axis=0, tiled=True)]
    all_to_all x1, waiting for transfers between devices: 0.01 us -> 6.83 us  [summed_on_arrival(): lax.all_to_all(parts, axis, split_axis=0, concat_axis=0, tiled=True)]
  transfers between devices with their start and end apart: 5 -> 6, of which waited for: 1 -> 3; matrix products, arithmetic and copies ran while one was open for 26% -> 28% of each run, Pallas kernels for 0% -> 0%
where the time goes in v2:
time: 300 us; the launch traced here: 299 us
  blocking collectives  108 us (36%)
  matrix products  70.6 us (24%)
  other arithmetic  50.2 us (17%)
  starting transfers between devices  29.3 us (10%)
  waiting for transfers between devices  22.1 us (7%)
  between operations  14.2 us (5%)
  local copies, waits for them, and re-layouts  4.74 us (2%)
    all_to_all x3, blocking collectives, summed_on_arrival(): lax.all_to_all(parts, axis, split_axis=0, concat_axis=0, tiled=True)  53 us
    all_to_all x4, blocking collectives, copy_for_each(): return lax.all_to_all(copies, axis, split_axis=0, concat_axis=0, tiled=True)  41.7 us
    dot_general x3, matrix products, against(): lax.dot_general(left, right, (((1,), (1,)), ((), ())), preferred_element_...  35.5 us
    all_to_all x4, starting transfers between devices, copy_for_each(): return lax.all_to_all(copies, axis, split_axis=0, concat_axis=0, tiled=True)  25.8 us
    reduce_sum x3, other arithmetic, per_device(): sample_local = jnp.sum(weight * col_scale[None, :], axis=1)  22.6 us
    dot_general x1, matrix products, per_device(): lax.dot_general(local_grads, s_piece, (((0,), (0,)), ((), ())), preferred...  19.9 us
    reduce_sum x2, other arithmetic, per_device(): mass_local = jnp.sum(weight * row_scale[:, None], axis=0)  17.2 us
    all_to_all x4, waiting for transfers between devices, copy_for_each(): return lax.all_to_all(copies, axis, split_axis=0, concat_axis=0, tiled=True)  15.2 us
  transfers between devices with their start and end apart: 6, of which 3 were waited for; matrix products, arithmetic and copies ran while one was open for 28% of the time, Pallas kernels for 0%

profile of v2, /device:TPU:1, one launch (start us, length us, event | category | flops | bytes accessed | tf_op | source)
XLA Modules:
  0.0 298.8 jit_solution(4938632157593564102)
XLA Ops:
  7.2 0.9 fusion.23
  8.2 1.0 fusion.26
  9.1 1.0 fusion.25
  10.1 13.0 %all_gather.6 = bf16[512,512]{1,0:T(8,128)(2,1)} all-gather(bf16[128,512]{1,0:T(8,128)(2,1)S(1)} %pad_maximum_fusion), channel_id=1, replica_groups=mesh['proto'=4,'batch'=64] {'proto'}, dimensions={0}, use_global_device_ids=true | all-gather | bytes 655360 | tf_op jit(solution)/shard_map/all_gather | solution.py:21
  23.1 3.3 %fusion.12 = f32[8192]{0:T(1024)S(1)} fusion(bf16[8192,256]{1,0:T(8,128)(2,1)} %param.5), kind=kLoop, calls=%fused_computation.24 | loop fusion | flops 6283264 | bytes 4227072 | tf_op jit(solution)/shard_map/reduce_sum | solution.py:73
  26.5 2.9 fusion.14
  29.4 2.0 copy-done
  31.4 8.0 %fusion.45 = (f32[8192]{0:T(1024)S(1)}, f32[512,8192]{1,0:T(8,128)}) fusion(bf16[8192,256]{1,0:T(8,128)(2,1)S(1)} %fusion.14, bf16[512,512]{1,0:T(8,128)(2,1)} %all_gather.6), kind=kOutput, calls=%fused_computation.72 | convolution fusion | flops 2155864064 | bytes 21266432 | tf_op jit(solution)/shard_map/dot_general | solution.py:79
  39.3 23.4 %all_to_all.79 = f32[64,1,128]{2,1,0:T(1,128)S(1)} all-to-all(f32[64,1,128]{2,1,0:T(1,128)S(1)} %bitcast.22), channel_id=1, replica_groups=mesh['proto'=4,'batch'=64] {'batch'}, dimensions={0} | all-to-all | bytes 65536 | tf_op jit(solution)/shard_map/all_to_all | solution.py:32
  62.8 13.4 %all_to_all.80 = f32[64,1,128]{2,1,0:T(1,128)S(1)} all-to-all(f32[64,1,128]{2,1,0:T(1,128)S(1)} %broadcast_in_dim.37), channel_id=1, replica_groups=mesh['proto'=4,'batch'=64] {'batch'}, dimensions={0} | all-to-all | bytes 65536 | tf_op jit(solution)/shard_map/all_to_all | solution.py:44
  76.3 7.3 %multiply_reduce_fusion.4 = f32[512]{0:T(512)S(1)} fusion(f32[512,8192]{1,0:T(8,128)} %get-tuple-element.9, f32[8192]{0:T(1024)S(1)} %bitcast.23), kind=kLoop, calls=%fused_computation.16 | loop fusion | flops 8388096 | bytes 16812032 | tf_op jit(solution)/shard_map/reduce_sum | solution.py:101
  83.5 8.1 %all_to_all.81 = f32[4,1,512]{2,1,0:T(1,128)S(1)} all-to-all(f32[4,1,512]{2,1,0:T(1,128)S(1)} %broadcast_in_dim.38), channel_id=1, replica_groups=mesh['proto'=4,'batch'=64] {'proto'}, dimensions={0} | all-to-all | bytes 16384 | tf_op jit(solution)/shard_map/all_to_all | solution.py:44
  91.7 8.7 %multiply_reduce_fusion.3 = f32[8192]{0:T(1024)S(1)} fusion(f32[512,8192]{1,0:T(8,128)} %get-tuple-element.9, f32[512]{0:T(512)S(1)} %multiply_divide_fusion.2), kind=kLoop, calls=%fused_computation.15 | loop fusion | flops 8380416 | bytes 16812032 | tf_op jit(solution)/shard_map/reduce_sum | solution.py:98
  100.3 15.0 %all_to_all.82 = f32[64,1,128]{2,1,0:T(1,128)S(1)} all-to-all(f32[64,1,128]{2,1,0:T(1,128)S(1)} %bitcast.24), channel_id=1, replica_groups=mesh['proto'=4,'batch'=64] {'batch'}, dimensions={0} | all-to-all | bytes 65536 | tf_op jit(solution)/shard_map/all_to_all | solution.py:32
  115.4 13.6 %all_to_all.83 = f32[64,1,128]{2,1,0:T(1,128)S(1)} all-to-all(f32[64,1,128]{2,1,0:T(1,128)S(1)} %broadcast_in_dim.39), channel_id=1, replica_groups=mesh['proto'=4,'batch'=64] {'batch'}, dimensions={0} | all-to-all | bytes 65536 | tf_op jit(solution)/shard_map/all_to_all | solution.py:44
  129.0 8.3 %multiply_reduce_fusion.2 = f32[512]{0:T(512)S(1)} fusion(f32[512,8192]{1,0:T(8,128)} %get-tuple-element.9, f32[8192]{0:T(1024)S(1)} %bitcast.25), kind=kLoop, calls=%fused_computation.14 | loop fusion | flops 8388096 | bytes 16812032 | tf_op jit(solution)/shard_map/reduce_sum | solution.py:101
  137.3 6.6 %all_to_all.84 = f32[4,1,512]{2,1,0:T(1,128)S(1)} all-to-all(f32[4,1,512]{2,1,0:T(1,128)S(1)} %broadcast_in_dim.40), channel_id=1, replica_groups=mesh['proto'=4,'batch'=64] {'proto'}, dimensions={0} | all-to-all | bytes 16384 | tf_op jit(solution)/shard_map/all_to_all | solution.py:44
  143.9 8.5 %multiply_reduce_fusion.1 = f32[8192]{0:T(1024)S(1)} fusion(f32[512,8192]{1,0:T(8,128)} %get-tuple-element.9, f32[512]{0:T(512)S(1)} %multiply_divide_fusion.1), kind=kLoop, calls=%fused_computation.13 | loop fusion | flops 8380416 | bytes 16812032 | tf_op jit(solution)/shard_map/reduce_sum | solution.py:98
  152.4 14.6 %all_to_all.85 = f32[64,1,128]{2,1,0:T(1,128)S(1)} all-to-all(f32[64,1,128]{2,1,0:T(1,128)S(1)} %bitcast.26), channel_id=1, replica_groups=mesh['proto'=4,'batch'=64] {'batch'}, dimensions={0} | all-to-all | bytes 65536 | tf_op jit(solution)/shard_map/all_to_all | solution.py:32
  167.7 4.6 %all-to-all-start.8 = ((f32[64,1,128]{2,1,0:T(1,128)}), f32[64,1,128]{2,1,0:T(1,128)S(1)}, u32[]{:S(2)}, u32[]{:S(2)}) async-start(f32[64,1,128]{2,1,0:T(1,128)} %broadcast_in_dim.41), calls=%async_computation.8 | async-start | bytes 65536 | tf_op jit(solution)/shard_map/all_to_all | solution.py:44
  172.3 9.3 %exponential_reduce_fusion = (f32[512]{0:T(512)S(1)}, f32[512,8192]{1,0:T(8,128)}) fusion(bf16[8192,256]{1,0:T(8,128)(2,1)} %copy-done, bf16[512,512]{1,0:T(8,128)(2,1)S(1)} %copy-done.1), kind=kOutput, calls=%fused_computation.18 | convolution fusion | flops 2155871744 | bytes 21235712 | tf_op jit(solution)/shard_map/dot_general | solution.py:79
  182.3 3.2 %all-to-all-start = ((f32[4,1,512]{2,1,0:T(1,128)}), f32[4,1,512]{2,1,0:T(1,128)S(1)}, u32[]{:S(2)}, u32[]{:S(2)}) async-start(f32[4,1,512]{2,1,0:T(1,128)} %broadcast_in_dim.36), calls=%async_computation | async-start | bytes 16384 | tf_op jit(solution)/shard_map/all_to_all | solution.py:44
  185.6 7.0 %multiply_reduce_fusion = f32[512]{0:T(512)S(1)} fusion(f32[512,8192]{1,0:T(8,128)} %get-tuple-element.9, f32[8192]{0:T(1024)S(1)} %bitcast.19), kind=kLoop, calls=%fused_computation.12 | loop fusion | flops 8388096 | bytes 16812032 | tf_op jit(solution)/shard_map/reduce_sum | solution.py:101
  193.2 4.2 %all-to-all-start.9 = ((f32[4,1,512]{2,1,0:T(1,128)}), f32[4,1,512]{2,1,0:T(1,128)S(1)}, u32[]{:S(2)}, u32[]{:S(2)}) async-start(f32[4,1,512]{2,1,0:T(1,128)} %broadcast_in_dim.42), calls=%async_computation.9 | async-start | bytes 16384 | tf_op jit(solution)/shard_map/all_to_all | solution.py:44
  197.4 4.1 %all-to-all-done.9 = f32[4,1,512]{2,1,0:T(1,128)S(1)} async-done(((f32[4,1,512]{2,1,0:T(1,128)}), f32[4,1,512]{2,1,0:T(1,128)S(1)}, u32[]{:S(2)}, u32[]{:S(2)}) %all-to-all-start.9) | async-done | bytes 8224 | tf_op jit(solution)/shard_map/all_to_all | solution.py:44
  201.6 15.1 %fusion.16 = f32[512,256]{1,0:T(8,128)} fusion(bf16[8192,256]{1,0:T(8,128)(2,1)} %copy-done, f32[512,8192]{1,0:T(8,128)} %get-tuple-element.9, f32[512,8192]{1,0:T(8,128)} %get-tuple-element.11, f32[512]{0:T(512)S(1)} %get-tuple-element.2, f32[8192]{0:T(1024)S(1)} %bitcast.20, f32[512]{0:T(512)S(1)} %log.14), kind=kOutput, calls=%fused_computation.28 | convolution fusion | flops 2176974848 | bytes 38309888 | tf_op jit(solution)/shard_map/dot_general | solution.py:110
  216.7 3.5 %all-to-all-start.10 = ((f32[4,128,256]{2,1,0:T(8,128)}), f32[4,128,256]{2,1,0:T(8,128)S(1)}, u32[]{:S(2)}, u32[]{:S(2)}) async-start(f32[4,128,256]{2,1,0:T(8,128)} %bitcast.9), calls=%async_computation.10 | async-start | bytes 1048576 | tf_op jit(solution)/shard_map/all_to_all | solution.py:32
  220.3 6.8 %all-to-all-done.10 = f32[4,128,256]{2,1,0:T(8,128)S(1)} async-done(((f32[4,128,256]{2,1,0:T(8,128)}), f32[4,128,256]{2,1,0:T(8,128)S(1)}, u32[]{:S(2)}, u32[]{:S(2)}) %all-to-all-start.10) | async-done | bytes 524320 | tf_op jit(solution)/shard_map/all_to_all | solution.py:32
  227.9 13.7 %all-to-all-start.11 = ((f32[64,512,2]{1,2,0:T(2,128)}), f32[64,512,2]{1,2,0:T(2,128)S(1)}, u32[]{:S(2)}, u32[]{:S(2)}) async-start(f32[64,512,2]{1,2,0:T(2,128)} %broadcast_in_dim.44), calls=%async_computation.11 | async-start | bytes 524288 | tf_op jit(solution)/shard_map/all_to_all | solution.py:44
  242.5 11.0 %all-to-all-done.11 = f32[64,512,2]{1,2,0:T(2,128)S(1)} async-done(((f32[64,512,2]{1,2,0:T(2,128)}), f32[64,512,2]{1,2,0:T(2,128)S(1)}, u32[]{:S(2)}, u32[]{:S(2)}) %all-to-all-start.11) | async-done | bytes 262176 | tf_op jit(solution)/shard_map/all_to_all | solution.py:44
  253.8 18.2 %fusion.2 = f32[32768,128]{1,0:T(8,128)} fusion(bf16[32768,512]{1,0:T(8,128)(2,1)} %all-gather.2.cloned.1.call-done, f32[128]{0:T(128)S(1)} %dynamic_slice.7, f32[32768]{0:T(1024)S(1)} %bitcast.31, bf16[8192,256]{1,0:T(8,128)(2,1)} %copy-done, s32[]{:T(128)S(6)} %select_n.4), kind=kOutput, calls=%fused_computation.3 | convolution fusion | flops 2160066560 | bytes 33751556 | tf_op jit(solution)/shard_map/dot_general | solution.py:79
  272.0 19.9 %fusion.17 = f32[128,256]{1,0:T(8,128)} fusion(bf16[32768,512]{1,0:T(8,128)(2,1)} %all-gather.2.cloned.1.call-done, f32[32768,128]{1,0:T(8,128)} %fusion.2, f32[32768]{0:T(1024)S(1)} %bitcast.30, bf16[8192,256]{1,0:T(8,128)(2,1)} %copy-done, s32[]{:T(128)S(6)} %select_n.4), kind=kOutput, calls=%fused_computation.29 | convolution fusion | flops 4315971584 | bytes 50659332 | tf_op jit(solution)/shard_map/dot_general | solution.py:130
  (43 shorter events, 4.3 us)
Async XLA Ops:
  7.2 246.6 %all-gather.2.cloned.1.call-start = ((), (), s32[]{:S(2)}) async-start(), calls=%async_computation.12 | async-start | bytes 34078720 | tf_op jit(solution)/shard_map/all_gather | solution.py:21
  29.4 2.0 copy-start
  129.0 43.4 %copy-start.1 = (bf16[512,512]{1,0:T(8,128)(2,1)S(1)}, bf16[512,512]{1,0:T(8,128)(2,1)}, u32[]{:S(2)}) copy-start(bf16[512,512]{1,0:T(8,128)(2,1)} %all_gather.6) | copy-start | bytes 1572868
  167.7 14.0 %all-to-all-start.8 = ((f32[64,1,128]{2,1,0:T(1,128)}), f32[64,1,128]{2,1,0:T(1,128)S(1)}, u32[]{:S(2)}, u32[]{:S(2)}) async-start(f32[64,1,128]{2,1,0:T(1,128)} %broadcast_in_dim.41), calls=%async_computation.8 | async-start | bytes 65536 | tf_op jit(solution)/shard_map/all_to_all | solution.py:44
  182.3 10.3 %all-to-all-start = ((f32[4,1,512]{2,1,0:T(1,128)}), f32[4,1,512]{2,1,0:T(1,128)S(1)}, u32[]{:S(2)}, u32[]{:S(2)}) async-start(f32[4,1,512]{2,1,0:T(1,128)} %broadcast_in_dim.36), calls=%async_computation | async-start | bytes 16384 | tf_op jit(solution)/shard_map/all_to_all | solution.py:44
  193.2 8.4 %all-to-all-start.9 = ((f32[4,1,512]{2,1,0:T(1,128)}), f32[4,1,512]{2,1,0:T(1,128)S(1)}, u32[]{:S(2)}, u32[]{:S(2)}) async-start(f32[4,1,512]{2,1,0:T(1,128)} %broadcast_in_dim.42), calls=%async_computation.9 | async-start | bytes 16384 | tf_op jit(solution)/shard_map/all_to_all | solution.py:44
  201.6 40.1 %copy-start.2 = (bf16[128,256]{1,0:T(8,128)(2,1)S(1)}, bf16[128,256]{1,0:T(8,128)(2,1)}, u32[]{:S(2)}) copy-start(bf16[128,256]{1,0:T(8,128)(2,1)} %param.4) | copy-start | bytes 196612
  216.7 10.4 %all-to-all-start.10 = ((f32[4,128,256]{2,1,0:T(8,128)}), f32[4,128,256]{2,1,0:T(8,128)S(1)}, u32[]{:S(2)}, u32[]{:S(2)}) async-start(f32[4,128,256]{2,1,0:T(8,128)} %bitcast.9), calls=%async_computation.10 | async-start | bytes 1048576 | tf_op jit(solution)/shard_map/all_to_all | solution.py:32
  227.9 25.7 %all-to-all-start.11 = ((f32[64,512,2]{1,2,0:T(2,128)}), f32[64,512,2]{1,2,0:T(2,128)S(1)}, u32[]{:S(2)}, u32[]{:S(2)}) async-start(f32[64,512,2]{1,2,0:T(2,128)} %broadcast_in_dim.44), calls=%async_computation.11 | async-start | bytes 524288 | tf_op jit(solution)/shard_map/all_to_all | solution.py:44
Sparse Core Ops, SparseCore 0:
  23.3 149.1 all-gather.1

commit v3 on v2

--- a/solution.py
+++ b/solution.py
@@ -4,12 +4,55 @@
 import jax.numpy as jnp
 from jax import lax
 from jax.sharding import PartitionSpec as P
+from jax.experimental import pallas as pl
+from jax.experimental.pallas import tpu as pltpu
+import functools
 
 ITERS = 3
 
 
 teacher_temp = 0.05
 student_temp = 0.1
+
+def _protos_kernel(ts_ref, c_ref, col_ref, al_ref, out_ref, *, rows_all, scale, width):
+    @pl.when(pl.program_id(0) == 0)
+    def _():
+        out_ref[...] = jnp.zeros_like(out_ref)
+
+    t = ts_ref[:, :width]
+    s = ts_ref[:, width:]
+    c = c_ref[...]
+    dims = (((1,), (1,)), ((), ()))
+    tl = lax.dot_general(c, t, dims, preferred_element_type=jnp.float32)
+    sl = lax.dot_general(c, s, dims, preferred_element_type=jnp.float32)
+    a = al_ref[0:1, :]
+    logz = al_ref[1:2, :]
+    target = rows_all * jnp.exp(tl / teacher_temp) * a * col_ref[...]
+    probs = jnp.exp(sl / student_temp - logz)
+    g = (scale * (probs - target)).astype(jnp.bfloat16)
+    out_ref[...] += jnp.dot(g, s, preferred_element_type=jnp.float32)
+
+
+def protos_grad(ts, c_mine, col_mine, al, rows_all, scale, block=2048, interpret=False):
+    n, w2 = ts.shape
+    width = w2 // 2
+    m = c_mine.shape[0]
+    kern = functools.partial(_protos_kernel, rows_all=rows_all, scale=scale, width=width)
+    out = pl.pallas_call(
+        kern,
+        grid=(n // block,),
+        in_specs=[
+            pl.BlockSpec((block, w2), lambda i: (i, 0)),
+            pl.BlockSpec((m, width), lambda i: (0, 0)),
+            pl.BlockSpec((m, 1), lambda i: (0, 0)),
+            pl.BlockSpec((2, block), lambda i: (0, i)),
+        ],
+        out_specs=pl.BlockSpec((m, width), lambda i: (0, 0)),
+        out_shape=jax.ShapeDtypeStruct((m, width), jnp.float32),
+        compiler_params=pltpu.CompilerParams(dimension_semantics=("arbitrary",)),
+        interpret=interpret,
+    )(ts, c_mine, col_mine.reshape(m, 1), al)
+    return out / student_temp
 
 
 def side_by_side(arrays, axis, dim, along):
@@ -116,22 +159,10 @@
     c_mine = lax.dynamic_slice_in_dim(cn, offset, mine_rows, 0)
     col_mine = lax.dynamic_slice_in_dim(col_scale, offset, mine_rows, 0)
     both = gather_directly(jnp.stack([row_scale, logz], axis=1), "batch", 0)
-    all_scale, all_logz = both[:, 0], both[:, 1]
-    t_piece, s_piece = side_by_side((tn_group, sn_group), "batch", 0, 1)
-    target = (
-        rows_all
-        * jnp.exp(against(t_piece, c_mine) / teacher_temp)
-        * all_scale[:, None]
-        * col_mine[None, :]
+    pieces = lax.all_gather(
+        jnp.concatenate((tn_group, sn_group), axis=1), "batch", axis=0, tiled=True
     )
-    probs = jnp.exp(against(s_piece, c_mine) / student_temp - all_logz[:, None])
-    local_grads = (scale * (probs - target)).astype(jnp.bfloat16)
-    grad_protos = (
-        lax.dot_general(
-            local_grads, s_piece, (((0,), (0,)), ((), ())), preferred_element_type=jnp.float32
-        )
-        / student_temp
-    )
+    grad_protos = protos_grad(pieces, c_mine, col_mine, both.T, rows_all, scale)
     return (grad_student, grad_protos)
 
 

time: 300 us -> 288 us (0.960)
  matrix products: 70.6 us -> 32.4 us
  Pallas kernels: 0 us -> 23.9 us
    pallas_call x0 -> x1, Pallas kernels: none -> 23.9 us  [protos_grad(): pl.pallas_call(kern, grid=(n // block,), in_specs=[pl.BlockSpec((block, w...]
    dot_general x1 -> x0, matrix products: 19.9 us -> none  [per_device(): lax.dot_general(local_grads, s_piece, (((0,), (0,)), ((), ())), preferred...]
    dot_general x3 -> x2, matrix products: 35.5 us -> 17.3 us  [against(): lax.dot_general(left, right, (((1,), (1,)), ((), ())), preferred_element_...]
  transfers between devices with their start and end apart: 6 -> 6, of which waited for: 3 -> 3; matrix products, arithmetic and copies ran while one was open for 28% -> 30% of each run, Pallas kernels for 0% -> 0%
where the time goes in v3:
time: 288 us; the launch traced here: 286 us
  blocking collectives  108 us (38%)
  other arithmetic  51.6 us (18%)
  matrix products  32.4 us (11%)
  starting transfers between devices  29.1 us (10%)
  Pallas kernels  23.9 us (8%)
  waiting for transfers between devices  19.8 us (7%)
  between operations  14.2 us (5%)
  local copies, waits for them, and re-layouts  7.63 us (3%)
    all_to_all x3, blocking collectives, summed_on_arrival(): lax.all_to_all(parts, axis, split_axis=0, concat_axis=0, tiled=True)  53 us
    all_to_all x4, blocking collectives, copy_for_each(): return lax.all_to_all(copies, axis, split_axis=0, concat_axis=0, tiled=True)  41.7 us
    all_to_all x4, starting transfers between devices, copy_for_each(): return lax.all_to_all(copies, axis, split_axis=0, concat_axis=0, tiled=True)  25.6 us
    pallas_call x1, Pallas kernels, protos_grad(): pl.pallas_call(kern, grid=(n // block,), in_specs=[pl.BlockSpec((block, w...  23.9 us
    reduce_sum x3, other arithmetic, per_device(): sample_local = jnp.sum(weight * col_scale[None, :], axis=1)  22.6 us
    dot_general x2, matrix products, against(): lax.dot_general(left, right, (((1,), (1,)), ((), ())), preferred_element_...  17.3 us
    reduce_sum x2, other arithmetic, per_device(): mass_local = jnp.sum(weight * row_scale[:, None], axis=0)  17.2 us
    all_to_all x4, waiting for transfers between devices, copy_for_each(): return lax.all_to_all(copies, axis, split_axis=0, concat_axis=0, tiled=True)  15.2 us
  transfers between devices with their start and end apart: 6, of which 3 were waited for; matrix products, arithmetic and copies ran while one was open for 30% of the time, Pallas kernels for 0%

profile of v3, /device:TPU:1, one launch (start us, length us, event | category | flops | bytes accessed | tf_op | source)
XLA Modules:
  0.0 286.3 jit_solution(2193659616519914394)
XLA Ops:
  8.2 1.0 fusion.11
  9.1 1.0 fusion.10
  10.1 13.0 %all_gather.6 = bf16[512,512]{1,0:T(8,128)(2,1)} all-gather(bf16[128,512]{1,0:T(8,128)(2,1)S(1)} %pad_maximum_fusion), channel_id=1, replica_groups=mesh['proto'=4,'batch'=64] {'proto'}, dimensions={0}, use_global_device_ids=true | all-gather | bytes 655360 | tf_op jit(solution)/shard_map/all_gather | solution.py:64
  23.1 3.3 %fusion = f32[8192]{0:T(1024)S(1)} fusion(bf16[8192,256]{1,0:T(8,128)(2,1)} %param.5), kind=kLoop, calls=%fused_computation.10 | loop fusion | flops 6283264 | bytes 4227072 | tf_op jit(solution)/shard_map/reduce_sum | solution.py:116
  26.5 2.9 %fusion.2 = bf16[8192,256]{1,0:T(8,128)(2,1)S(1)} fusion(bf16[8192,256]{1,0:T(8,128)(2,1)} %param.5, f32[8192]{0:T(1024)S(1)} %add_rsqrt_fusion), kind=kLoop, calls=%fused_computation.12 | loop fusion | flops 8388608 | bytes 8421376 | tf_op jit(solution)/shard_map/convert_element_type | solution.py:135
  29.4 2.0 copy-done
  31.4 8.0 %fusion.18 = (f32[8192]{0:T(1024)S(1)}, f32[512,8192]{1,0:T(8,128)}) fusion(bf16[8192,256]{1,0:T(8,128)(2,1)S(1)} %fusion.2, bf16[512,512]{1,0:T(8,128)(2,1)} %all_gather.6), kind=kOutput, calls=%fused_computation.52 | convolution fusion | flops 2155864064 | bytes 21266432 | tf_op jit(solution)/shard_map/dot_general | solution.py:122
  39.3 23.4 %all_to_all.79 = f32[64,1,128]{2,1,0:T(1,128)S(1)} all-to-all(f32[64,1,128]{2,1,0:T(1,128)S(1)} %bitcast.24), channel_id=1, replica_groups=mesh['proto'=4,'batch'=64] {'batch'}, dimensions={0} | all-to-all | bytes 65536 | tf_op jit(solution)/shard_map/all_to_all | solution.py:75
  62.8 13.4 %all_to_all.80 = f32[64,1,128]{2,1,0:T(1,128)S(1)} all-to-all(f32[64,1,128]{2,1,0:T(1,128)S(1)} %broadcast_in_dim.36), channel_id=1, replica_groups=mesh['proto'=4,'batch'=64] {'batch'}, dimensions={0} | all-to-all | bytes 65536 | tf_op jit(solution)/shard_map/all_to_all | solution.py:87
  76.3 7.3 %multiply_reduce_fusion.4 = f32[512]{0:T(512)S(1)} fusion(f32[512,8192]{1,0:T(8,128)} %get-tuple-element.7, f32[8192]{0:T(1024)S(1)} %bitcast.25), kind=kLoop, calls=%fused_computation.5 | loop fusion | flops 8388096 | bytes 16812032 | tf_op jit(solution)/shard_map/reduce_sum | solution.py:144
  83.5 8.1 %all_to_all.81 = f32[4,1,512]{2,1,0:T(1,128)S(1)} all-to-all(f32[4,1,512]{2,1,0:T(1,128)S(1)} %broadcast_in_dim.37), channel_id=1, replica_groups=mesh['proto'=4,'batch'=64] {'proto'}, dimensions={0} | all-to-all | bytes 16384 | tf_op jit(solution)/shard_map/all_to_all | solution.py:87
  91.7 8.7 %multiply_reduce_fusion.3 = f32[8192]{0:T(1024)S(1)} fusion(f32[512,8192]{1,0:T(8,128)} %get-tuple-element.7, f32[512]{0:T(512)S(1)} %multiply_divide_fusion.2), kind=kLoop, calls=%fused_computation.4 | loop fusion | flops 8380416 | bytes 16812032 | tf_op jit(solution)/shard_map/reduce_sum | solution.py:141
  100.3 15.0 %all_to_all.82 = f32[64,1,128]{2,1,0:T(1,128)S(1)} all-to-all(f32[64,1,128]{2,1,0:T(1,128)S(1)} %bitcast.26), channel_id=1, replica_groups=mesh['proto'=4,'batch'=64] {'batch'}, dimensions={0} | all-to-all | bytes 65536 | tf_op jit(solution)/shard_map/all_to_all | solution.py:75
  115.4 13.6 %all_to_all.83 = f32[64,1,128]{2,1,0:T(1,128)S(1)} all-to-all(f32[64,1,128]{2,1,0:T(1,128)S(1)} %broadcast_in_dim.38), channel_id=1, replica_groups=mesh['proto'=4,'batch'=64] {'batch'}, dimensions={0} | all-to-all | bytes 65536 | tf_op jit(solution)/shard_map/all_to_all | solution.py:87
  129.0 8.3 %multiply_reduce_fusion.2 = f32[512]{0:T(512)S(1)} fusion(f32[512,8192]{1,0:T(8,128)} %get-tuple-element.7, f32[8192]{0:T(1024)S(1)} %bitcast.27), kind=kLoop, calls=%fused_computation.3 | loop fusion | flops 8388096 | bytes 16812032 | tf_op jit(solution)/shard_map/reduce_sum | solution.py:144
  137.3 6.6 %all_to_all.84 = f32[4,1,512]{2,1,0:T(1,128)S(1)} all-to-all(f32[4,1,512]{2,1,0:T(1,128)S(1)} %broadcast_in_dim.39), channel_id=1, replica_groups=mesh['proto'=4,'batch'=64] {'proto'}, dimensions={0} | all-to-all | bytes 16384 | tf_op jit(solution)/shard_map/all_to_all | solution.py:87
  143.9 8.5 %multiply_reduce_fusion.1 = f32[8192]{0:T(1024)S(1)} fusion(f32[512,8192]{1,0:T(8,128)} %get-tuple-element.7, f32[512]{0:T(512)S(1)} %multiply_divide_fusion.1), kind=kLoop, calls=%fused_computation.2 | loop fusion | flops 8380416 | bytes 16812032 | tf_op jit(solution)/shard_map/reduce_sum | solution.py:141
  152.4 14.6 %all_to_all.85 = f32[64,1,128]{2,1,0:T(1,128)S(1)} all-to-all(f32[64,1,128]{2,1,0:T(1,128)S(1)} %bitcast.28), channel_id=1, replica_groups=mesh['proto'=4,'batch'=64] {'batch'}, dimensions={0} | all-to-all | bytes 65536 | tf_op jit(solution)/shard_map/all_to_all | solution.py:75
  167.7 4.6 %all-to-all-start.8 = ((f32[64,1,128]{2,1,0:T(1,128)}), f32[64,1,128]{2,1,0:T(1,128)S(1)}, u32[]{:S(2)}, u32[]{:S(2)}) async-start(f32[64,1,128]{2,1,0:T(1,128)} %broadcast_in_dim.40), calls=%async_computation.8 | async-start | bytes 65536 | tf_op jit(solution)/shard_map/all_to_all | solution.py:87
  172.3 9.3 %exponential_reduce_fusion = (f32[512]{0:T(512)S(1)}, f32[512,8192]{1,0:T(8,128)}) fusion(bf16[8192,256]{1,0:T(8,128)(2,1)} %copy-done, bf16[512,512]{1,0:T(8,128)(2,1)S(1)} %copy-done.1), kind=kOutput, calls=%fused_computation.7 | convolution fusion | flops 2155871744 | bytes 21235712 | tf_op jit(solution)/shard_map/dot_general | solution.py:122
  182.3 3.2 %all-to-all-start = ((f32[4,1,512]{2,1,0:T(1,128)}), f32[4,1,512]{2,1,0:T(1,128)S(1)}, u32[]{:S(2)}, u32[]{:S(2)}) async-start(f32[4,1,512]{2,1,0:T(1,128)} %broadcast_in_dim.35), calls=%async_computation | async-start | bytes 16384 | tf_op jit(solution)/shard_map/all_to_all | solution.py:87
  185.6 7.0 %multiply_reduce_fusion = f32[512]{0:T(512)S(1)} fusion(f32[512,8192]{1,0:T(8,128)} %get-tuple-element.7, f32[8192]{0:T(1024)S(1)} %bitcast.21), kind=kLoop, calls=%fused_computation.1 | loop fusion | flops 8388096 | bytes 16812032 | tf_op jit(solution)/shard_map/reduce_sum | solution.py:144
  193.2 4.2 %all-to-all-start.9 = ((f32[4,1,512]{2,1,0:T(1,128)}), f32[4,1,512]{2,1,0:T(1,128)S(1)}, u32[]{:S(2)}, u32[]{:S(2)}) async-start(f32[4,1,512]{2,1,0:T(1,128)} %broadcast_in_dim.41), calls=%async_computation.9 | async-start | bytes 16384 | tf_op jit(solution)/shard_map/all_to_all | solution.py:87
  197.4 4.1 %all-to-all-done.9 = f32[4,1,512]{2,1,0:T(1,128)S(1)} async-done(((f32[4,1,512]{2,1,0:T(1,128)}), f32[4,1,512]{2,1,0:T(1,128)S(1)}, u32[]{:S(2)}, u32[]{:S(2)}) %all-to-all-start.9) | async-done | bytes 8224 | tf_op jit(solution)/shard_map/all_to_all | solution.py:87
  201.6 15.1 %fusion.4 = f32[512,256]{1,0:T(8,128)} fusion(bf16[8192,256]{1,0:T(8,128)(2,1)} %copy-done, f32[512,8192]{1,0:T(8,128)} %get-tuple-element.7, f32[512,8192]{1,0:T(8,128)} %get-tuple-element.9, f32[512]{0:T(512)S(1)} %get-tuple-element.2, f32[8192]{0:T(1024)S(1)} %bitcast.22, f32[512]{0:T(512)S(1)} %log.14), kind=kOutput, calls=%fused_computation.14 | convolution fusion | flops 2176974848 | bytes 38309888 | tf_op jit(solution)/shard_map/dot_general | solution.py:153
  216.7 3.5 %all-to-all-start.10 = ((f32[4,128,256]{2,1,0:T(8,128)}), f32[4,128,256]{2,1,0:T(8,128)S(1)}, u32[]{:S(2)}, u32[]{:S(2)}) async-start(f32[4,128,256]{2,1,0:T(8,128)} %bitcast.9), calls=%async_computation.10 | async-start | bytes 1048576 | tf_op jit(solution)/shard_map/all_to_all | solution.py:75
  220.2 1.5 constant_dynamic-slice_fusion.c_ref
  222.5 4.6 %all-to-all-done.10 = f32[4,128,256]{2,1,0:T(8,128)S(1)} async-done(((f32[4,128,256]{2,1,0:T(8,128)}), f32[4,128,256]{2,1,0:T(8,128)S(1)}, u32[]{:S(2)}, u32[]{:S(2)}) %all-to-all-start.10) | async-done | bytes 524320 | tf_op jit(solution)/shard_map/all_to_all | solution.py:75
  227.9 13.5 %all-to-all-start.11 = ((f32[64,512,2]{1,2,0:T(2,128)}), f32[64,512,2]{1,2,0:T(2,128)S(1)}, u32[]{:S(2)}, u32[]{:S(2)}) async-start(f32[64,512,2]{1,2,0:T(2,128)} %broadcast_in_dim.43), calls=%async_computation.11 | async-start | bytes 524288 | tf_op jit(solution)/shard_map/all_to_all | solution.py:87
  242.3 11.0 %all-to-all-done.11 = f32[64,512,2]{1,2,0:T(2,128)S(1)} async-done(((f32[64,512,2]{1,2,0:T(2,128)}), f32[64,512,2]{1,2,0:T(2,128)S(1)}, u32[]{:S(2)}, u32[]{:S(2)}) %all-to-all-start.11) | async-done | bytes 262176 | tf_op jit(solution)/shard_map/all_to_all | solution.py:87
  254.0 23.9 %shard_map.50 = f32[128,256]{1,0:T(8,128)} custom-call(bf16[32768,512]{1,0:T(8,128)(2,1)} %all-gather.2.cloned.1.call-done.ts_ref, bf16[128,256]{1,0:T(8,128)(2,1)} %constant_dynamic-slice_fusion.c_ref, f32[128,1]{1,0:T(8,128)} %copy.15.col_ref, f32[2,32768]{1,0:T(2,128)} %bitcast.20), custom_call_target="tpu_custom_call" | custom-call | tf_op jit(solution)/shard_map/pallas_call | solution.py:41
  277.9 1.6 broadcast_multiply_fusion
  (46 shorter events, 6.4 us)
Async XLA Ops:
  7.2 246.2 %all-gather.2.cloned.1.call-start = ((), (), s32[]{:S(2)}) async-start(), calls=%async_computation.12 | async-start | bytes 34078720 | tf_op jit(solution)/shard_map/all_gather | solution.py:162
  29.4 2.0 copy-start
  129.0 43.4 %copy-start.1 = (bf16[512,512]{1,0:T(8,128)(2,1)S(1)}, bf16[512,512]{1,0:T(8,128)(2,1)}, u32[]{:S(2)}) copy-start(bf16[512,512]{1,0:T(8,128)(2,1)} %all_gather.6) | copy-start | bytes 1572868
  167.7 14.0 %all-to-all-start.8 = ((f32[64,1,128]{2,1,0:T(1,128)}), f32[64,1,128]{2,1,0:T(1,128)S(1)}, u32[]{:S(2)}, u32[]{:S(2)}) async-start(f32[64,1,128]{2,1,0:T(1,128)} %broadcast_in_dim.40), calls=%async_computation.8 | async-start | bytes 65536 | tf_op jit(solution)/shard_map/all_to_all | solution.py:87
  182.3 10.3 %all-to-all-start = ((f32[4,1,512]{2,1,0:T(1,128)}), f32[4,1,512]{2,1,0:T(1,128)S(1)}, u32[]{:S(2)}, u32[]{:S(2)}) async-start(f32[4,1,512]{2,1,0:T(1,128)} %broadcast_in_dim.35), calls=%async_computation | async-start | bytes 16384 | tf_op jit(solution)/shard_map/all_to_all | solution.py:87
  193.2 8.4 %all-to-all-start.9 = ((f32[4,1,512]{2,1,0:T(1,128)}), f32[4,1,512]{2,1,0:T(1,128)S(1)}, u32[]{:S(2)}, u32[]{:S(2)}) async-start(f32[4,1,512]{2,1,0:T(1,128)} %broadcast_in_dim.41), calls=%async_computation.9 | async-start | bytes 16384 | tf_op jit(solution)/shard_map/all_to_all | solution.py:87
  201.6 39.8 %copy-start.3 = (bf16[128,256]{1,0:T(8,128)(2,1)S(1)}, bf16[128,256]{1,0:T(8,128)(2,1)}, u32[]{:S(2)}) copy-start(bf16[128,256]{1,0:T(8,128)(2,1)} %param.4) | copy-start | bytes 196612
  216.7 10.4 %all-to-all-start.10 = ((f32[4,128,256]{2,1,0:T(8,128)}), f32[4,128,256]{2,1,0:T(8,128)S(1)}, u32[]{:S(2)}, u32[]{:S(2)}) async-start(f32[4,128,256]{2,1,0:T(8,128)} %bitcast.9), calls=%async_computation.10 | async-start | bytes 1048576 | tf_op jit(solution)/shard_map/all_to_all | solution.py:75
  227.9 25.5 %all-to-all-start.11 = ((f32[64,512,2]{1,2,0:T(2,128)}), f32[64,512,2]{1,2,0:T(2,128)S(1)}, u32[]{:S(2)}, u32[]{:S(2)}) async-start(f32[64,512,2]{1,2,0:T(2,128)} %broadcast_in_dim.43), calls=%async_computation.11 | async-start | bytes 524288 | tf_op jit(solution)/shard_map/all_to_all | solution.py:87
  253.3 0.7 copy-start.2
Sparse Core Ops, SparseCore 0:
  23.3 149.1 all-gather.1

commit v4 on v3

--- a/solution.py
+++ b/solution.py
@@ -149,20 +149,20 @@
     logp = logits - logz[:, None]
     scale = 16.0 * math.sqrt(count_all)
     grads = (scale * (jnp.exp(logp) - targets)).astype(jnp.bfloat16)
-    grad_sn = summed_on_arrival(
-        jnp.dot(grads, cn, preferred_element_type=jnp.float32) / student_temp, "proto", 0
-    )
-    _, pull = jax.vjp(unit_rows, student.astype(jnp.float32))
-    grad_student = pull(grad_sn)[0]
+    sn_partial = jnp.dot(grads, cn, preferred_element_type=jnp.float32) / student_temp
     mine_rows = prototypes.shape[0] // n_batch
     offset = lax.axis_index("batch") * mine_rows
     c_mine = lax.dynamic_slice_in_dim(cn, offset, mine_rows, 0)
     col_mine = lax.dynamic_slice_in_dim(col_scale, offset, mine_rows, 0)
     both = gather_directly(jnp.stack([row_scale, logz], axis=1), "batch", 0)
+    sn_partial, both = lax.optimization_barrier((sn_partial, both))
+    grad_sn = summed_on_arrival(sn_partial, "proto", 0)
     pieces = lax.all_gather(
         jnp.concatenate((tn_group, sn_group), axis=1), "batch", axis=0, tiled=True
     )
     grad_protos = protos_grad(pieces, c_mine, col_mine, both.T, rows_all, scale)
+    _, pull = jax.vjp(unit_rows, student.astype(jnp.float32))
+    grad_student = pull(grad_sn)[0]
     return (grad_student, grad_protos)
 
 

time: 288 us -> 277 us (0.962)
  waiting for transfers between devices: 19.8 us -> 10.8 us
    all_to_all x4, waiting for transfers between devices: 15.2 us -> 4.17 us  [copy_for_each(): return lax.all_to_all(copies, axis, split_axis=0, concat_axis=0, tiled=True)]
  transfers between devices with their start and end apart: 6 -> 6, of which waited for: 3 -> 2; matrix products, arithmetic and copies ran while one was open for 30% -> 31% of each run, Pallas kernels for 0% -> 0%
where the time goes in v4:
time: 277 us; the launch traced here: 275 us
  blocking collectives  108 us (39%)
  other arithmetic  51.6 us (19%)
  matrix products  32.4 us (12%)
  starting transfers between devices  27.7 us (10%)
  Pallas kernels  23.9 us (9%)
  between operations  14.2 us (5%)
  waiting for transfers between devices  10.8 us (4%)
  local copies, waits for them, and re-layouts  6.95 us (3%)
    all_to_all x3, blocking collectives, summed_on_arrival(): lax.all_to_all(parts, axis, split_axis=0, concat_axis=0, tiled=True)  53 us
    all_to_all x4, blocking collectives, copy_for_each(): return lax.all_to_all(copies, axis, split_axis=0, concat_axis=0, tiled=True)  41.7 us
    all_to_all x4, starting transfers between devices, copy_for_each(): return lax.all_to_all(copies, axis, split_axis=0, concat_axis=0, tiled=True)  24.2 us
    pallas_call x1, Pallas kernels, protos_grad(): pl.pallas_call(kern, grid=(n // block,), in_specs=[pl.BlockSpec((block, w...  23.9 us
    reduce_sum x3, other arithmetic, per_device(): sample_local = jnp.sum(weight * col_scale[None, :], axis=1)  22.6 us
    dot_general x2, matrix products, against(): lax.dot_general(left, right, (((1,), (1,)), ((), ())), preferred_element_...  17.3 us
    reduce_sum x2, other arithmetic, per_device(): mass_local = jnp.sum(weight * row_scale[:, None], axis=0)  17.2 us
    dot_general x1, matrix products, per_device(): jnp.dot(grads, cn, preferred_element_type=jnp.float32) / student_temp  15.1 us
  transfers between devices with their start and end apart: 6, of which 2 were waited for; matrix products, arithmetic and copies ran while one was open for 31% of the time, Pallas kernels for 0%

profile of v4, /device:TPU:1, one launch (start us, length us, event | category | flops | bytes accessed | tf_op | source)
XLA Modules:
  0.0 275.2 jit_solution(6756104844142527830)
XLA Ops:
  7.2 0.9 fusion.11
  8.2 1.0 fusion.8
  9.1 1.0 fusion.10
  10.1 13.0 %all_gather.6 = bf16[512,512]{1,0:T(8,128)(2,1)} all-gather(bf16[128,512]{1,0:T(8,128)(2,1)S(1)} %pad_maximum_fusion), channel_id=1, replica_groups=mesh['proto'=4,'batch'=64] {'proto'}, dimensions={0}, use_global_device_ids=true | all-gather | bytes 655360 | tf_op jit(solution)/shard_map/all_gather | solution.py:64
  23.1 3.3 %fusion = f32[8192]{0:T(1024)S(1)} fusion(bf16[8192,256]{1,0:T(8,128)(2,1)} %param.5), kind=kLoop, calls=%fused_computation.10 | loop fusion | flops 6283264 | bytes 4227072 | tf_op jit(solution)/shard_map/reduce_sum | solution.py:116
  26.5 2.9 %fusion.2 = bf16[8192,256]{1,0:T(8,128)(2,1)S(1)} fusion(bf16[8192,256]{1,0:T(8,128)(2,1)} %param.5, f32[8192]{0:T(1024)S(1)} %add_rsqrt_fusion), kind=kLoop, calls=%fused_computation.12 | loop fusion | flops 8388608 | bytes 8421376 | tf_op jit(solution)/shard_map/convert_element_type | solution.py:135
  29.4 2.0 copy-done
  31.4 8.0 %fusion.18 = (f32[8192]{0:T(1024)S(1)}, f32[512,8192]{1,0:T(8,128)}) fusion(bf16[8192,256]{1,0:T(8,128)(2,1)S(1)} %fusion.2, bf16[512,512]{1,0:T(8,128)(2,1)} %all_gather.6), kind=kOutput, calls=%fused_computation.52 | convolution fusion | flops 2155864064 | bytes 21266432 | tf_op jit(solution)/shard_map/dot_general | solution.py:122
  39.3 23.4 %all_to_all.79 = f32[64,1,128]{2,1,0:T(1,128)S(1)} all-to-all(f32[64,1,128]{2,1,0:T(1,128)S(1)} %bitcast.23), channel_id=1, replica_groups=mesh['proto'=4,'batch'=64] {'batch'}, dimensions={0} | all-to-all | bytes 65536 | tf_op jit(solution)/shard_map/all_to_all | solution.py:75
  62.8 13.4 %all_to_all.80 = f32[64,1,128]{2,1,0:T(1,128)S(1)} all-to-all(f32[64,1,128]{2,1,0:T(1,128)S(1)} %broadcast_in_dim.36), channel_id=1, replica_groups=mesh['proto'=4,'batch'=64] {'batch'}, dimensions={0} | all-to-all | bytes 65536 | tf_op jit(solution)/shard_map/all_to_all | solution.py:87
  76.3 7.3 %multiply_reduce_fusion.4 = f32[512]{0:T(512)S(1)} fusion(f32[512,8192]{1,0:T(8,128)} %get-tuple-element.11, f32[8192]{0:T(1024)S(1)} %bitcast.24), kind=kLoop, calls=%fused_computation.5 | loop fusion | flops 8388096 | bytes 16812032 | tf_op jit(solution)/shard_map/reduce_sum | solution.py:144
  83.5 8.1 %all_to_all.81 = f32[4,1,512]{2,1,0:T(1,128)S(1)} all-to-all(f32[4,1,512]{2,1,0:T(1,128)S(1)} %broadcast_in_dim.37), channel_id=1, replica_groups=mesh['proto'=4,'batch'=64] {'proto'}, dimensions={0} | all-to-all | bytes 16384 | tf_op jit(solution)/shard_map/all_to_all | solution.py:87
  91.7 8.7 %multiply_reduce_fusion.3 = f32[8192]{0:T(1024)S(1)} fusion(f32[512,8192]{1,0:T(8,128)} %get-tuple-element.11, f32[512]{0:T(512)S(1)} %multiply_divide_fusion.2), kind=kLoop, calls=%fused_computation.4 | loop fusion | flops 8380416 | bytes 16812032 | tf_op jit(solution)/shard_map/reduce_sum | solution.py:141
  100.3 15.0 %all_to_all.82 = f32[64,1,128]{2,1,0:T(1,128)S(1)} all-to-all(f32[64,1,128]{2,1,0:T(1,128)S(1)} %bitcast.25), channel_id=1, replica_groups=mesh['proto'=4,'batch'=64] {'batch'}, dimensions={0} | all-to-all | bytes 65536 | tf_op jit(solution)/shard_map/all_to_all | solution.py:75
  115.4 13.6 %all_to_all.83 = f32[64,1,128]{2,1,0:T(1,128)S(1)} all-to-all(f32[64,1,128]{2,1,0:T(1,128)S(1)} %broadcast_in_dim.38), channel_id=1, replica_groups=mesh['proto'=4,'batch'=64] {'batch'}, dimensions={0} | all-to-all | bytes 65536 | tf_op jit(solution)/shard_map/all_to_all | solution.py:87
  129.0 8.3 %multiply_reduce_fusion.2 = f32[512]{0:T(512)S(1)} fusion(f32[512,8192]{1,0:T(8,128)} %get-tuple-element.11, f32[8192]{0:T(1024)S(1)} %bitcast.26), kind=kLoop, calls=%fused_computation.3 | loop fusion | flops 8388096 | bytes 16812032 | tf_op jit(solution)/shard_map/reduce_sum | solution.py:144
  137.3 6.6 %all_to_all.84 = f32[4,1,512]{2,1,0:T(1,128)S(1)} all-to-all(f32[4,1,512]{2,1,0:T(1,128)S(1)} %broadcast_in_dim.39), channel_id=1, replica_groups=mesh['proto'=4,'batch'=64] {'proto'}, dimensions={0} | all-to-all | bytes 16384 | tf_op jit(solution)/shard_map/all_to_all | solution.py:87
  143.9 8.5 %multiply_reduce_fusion.1 = f32[8192]{0:T(1024)S(1)} fusion(f32[512,8192]{1,0:T(8,128)} %get-tuple-element.11, f32[512]{0:T(512)S(1)} %multiply_divide_fusion.1), kind=kLoop, calls=%fused_computation.2 | loop fusion | flops 8380416 | bytes 16812032 | tf_op jit(solution)/shard_map/reduce_sum | solution.py:141
  152.4 14.6 %all_to_all.85 = f32[64,1,128]{2,1,0:T(1,128)S(1)} all-to-all(f32[64,1,128]{2,1,0:T(1,128)S(1)} %bitcast.27), channel_id=1, replica_groups=mesh['proto'=4,'batch'=64] {'batch'}, dimensions={0} | all-to-all | bytes 65536 | tf_op jit(solution)/shard_map/all_to_all | solution.py:75
  167.7 4.6 %all-to-all-start.8 = ((f32[64,1,128]{2,1,0:T(1,128)}), f32[64,1,128]{2,1,0:T(1,128)S(1)}, u32[]{:S(2)}, u32[]{:S(2)}) async-start(f32[64,1,128]{2,1,0:T(1,128)} %broadcast_in_dim.40), calls=%async_computation.8 | async-start | bytes 65536 | tf_op jit(solution)/shard_map/all_to_all | solution.py:87
  172.4 9.3 %exponential_reduce_fusion = (f32[512]{0:T(512)S(1)}, f32[512,8192]{1,0:T(8,128)}) fusion(bf16[8192,256]{1,0:T(8,128)(2,1)} %copy-done, bf16[512,512]{1,0:T(8,128)(2,1)S(1)} %copy-done.1), kind=kOutput, calls=%fused_computation.7 | convolution fusion | flops 2155871744 | bytes 21235712 | tf_op jit(solution)/shard_map/dot_general | solution.py:122
  182.3 3.2 %all-to-all-start = ((f32[4,1,512]{2,1,0:T(1,128)}), f32[4,1,512]{2,1,0:T(1,128)S(1)}, u32[]{:S(2)}, u32[]{:S(2)}) async-start(f32[4,1,512]{2,1,0:T(1,128)} %broadcast_in_dim.35), calls=%async_computation | async-start | bytes 16384 | tf_op jit(solution)/shard_map/all_to_all | solution.py:87
  185.6 7.0 %multiply_reduce_fusion = f32[512]{0:T(512)S(1)} fusion(f32[512,8192]{1,0:T(8,128)} %get-tuple-element.11, f32[8192]{0:T(1024)S(1)} %bitcast.20), kind=kLoop, calls=%fused_computation.1 | loop fusion | flops 8388096 | bytes 16812032 | tf_op jit(solution)/shard_map/reduce_sum | solution.py:144
  193.2 4.2 %all-to-all-start.9 = ((f32[4,1,512]{2,1,0:T(1,128)}), f32[4,1,512]{2,1,0:T(1,128)S(1)}, u32[]{:S(2)}, u32[]{:S(2)}) async-start(f32[4,1,512]{2,1,0:T(1,128)} %broadcast_in_dim.41), calls=%async_computation.9 | async-start | bytes 16384 | tf_op jit(solution)/shard_map/all_to_all | solution.py:87
  197.4 4.1 %all-to-all-done.9 = f32[4,1,512]{2,1,0:T(1,128)S(1)} async-done(((f32[4,1,512]{2,1,0:T(1,128)}), f32[4,1,512]{2,1,0:T(1,128)S(1)}, u32[]{:S(2)}, u32[]{:S(2)}) %all-to-all-start.9) | async-done | bytes 8224 | tf_op jit(solution)/shard_map/all_to_all | solution.py:87
  202.4 12.1 %all-to-all-start.10 = ((f32[64,512,2]{1,2,0:T(2,128)}), f32[64,512,2]{1,2,0:T(2,128)S(1)}, u32[]{:S(2)}, u32[]{:S(2)}) async-start(f32[64,512,2]{1,2,0:T(2,128)} %broadcast_in_dim.42), calls=%async_computation.10 | async-start | bytes 524288 | tf_op jit(solution)/shard_map/all_to_all | solution.py:87
  214.5 15.1 %fusion.4 = f32[512,256]{1,0:T(8,128)} fusion(bf16[8192,256]{1,0:T(8,128)(2,1)} %copy-done, f32[512,8192]{1,0:T(8,128)} %get-tuple-element.11, f32[512,8192]{1,0:T(8,128)} %get-tuple-element.13, f32[512]{0:T(512)S(1)} %get-tuple-element.6, f32[8192]{0:T(1024)S(1)} %bitcast.21, f32[512]{0:T(512)S(1)} %log.14), kind=kOutput, calls=%fused_computation.14 | convolution fusion | flops 2176974848 | bytes 38309888 | tf_op jit(solution)/shard_map/dot_general | solution.py:152
  229.6 3.5 %all-to-all-start.11 = ((f32[4,128,256]{2,1,0:T(8,128)}), f32[4,128,256]{2,1,0:T(8,128)S(1)}, u32[]{:S(2)}, u32[]{:S(2)}) async-start(f32[4,128,256]{2,1,0:T(8,128)} %bitcast.12), calls=%async_computation.11 | async-start | bytes 1048576 | tf_op jit(solution)/shard_map/all_to_all | solution.py:75
  233.1 1.5 constant_dynamic-slice_fusion.c_ref
  235.4 6.6 %all-to-all-done.11 = f32[4,128,256]{2,1,0:T(8,128)S(1)} async-done(((f32[4,128,256]{2,1,0:T(8,128)}), f32[4,128,256]{2,1,0:T(8,128)S(1)}, u32[]{:S(2)}, u32[]{:S(2)}) %all-to-all-start.11) | async-done | bytes 524320 | tf_op jit(solution)/shard_map/all_to_all | solution.py:75
  242.9 23.9 %shard_map.50 = f32[128,256]{1,0:T(8,128)} custom-call(bf16[32768,512]{1,0:T(8,128)(2,1)} %all-gather.2.cloned.1.call-done.ts_ref, bf16[128,256]{1,0:T(8,128)(2,1)} %constant_dynamic-slice_fusion.c_ref, f32[128,1]{1,0:T(8,128)} %copy.15.col_ref, f32[2,32768]{1,0:T(2,128)} %bitcast.19), custom_call_target="tpu_custom_call" | custom-call | tf_op jit(solution)/shard_map/pallas_call | solution.py:41
  266.8 1.6 broadcast_multiply_fusion
  (46 shorter events, 4.8 us)
Async XLA Ops:
  7.2 235.8 %all-gather.2.cloned.1.call-start = ((), (), s32[]{:S(2)}) async-start(), calls=%async_computation.12 | async-start | bytes 34078720 | tf_op jit(solution)/shard_map/all_gather | solution.py:160
  29.4 2.0 copy-start
  129.0 43.4 %copy-start.1 = (bf16[512,512]{1,0:T(8,128)(2,1)S(1)}, bf16[512,512]{1,0:T(8,128)(2,1)}, u32[]{:S(2)}) copy-start(bf16[512,512]{1,0:T(8,128)(2,1)} %all_gather.6) | copy-start | bytes 1572868
  167.7 14.0 %all-to-all-start.8 = ((f32[64,1,128]{2,1,0:T(1,128)}), f32[64,1,128]{2,1,0:T(1,128)S(1)}, u32[]{:S(2)}, u32[]{:S(2)}) async-start(f32[64,1,128]{2,1,0:T(1,128)} %broadcast_in_dim.40), calls=%async_computation.8 | async-start | bytes 65536 | tf_op jit(solution)/shard_map/all_to_all | solution.py:87
  182.3 10.3 %all-to-all-start = ((f32[4,1,512]{2,1,0:T(1,128)}), f32[4,1,512]{2,1,0:T(1,128)S(1)}, u32[]{:S(2)}, u32[]{:S(2)}) async-start(f32[4,1,512]{2,1,0:T(1,128)} %broadcast_in_dim.35), calls=%async_computation | async-start | bytes 16384 | tf_op jit(solution)/shard_map/all_to_all | solution.py:87
  193.2 8.4 %all-to-all-start.9 = ((f32[4,1,512]{2,1,0:T(1,128)}), f32[4,1,512]{2,1,0:T(1,128)S(1)}, u32[]{:S(2)}, u32[]{:S(2)}) async-start(f32[4,1,512]{2,1,0:T(1,128)} %broadcast_in_dim.41), calls=%async_computation.9 | async-start | bytes 16384 | tf_op jit(solution)/shard_map/all_to_all | solution.py:87
  202.4 27.2 %all-to-all-start.10 = ((f32[64,512,2]{1,2,0:T(2,128)}), f32[64,512,2]{1,2,0:T(2,128)S(1)}, u32[]{:S(2)}, u32[]{:S(2)}) async-start(f32[64,512,2]{1,2,0:T(2,128)} %broadcast_in_dim.42), calls=%async_computation.10 | async-start | bytes 524288 | tf_op jit(solution)/shard_map/all_to_all | solution.py:87
  214.5 27.5 %copy-start.3 = (bf16[128,256]{1,0:T(8,128)(2,1)S(1)}, bf16[128,256]{1,0:T(8,128)(2,1)}, u32[]{:S(2)}) copy-start(bf16[128,256]{1,0:T(8,128)(2,1)} %param.4) | copy-start | bytes 196612
  229.6 13.3 %copy-start.2 = (f32[64,512,2]{1,2,0:T(2,128)}, f32[64,512,2]{1,2,0:T(2,128)S(1)}, u32[]{:S(2)}) copy-start(f32[64,512,2]{1,2,0:T(2,128)S(1)} %all-to-all-done.10) | copy-start | bytes 786436
  229.6 12.4 %all-to-all-start.11 = ((f32[4,128,256]{2,1,0:T(8,128)}), f32[4,128,256]{2,1,0:T(8,128)S(1)}, u32[]{:S(2)}, u32[]{:S(2)}) async-start(f32[4,128,256]{2,1,0:T(8,128)} %bitcast.12), calls=%async_computation.11 | async-start | bytes 1048576 | tf_op jit(solution)/shard_map/all_to_all | solution.py:75
Sparse Core Ops, SparseCore 0:
  23.3 149.1 all-gather.1

commit v5 on v4

--- a/solution.py
+++ b/solution.py
@@ -14,7 +14,7 @@
 teacher_temp = 0.05
 student_temp = 0.1
 
-def _protos_kernel(ts_ref, c_ref, col_ref, al_ref, out_ref, *, rows_all, scale, width):
+def _protos_kernel(ts_ref, c_ref, col_ref, al_ref, out_ref, *, width):
     @pl.when(pl.program_id(0) == 0)
     def _():
         out_ref[...] = jnp.zeros_like(out_ref)
@@ -25,21 +25,21 @@
     dims = (((1,), (1,)), ((), ()))
     tl = lax.dot_general(c, t, dims, preferred_element_type=jnp.float32)
     sl = lax.dot_general(c, s, dims, preferred_element_type=jnp.float32)
-    a = al_ref[0:1, :]
-    logz = al_ref[1:2, :]
-    target = rows_all * jnp.exp(tl / teacher_temp) * a * col_ref[...]
-    probs = jnp.exp(sl / student_temp - logz)
-    g = (scale * (probs - target)).astype(jnp.bfloat16)
+    fac = al_ref[0:1, :]
+    shift = al_ref[1:2, :]
+    target = jnp.exp(tl * (1.0 / teacher_temp)) * fac * col_ref[...]
+    probs = jnp.exp(sl * (1.0 / student_temp) - shift)
+    g = (probs - target).astype(jnp.bfloat16)
     out_ref[...] += jnp.dot(g, s, preferred_element_type=jnp.float32)
 
 
-def protos_grad(ts, c_mine, col_mine, al, rows_all, scale, block=2048, interpret=False):
+def protos_grad(ts, c_mine, col_mine, scales, rows_all, scale, block=2048, interpret=False):
     n, w2 = ts.shape
     width = w2 // 2
     m = c_mine.shape[0]
-    kern = functools.partial(_protos_kernel, rows_all=rows_all, scale=scale, width=width)
+    al = jnp.stack([(scale * rows_all) * scales[:, 0], scales[:, 1] - math.log(scale)])
     out = pl.pallas_call(
-        kern,
+        functools.partial(_protos_kernel, width=width),
         grid=(n // block,),
         in_specs=[
             pl.BlockSpec((block, w2), lambda i: (i, 0)),
@@ -160,7 +160,7 @@
     pieces = lax.all_gather(
         jnp.concatenate((tn_group, sn_group), axis=1), "batch", axis=0, tiled=True
     )
-    grad_protos = protos_grad(pieces, c_mine, col_mine, both.T, rows_all, scale)
+    grad_protos = protos_grad(pieces, c_mine, col_mine, both, rows_all, scale)
     _, pull = jax.vjp(unit_rows, student.astype(jnp.float32))
     grad_student = pull(grad_sn)[0]
     return (grad_student, grad_protos)

time: 277 us -> 282 us (1.018)
  blocking collectives: 108 us -> 93.1 us
  waiting for transfers between devices: 10.8 us -> 22.8 us
  starting transfers between devices: 27.7 us -> 33.1 us
    all_to_all x3 -> x2, blocking collectives: 53 us -> 38.4 us  [summed_on_arrival(): lax.all_to_all(parts, axis, split_axis=0, concat_axis=0, tiled=True)]
    all_to_all x4, waiting for transfers between devices: 4.17 us -> 15.2 us  [copy_for_each(): return lax.all_to_all(copies, axis, split_axis=0, concat_axis=0, tiled=True)]
    all_to_all x1 -> x2, starting transfers between devices: 3.48 us -> 9.18 us  [summed_on_arrival(): lax.all_to_all(parts, axis, split_axis=0, concat_axis=0, tiled=True)]
    all_to_all x1 -> x2, waiting for transfers between devices: 6.6 us -> 7.61 us  [summed_on_arrival(): lax.all_to_all(parts, axis, split_axis=0, concat_axis=0, tiled=True)]
  transfers between devices with their start and end apart: 6 -> 7, of which waited for: 2 -> 5; matrix products, arithmetic and copies ran while one was open for 31% -> 31% of each run, Pallas kernels for 0% -> 0%
where the time goes in v5:
time: 282 us; the launch traced here: 280 us
  blocking collectives  93.1 us (33%)
  other arithmetic  53.4 us (19%)
  starting transfers between devices  33.1 us (12%)
  matrix products  32.7 us (12%)
  Pallas kernels  23.8 us (8%)
  waiting for transfers between devices  22.8 us (8%)
  between operations  14.2 us (5%)
  local copies, waits for them, and re-layouts  6.95 us (2%)
    all_to_all x4, blocking collectives, copy_for_each(): return lax.all_to_all(copies, axis, split_axis=0, concat_axis=0, tiled=True)  41.7 us
    all_to_all x2, blocking collectives, summed_on_arrival(): lax.all_to_all(parts, axis, split_axis=0, concat_axis=0, tiled=True)  38.4 us
    all_to_all x4, starting transfers between devices, copy_for_each(): return lax.all_to_all(copies, axis, split_axis=0, concat_axis=0, tiled=True)  23.9 us
    pallas_call x1, Pallas kernels, protos_grad(): pl.pallas_call(functools.partial(_protos_kernel, width=width), grid=(n //...  23.8 us
    reduce_sum x3, other arithmetic, per_device(): sample_local = jnp.sum(weight * col_scale[None, :], axis=1)  22.6 us
    reduce_sum x2, other arithmetic, per_device(): mass_local = jnp.sum(weight * row_scale[:, None], axis=0)  17.8 us
    dot_general x2, matrix products, against(): lax.dot_general(left, right, (((1,), (1,)), ((), ())), preferred_element_...  17.6 us
    all_to_all x4, waiting for transfers between devices, copy_for_each(): return lax.all_to_all(copies, axis, split_axis=0, concat_axis=0, tiled=True)  15.2 us
  transfers between devices with their start and end apart: 7, of which 5 were waited for; matrix products, arithmetic and copies ran while one was open for 31% of the time, Pallas kernels for 0%

profile of v5, /device:TPU:1, one launch (start us, length us, event | category | flops | bytes accessed | tf_op | source)
XLA Modules:
  0.0 280.0 jit_solution(10850211416799619836)
XLA Ops:
  9.1 1.0 fusion.10
  10.1 13.0 %all_gather.6 = bf16[512,512]{1,0:T(8,128)(2,1)} all-gather(bf16[128,512]{1,0:T(8,128)(2,1)S(1)} %pad_maximum_fusion.1), channel_id=1, replica_groups=mesh['proto'=4,'batch'=64] {'proto'}, dimensions={0}, use_global_device_ids=true | all-gather | bytes 655360 | tf_op jit(solution)/shard_map/all_gather | solution.py:64
  23.1 3.3 %fusion = f32[8192]{0:T(1024)S(1)} fusion(bf16[8192,256]{1,0:T(8,128)(2,1)} %param.5), kind=kLoop, calls=%fused_computation.10 | loop fusion | flops 6283264 | bytes 4227072 | tf_op jit(solution)/shard_map/reduce_sum | solution.py:116
  26.5 2.9 %fusion.2 = bf16[8192,256]{1,0:T(8,128)(2,1)S(1)} fusion(bf16[8192,256]{1,0:T(8,128)(2,1)} %param.5, f32[8192]{0:T(1024)S(1)} %add_rsqrt_fusion), kind=kLoop, calls=%fused_computation.12 | loop fusion | flops 8388608 | bytes 8421376 | tf_op jit(solution)/shard_map/convert_element_type | solution.py:135
  29.4 2.0 copy-done
  31.4 8.0 %fusion.18 = (f32[8192]{0:T(1024)S(1)}, f32[512,8192]{1,0:T(8,128)}) fusion(bf16[8192,256]{1,0:T(8,128)(2,1)S(1)} %fusion.2, bf16[512,512]{1,0:T(8,128)(2,1)} %all_gather.6), kind=kOutput, calls=%fused_computation.55 | convolution fusion | flops 2155864064 | bytes 21266432 | tf_op jit(solution)/shard_map/dot_general | solution.py:122
  39.3 23.4 %all_to_all.79 = f32[64,1,128]{2,1,0:T(1,128)S(1)} all-to-all(f32[64,1,128]{2,1,0:T(1,128)S(1)} %bitcast.26), channel_id=1, replica_groups=mesh['proto'=4,'batch'=64] {'batch'}, dimensions={0} | all-to-all | bytes 65536 | tf_op jit(solution)/shard_map/all_to_all | solution.py:75
  62.8 13.4 %all_to_all.80 = f32[64,1,128]{2,1,0:T(1,128)S(1)} all-to-all(f32[64,1,128]{2,1,0:T(1,128)S(1)} %broadcast_in_dim.36), channel_id=1, replica_groups=mesh['proto'=4,'batch'=64] {'batch'}, dimensions={0} | all-to-all | bytes 65536 | tf_op jit(solution)/shard_map/all_to_all | solution.py:87
  76.3 7.3 %multiply_reduce_fusion.4 = f32[512]{0:T(512)S(1)} fusion(f32[512,8192]{1,0:T(8,128)} %get-tuple-element.13, f32[8192]{0:T(1024)S(1)} %bitcast.27), kind=kLoop, calls=%fused_computation.5 | loop fusion | flops 8388096 | bytes 16812032 | tf_op jit(solution)/shard_map/reduce_sum | solution.py:144
  83.5 8.1 %all_to_all.81 = f32[4,1,512]{2,1,0:T(1,128)S(1)} all-to-all(f32[4,1,512]{2,1,0:T(1,128)S(1)} %broadcast_in_dim.37), channel_id=1, replica_groups=mesh['proto'=4,'batch'=64] {'proto'}, dimensions={0} | all-to-all | bytes 16384 | tf_op jit(solution)/shard_map/all_to_all | solution.py:87
  91.7 8.7 %multiply_reduce_fusion.3 = f32[8192]{0:T(1024)S(1)} fusion(f32[512,8192]{1,0:T(8,128)} %get-tuple-element.13, f32[512]{0:T(512)S(1)} %multiply_divide_fusion.2), kind=kLoop, calls=%fused_computation.4 | loop fusion | flops 8380416 | bytes 16812032 | tf_op jit(solution)/shard_map/reduce_sum | solution.py:141
  100.3 15.0 %all_to_all.82 = f32[64,1,128]{2,1,0:T(1,128)S(1)} all-to-all(f32[64,1,128]{2,1,0:T(1,128)S(1)} %bitcast.28), channel_id=1, replica_groups=mesh['proto'=4,'batch'=64] {'batch'}, dimensions={0} | all-to-all | bytes 65536 | tf_op jit(solution)/shard_map/all_to_all | solution.py:75
  115.4 13.6 %all_to_all.83 = f32[64,1,128]{2,1,0:T(1,128)S(1)} all-to-all(f32[64,1,128]{2,1,0:T(1,128)S(1)} %broadcast_in_dim.38), channel_id=1, replica_groups=mesh['proto'=4,'batch'=64] {'batch'}, dimensions={0} | all-to-all | bytes 65536 | tf_op jit(solution)/shard_map/all_to_all | solution.py:87
  129.0 8.3 %multiply_reduce_fusion.2 = f32[512]{0:T(512)S(1)} fusion(f32[512,8192]{1,0:T(8,128)} %get-tuple-element.13, f32[8192]{0:T(1024)S(1)} %bitcast.29), kind=kLoop, calls=%fused_computation.3 | loop fusion | flops 8388096 | bytes 16812032 | tf_op jit(solution)/shard_map/reduce_sum | solution.py:144
  137.3 6.6 %all_to_all.84 = f32[4,1,512]{2,1,0:T(1,128)S(1)} all-to-all(f32[4,1,512]{2,1,0:T(1,128)S(1)} %broadcast_in_dim.39), channel_id=1, replica_groups=mesh['proto'=4,'batch'=64] {'proto'}, dimensions={0} | all-to-all | bytes 16384 | tf_op jit(solution)/shard_map/all_to_all | solution.py:87
  143.9 9.1 %multiply_reduce_fusion.1 = f32[8192]{0:T(1024)} fusion(f32[512,8192]{1,0:T(8,128)} %get-tuple-element.13, f32[512]{0:T(512)S(1)} %multiply_divide_fusion.1), kind=kLoop, calls=%fused_computation.2 | loop fusion | flops 8380416 | bytes 16812032 | tf_op jit(solution)/shard_map/reduce_sum | solution.py:141
  153.0 5.7 %all-to-all-start.7 = ((f32[64,1,128]{2,1,0:T(1,128)}), f32[64,1,128]{2,1,0:T(1,128)S(1)}, u32[]{:S(2)}, u32[]{:S(2)}) async-start(f32[64,1,128]{2,1,0:T(1,128)} %bitcast.6), calls=%async_computation.7 | async-start | bytes 65536 | tf_op jit(solution)/shard_map/all_to_all | solution.py:75
  158.7 9.6 %exponential_reduce_fusion = (f32[512]{0:T(512)S(1)}, f32[512,8192]{1,0:T(8,128)}) fusion(bf16[8192,256]{1,0:T(8,128)(2,1)} %copy-done, bf16[512,512]{1,0:T(8,128)(2,1)S(1)} %copy-done.1), kind=kOutput, calls=%fused_computation.7 | convolution fusion | flops 2155871744 | bytes 21235712 | tf_op jit(solution)/shard_map/dot_general | solution.py:122
  169.0 3.2 %all-to-all-start = ((f32[4,1,512]{2,1,0:T(1,128)}), f32[4,1,512]{2,1,0:T(1,128)S(1)}, u32[]{:S(2)}, u32[]{:S(2)}) async-start(f32[4,1,512]{2,1,0:T(1,128)} %broadcast_in_dim.35), calls=%async_computation | async-start | bytes 16384 | tf_op jit(solution)/shard_map/all_to_all | solution.py:87
  172.3 4.1 %all-to-all-done = f32[4,1,512]{2,1,0:T(1,128)S(1)} async-done(((f32[4,1,512]{2,1,0:T(1,128)}), f32[4,1,512]{2,1,0:T(1,128)S(1)}, u32[]{:S(2)}, u32[]{:S(2)}) %all-to-all-start) | async-done | bytes 8224 | tf_op jit(solution)/shard_map/all_to_all | solution.py:87
  177.0 11.5 %all-to-all-start.8 = ((f32[64,1,128]{2,1,0:T(1,128)}), f32[64,1,128]{2,1,0:T(1,128)S(1)}, u32[]{:S(2)}, u32[]{:S(2)}) async-start(f32[64,1,128]{2,1,0:T(1,128)} %broadcast_in_dim.40), calls=%async_computation.8 | async-start | bytes 65536 | tf_op jit(solution)/shard_map/all_to_all | solution.py:87
  188.5 1.5 constant_dynamic-slice_fusion.c_ref
  190.0 7.7 %all-to-all-done.8 = f32[64,1,128]{2,1,0:T(1,128)S(1)} async-done(((f32[64,1,128]{2,1,0:T(1,128)}), f32[64,1,128]{2,1,0:T(1,128)S(1)}, u32[]{:S(2)}, u32[]{:S(2)}) %all-to-all-start.8) | async-done | bytes 32800 | tf_op jit(solution)/shard_map/all_to_all | solution.py:87
  197.8 7.0 %multiply_reduce_fusion = f32[512]{0:T(512)S(1)} fusion(f32[512,8192]{1,0:T(8,128)} %get-tuple-element.13, f32[8192]{0:T(1024)S(1)} %bitcast.23), kind=kLoop, calls=%fused_computation.1 | loop fusion | flops 8388096 | bytes 16812032 | tf_op jit(solution)/shard_map/reduce_sum | solution.py:144
  205.4 3.2 %all-to-all-start.9 = ((f32[4,1,512]{2,1,0:T(1,128)}), f32[4,1,512]{2,1,0:T(1,128)S(1)}, u32[]{:S(2)}, u32[]{:S(2)}) async-start(f32[4,1,512]{2,1,0:T(1,128)} %broadcast_in_dim.41), calls=%async_computation.9 | async-start | bytes 16384 | tf_op jit(solution)/shard_map/all_to_all | solution.py:87
  209.4 3.3 %all-to-all-done.9 = f32[4,1,512]{2,1,0:T(1,128)S(1)} async-done(((f32[4,1,512]{2,1,0:T(1,128)}), f32[4,1,512]{2,1,0:T(1,128)S(1)}, u32[]{:S(2)}, u32[]{:S(2)}) %all-to-all-start.9) | async-done | bytes 8224 | tf_op jit(solution)/shard_map/all_to_all | solution.py:87
  213.6 5.9 %all-to-all-start.10 = ((f32[64,512,2]{1,2,0:T(2,128)}), f32[64,512,2]{1,2,0:T(2,128)S(1)}, u32[]{:S(2)}, u32[]{:S(2)}) async-start(f32[64,512,2]{1,2,0:T(2,128)} %broadcast_in_dim.42), calls=%async_computation.10 | async-start | bytes 524288 | tf_op jit(solution)/shard_map/all_to_all | solution.py:87
  219.5 15.1 %fusion.4 = f32[512,256]{1,0:T(8,128)} fusion(bf16[8192,256]{1,0:T(8,128)(2,1)} %copy-done, f32[512,8192]{1,0:T(8,128)} %get-tuple-element.13, f32[512,8192]{1,0:T(8,128)} %get-tuple-element.15, f32[512]{0:T(512)S(1)} %get-tuple-element.6, f32[8192]{0:T(1024)S(1)} %bitcast.25, f32[512]{0:T(512)S(1)} %log.14), kind=kOutput, calls=%fused_computation.14 | convolution fusion | flops 2176974848 | bytes 38309888 | tf_op jit(solution)/shard_map/dot_general | solution.py:152
  234.6 3.5 %all-to-all-start.11 = ((f32[4,128,256]{2,1,0:T(8,128)}), f32[4,128,256]{2,1,0:T(8,128)S(1)}, u32[]{:S(2)}, u32[]{:S(2)}) async-start(f32[4,128,256]{2,1,0:T(8,128)} %bitcast.12), calls=%async_computation.11 | async-start | bytes 1048576 | tf_op jit(solution)/shard_map/all_to_all | solution.py:75
  239.3 7.5 %all-to-all-done.11 = f32[4,128,256]{2,1,0:T(8,128)S(1)} async-done(((f32[4,128,256]{2,1,0:T(8,128)}), f32[4,128,256]{2,1,0:T(8,128)S(1)}, u32[]{:S(2)}, u32[]{:S(2)}) %all-to-all-start.11) | async-done | bytes 524320 | tf_op jit(solution)/shard_map/all_to_all | solution.py:75
  247.8 23.8 %shard_map.50 = f32[128,256]{1,0:T(8,128)} custom-call(bf16[32768,512]{1,0:T(8,128)(2,1)} %all-gather.2.cloned.1.call-done.ts_ref, bf16[128,256]{1,0:T(8,128)(2,1)} %constant_dynamic-slice_fusion.c_ref, f32[128,1]{1,0:T(8,128)} %copy.16.col_ref, f32[2,32768]{1,0:T(2,128)} %pad_maximum_fusion.al_ref), custom_call_target="tpu_custom_call" | custom-call | tf_op jit(solution)/shard_map/pallas_call | solution.py:41
  271.6 1.6 broadcast_multiply_fusion
  (47 shorter events, 8.0 us)
Async XLA Ops:
  7.2 240.6 %all-gather.2.cloned.1.call-start = ((), (), s32[]{:S(2)}) async-start(), calls=%async_computation.12 | async-start | bytes 34078720 | tf_op jit(solution)/shard_map/all_gather | solution.py:160
  29.4 2.0 copy-start
  129.0 29.8 %copy-start.1 = (bf16[512,512]{1,0:T(8,128)(2,1)S(1)}, bf16[512,512]{1,0:T(8,128)(2,1)}, u32[]{:S(2)}) copy-start(bf16[512,512]{1,0:T(8,128)(2,1)} %all_gather.6) | copy-start | bytes 1572868
  153.0 15.4 %all-to-all-start.7 = ((f32[64,1,128]{2,1,0:T(1,128)}), f32[64,1,128]{2,1,0:T(1,128)S(1)}, u32[]{:S(2)}, u32[]{:S(2)}) async-start(f32[64,1,128]{2,1,0:T(1,128)} %bitcast.6), calls=%async_computation.7 | async-start | bytes 65536 | tf_op jit(solution)/shard_map/all_to_all | solution.py:75
  169.0 7.4 %all-to-all-start = ((f32[4,1,512]{2,1,0:T(1,128)}), f32[4,1,512]{2,1,0:T(1,128)S(1)}, u32[]{:S(2)}, u32[]{:S(2)}) async-start(f32[4,1,512]{2,1,0:T(1,128)} %broadcast_in_dim.35), calls=%async_computation | async-start | bytes 16384 | tf_op jit(solution)/shard_map/all_to_all | solution.py:87
  177.0 20.7 %all-to-all-start.8 = ((f32[64,1,128]{2,1,0:T(1,128)}), f32[64,1,128]{2,1,0:T(1,128)S(1)}, u32[]{:S(2)}, u32[]{:S(2)}) async-start(f32[64,1,128]{2,1,0:T(1,128)} %broadcast_in_dim.40), calls=%async_computation.8 | async-start | bytes 65536 | tf_op jit(solution)/shard_map/all_to_all | solution.py:87
  205.4 7.4 %all-to-all-start.9 = ((f32[4,1,512]{2,1,0:T(1,128)}), f32[4,1,512]{2,1,0:T(1,128)S(1)}, u32[]{:S(2)}, u32[]{:S(2)}) async-start(f32[4,1,512]{2,1,0:T(1,128)} %broadcast_in_dim.41), calls=%async_computation.9 | async-start | bytes 16384 | tf_op jit(solution)/shard_map/all_to_all | solution.py:87
  213.6 21.0 %all-to-all-start.10 = ((f32[64,512,2]{1,2,0:T(2,128)}), f32[64,512,2]{1,2,0:T(2,128)S(1)}, u32[]{:S(2)}, u32[]{:S(2)}) async-start(f32[64,512,2]{1,2,0:T(2,128)} %broadcast_in_dim.42), calls=%async_computation.10 | async-start | bytes 524288 | tf_op jit(solution)/shard_map/all_to_all | solution.py:87
  219.5 27.4 %copy-start.2 = (bf16[128,256]{1,0:T(8,128)(2,1)S(1)}, bf16[128,256]{1,0:T(8,128)(2,1)}, u32[]{:S(2)}) copy-start(bf16[128,256]{1,0:T(8,128)(2,1)} %param.4) | copy-start | bytes 196612
  234.6 12.2 %all-to-all-start.11 = ((f32[4,128,256]{2,1,0:T(8,128)}), f32[4,128,256]{2,1,0:T(8,128)S(1)}, u32[]{:S(2)}, u32[]{:S(2)}) async-start(f32[4,128,256]{2,1,0:T(8,128)} %bitcast.12), calls=%async_computation.11 | async-start | bytes 1048576 | tf_op jit(solution)/shard_map/all_to_all | solution.py:75
Sparse Core Ops, SparseCore 0:
  23.3 149.1 all-gather.1

commit v6 on v4

--- a/solution.py
+++ b/solution.py
@@ -33,7 +33,7 @@
     out_ref[...] += jnp.dot(g, s, preferred_element_type=jnp.float32)
 
 
-def protos_grad(ts, c_mine, col_mine, al, rows_all, scale, block=2048, interpret=False):
+def protos_grad(ts, c_mine, col_mine, al, rows_all, scale, block=4096, interpret=False):
     n, w2 = ts.shape
     width = w2 // 2
     m = c_mine.shape[0]
@@ -133,7 +133,9 @@
     tn = unit_rows(teacher).astype(jnp.bfloat16)
     sn = unit_rows(student).astype(jnp.bfloat16)
     cn = unit_rows(prototypes).astype(jnp.bfloat16)
-    tn_group, sn_group = side_by_side((tn, sn), "proto", 0, 1)
+    width = tn.shape[1]
+    group = gather_directly(jnp.concatenate((tn, sn), axis=1), "proto", 0)
+    tn_group, sn_group = group[:, :width], group[:, width:]
     weight = jnp.exp(against(tn_group, cn) / teacher_temp)
     row_scale = jnp.ones((tn_group.shape[0],), jnp.float32)
     col_scale = None

time: 277 us -> 271 us (0.978)
  Pallas kernels: 23.9 us -> 19.1 us
  blocking collectives: 108 us -> 105 us
    all_gather x1 -> x0, blocking collectives: 13 us -> none  [side_by_side(): lax.all_gather(both, axis, axis=dim, tiled=True)]
    all_to_all x4 -> x5, blocking collectives: 41.7 us -> 53.1 us  [copy_for_each(): return lax.all_to_all(copies, axis, split_axis=0, concat_axis=0, tiled=True)]
    pallas_call x1, Pallas kernels: 23.9 us -> 19.1 us  [protos_grad(): pl.pallas_call(kern, grid=(n // block,), in_specs=[pl.BlockSpec((block, w...]
  transfers between devices with their start and end apart: 6 -> 6, of which waited for: 2 -> 2; matrix products, arithmetic and copies ran while one was open for 31% -> 32% of each run, Pallas kernels for 0% -> 0%
where the time goes in v6:
time: 271 us; the launch traced here: 270 us
  blocking collectives  105 us (39%)
  other arithmetic  53.4 us (20%)
  matrix products  32.6 us (12%)
  starting transfers between devices  27.7 us (10%)
  Pallas kernels  19.1 us (7%)
  between operations  14.2 us (5%)
  waiting for transfers between devices  10.8 us (4%)
  local copies, waits for them, and re-layouts  6.99 us (3%)
    all_to_all x5, blocking collectives, copy_for_each(): return lax.all_to_all(copies, axis, split_axis=0, concat_axis=0, tiled=True)  53.1 us
    all_to_all x3, blocking collectives, summed_on_arrival(): lax.all_to_all(parts, axis, split_axis=0, concat_axis=0, tiled=True)  52 us
    reduce_sum x3, other arithmetic, per_device(): sample_local = jnp.sum(weight * col_scale[None, :], axis=1)  24.2 us
    all_to_all x4, starting transfers between devices, copy_for_each(): return lax.all_to_all(copies, axis, split_axis=0, concat_axis=0, tiled=True)  24.2 us
    pallas_call x1, Pallas kernels, protos_grad(): pl.pallas_call(kern, grid=(n // block,), in_specs=[pl.BlockSpec((block, w...  19.1 us
    dot_general x2, matrix products, against(): lax.dot_general(left, right, (((1,), (1,)), ((), ())), preferred_element_...  17.5 us
    reduce_sum x2, other arithmetic, per_device(): mass_local = jnp.sum(weight * row_scale[:, None], axis=0)  17.3 us
    dot_general x1, matrix products, per_device(): jnp.dot(grads, cn, preferred_element_type=jnp.float32) / student_temp  15.1 us
  transfers between devices with their start and end apart: 6, of which 2 were waited for; matrix products, arithmetic and copies ran while one was open for 32% of the time, Pallas kernels for 0%

profile of v6, /device:TPU:1, one launch (start us, length us, event | category | flops | bytes accessed | tf_op | source)
XLA Modules:
  0.0 269.9 jit_solution(12127306465751257424)
XLA Ops:
  7.2 0.9 fusion.11
  8.2 1.0 fusion.8
  9.1 1.0 fusion.10
  10.2 12.8 %all_to_all.84 = bf16[4,128,512]{2,1,0:T(8,128)(2,1)} all-to-all(bf16[4,128,512]{2,1,0:T(8,128)(2,1)S(1)} %broadcast_in_dim.38), channel_id=1, replica_groups=mesh['proto'=4,'batch'=64] {'proto'}, dimensions={0} | all-to-all | bytes 1048576 | tf_op jit(solution)/shard_map/all_to_all | solution.py:87
  23.0 3.3 %fusion = f32[8192]{0:T(1024)S(1)} fusion(bf16[8192,256]{1,0:T(8,128)(2,1)} %param.5), kind=kLoop, calls=%fused_computation.10 | loop fusion | flops 6283264 | bytes 4227072 | tf_op jit(solution)/shard_map/reduce_sum | solution.py:116
  26.4 2.9 %fusion.2 = bf16[8192,256]{1,0:T(8,128)(2,1)S(1)} fusion(bf16[8192,256]{1,0:T(8,128)(2,1)} %param.5, f32[8192]{0:T(1024)S(1)} %add_rsqrt_fusion), kind=kLoop, calls=%fused_computation.12 | loop fusion | flops 8388608 | bytes 8421376 | tf_op jit(solution)/shard_map/convert_element_type | solution.py:135
  29.3 2.0 copy-done
  31.3 8.2 %fusion.18 = (f32[8192]{0:T(1024)S(1)}, f32[512,8192]{1,0:T(8,128)}) fusion(bf16[8192,256]{1,0:T(8,128)(2,1)S(1)} %fusion.2, bf16[512,512]{1,0:T(8,128)(2,1)} %bitcast.21), kind=kOutput, calls=%fused_computation.52 | convolution fusion | flops 2155864064 | bytes 21266432 | tf_op jit(solution)/shard_map/dot_general | solution.py:122
  39.5 23.1 %all_to_all.85 = f32[64,1,128]{2,1,0:T(1,128)S(1)} all-to-all(f32[64,1,128]{2,1,0:T(1,128)S(1)} %bitcast.27), channel_id=1, replica_groups=mesh['proto'=4,'batch'=64] {'batch'}, dimensions={0} | all-to-all | bytes 65536 | tf_op jit(solution)/shard_map/all_to_all | solution.py:75
  62.6 13.4 %all_to_all.86 = f32[64,1,128]{2,1,0:T(1,128)S(1)} all-to-all(f32[64,1,128]{2,1,0:T(1,128)S(1)} %broadcast_in_dim.40), channel_id=1, replica_groups=mesh['proto'=4,'batch'=64] {'batch'}, dimensions={0} | all-to-all | bytes 65536 | tf_op jit(solution)/shard_map/all_to_all | solution.py:87
  76.0 8.9 %multiply_reduce_fusion.4 = f32[512]{0:T(512)S(1)} fusion(f32[512,8192]{1,0:T(8,128)} %get-tuple-element.11, f32[8192]{0:T(1024)S(1)} %bitcast.28), kind=kLoop, calls=%fused_computation.5 | loop fusion | flops 8388096 | bytes 16812032 | tf_op jit(solution)/shard_map/reduce_sum | solution.py:146
  84.9 6.6 %all_to_all.87 = f32[4,1,512]{2,1,0:T(1,128)S(1)} all-to-all(f32[4,1,512]{2,1,0:T(1,128)S(1)} %broadcast_in_dim.41), channel_id=1, replica_groups=mesh['proto'=4,'batch'=64] {'proto'}, dimensions={0} | all-to-all | bytes 16384 | tf_op jit(solution)/shard_map/all_to_all | solution.py:87
  91.5 8.8 %multiply_reduce_fusion.3 = f32[8192]{0:T(1024)S(1)} fusion(f32[512,8192]{1,0:T(8,128)} %get-tuple-element.11, f32[512]{0:T(512)S(1)} %multiply_divide_fusion.2), kind=kLoop, calls=%fused_computation.4 | loop fusion | flops 8380416 | bytes 16812032 | tf_op jit(solution)/shard_map/reduce_sum | solution.py:143
  100.4 14.3 %all_to_all.88 = f32[64,1,128]{2,1,0:T(1,128)S(1)} all-to-all(f32[64,1,128]{2,1,0:T(1,128)S(1)} %bitcast.29), channel_id=1, replica_groups=mesh['proto'=4,'batch'=64] {'batch'}, dimensions={0} | all-to-all | bytes 65536 | tf_op jit(solution)/shard_map/all_to_all | solution.py:75
  114.7 13.7 %all_to_all.89 = f32[64,1,128]{2,1,0:T(1,128)S(1)} all-to-all(f32[64,1,128]{2,1,0:T(1,128)S(1)} %broadcast_in_dim.42), channel_id=1, replica_groups=mesh['proto'=4,'batch'=64] {'batch'}, dimensions={0} | all-to-all | bytes 65536 | tf_op jit(solution)/shard_map/all_to_all | solution.py:87
  128.4 8.4 %multiply_reduce_fusion.2 = f32[512]{0:T(512)S(1)} fusion(f32[512,8192]{1,0:T(8,128)} %get-tuple-element.11, f32[8192]{0:T(1024)S(1)} %bitcast.30), kind=kLoop, calls=%fused_computation.3 | loop fusion | flops 8388096 | bytes 16812032 | tf_op jit(solution)/shard_map/reduce_sum | solution.py:146
  136.8 6.6 %all_to_all.90 = f32[4,1,512]{2,1,0:T(1,128)S(1)} all-to-all(f32[4,1,512]{2,1,0:T(1,128)S(1)} %broadcast_in_dim.43), channel_id=1, replica_groups=mesh['proto'=4,'batch'=64] {'proto'}, dimensions={0} | all-to-all | bytes 16384 | tf_op jit(solution)/shard_map/all_to_all | solution.py:87
  143.4 8.5 %multiply_reduce_fusion.1 = f32[8192]{0:T(1024)S(1)} fusion(f32[512,8192]{1,0:T(8,128)} %get-tuple-element.11, f32[512]{0:T(512)S(1)} %multiply_divide_fusion.1), kind=kLoop, calls=%fused_computation.2 | loop fusion | flops 8380416 | bytes 16812032 | tf_op jit(solution)/shard_map/reduce_sum | solution.py:143
  151.9 14.6 %all_to_all.91 = f32[64,1,128]{2,1,0:T(1,128)S(1)} all-to-all(f32[64,1,128]{2,1,0:T(1,128)S(1)} %bitcast.31), channel_id=1, replica_groups=mesh['proto'=4,'batch'=64] {'batch'}, dimensions={0} | all-to-all | bytes 65536 | tf_op jit(solution)/shard_map/all_to_all | solution.py:75
  167.2 4.6 %all-to-all-start.9 = ((f32[64,1,128]{2,1,0:T(1,128)}), f32[64,1,128]{2,1,0:T(1,128)S(1)}, u32[]{:S(2)}, u32[]{:S(2)}) async-start(f32[64,1,128]{2,1,0:T(1,128)} %broadcast_in_dim.44), calls=%async_computation.9 | async-start | bytes 65536 | tf_op jit(solution)/shard_map/all_to_all | solution.py:87
  171.8 9.3 %exponential_reduce_fusion = (f32[512]{0:T(512)S(1)}, f32[512,8192]{1,0:T(8,128)}) fusion(bf16[8192,256]{1,0:T(8,128)(2,1)} %copy-done, bf16[512,512]{1,0:T(8,128)(2,1)S(1)} %bitcast.22), kind=kOutput, calls=%fused_computation.7 | convolution fusion | flops 2155871744 | bytes 21235712 | tf_op jit(solution)/shard_map/dot_general | solution.py:122
  181.7 3.2 %all-to-all-start.1 = ((f32[4,1,512]{2,1,0:T(1,128)}), f32[4,1,512]{2,1,0:T(1,128)S(1)}, u32[]{:S(2)}, u32[]{:S(2)}) async-start(f32[4,1,512]{2,1,0:T(1,128)} %broadcast_in_dim.39), calls=%async_computation.1 | async-start | bytes 16384 | tf_op jit(solution)/shard_map/all_to_all | solution.py:87
  185.0 7.0 %multiply_reduce_fusion = f32[512]{0:T(512)S(1)} fusion(f32[512,8192]{1,0:T(8,128)} %get-tuple-element.11, f32[8192]{0:T(1024)S(1)} %bitcast.24), kind=kLoop, calls=%fused_computation.1 | loop fusion | flops 8388096 | bytes 16812032 | tf_op jit(solution)/shard_map/reduce_sum | solution.py:146
  192.6 4.2 %all-to-all-start.10 = ((f32[4,1,512]{2,1,0:T(1,128)}), f32[4,1,512]{2,1,0:T(1,128)S(1)}, u32[]{:S(2)}, u32[]{:S(2)}) async-start(f32[4,1,512]{2,1,0:T(1,128)} %broadcast_in_dim.45), calls=%async_computation.10 | async-start | bytes 16384 | tf_op jit(solution)/shard_map/all_to_all | solution.py:87
  196.9 4.1 %all-to-all-done.10 = f32[4,1,512]{2,1,0:T(1,128)S(1)} async-done(((f32[4,1,512]{2,1,0:T(1,128)}), f32[4,1,512]{2,1,0:T(1,128)S(1)}, u32[]{:S(2)}, u32[]{:S(2)}) %all-to-all-start.10) | async-done | bytes 8224 | tf_op jit(solution)/shard_map/all_to_all | solution.py:87
  201.8 12.1 %all-to-all-start.11 = ((f32[64,512,2]{1,2,0:T(2,128)}), f32[64,512,2]{1,2,0:T(2,128)S(1)}, u32[]{:S(2)}, u32[]{:S(2)}) async-start(f32[64,512,2]{1,2,0:T(2,128)} %broadcast_in_dim.46), calls=%async_computation.11 | async-start | bytes 524288 | tf_op jit(solution)/shard_map/all_to_all | solution.py:87
  214.0 15.1 %fusion.4 = f32[512,256]{1,0:T(8,128)} fusion(bf16[8192,256]{1,0:T(8,128)(2,1)} %copy-done, f32[512,8192]{1,0:T(8,128)} %get-tuple-element.11, f32[512,8192]{1,0:T(8,128)} %get-tuple-element.13, f32[512]{0:T(512)S(1)} %get-tuple-element.6, f32[8192]{0:T(1024)S(1)} %bitcast.25, f32[512]{0:T(512)S(1)} %log.14), kind=kOutput, calls=%fused_computation.14 | convolution fusion | flops 2176974848 | bytes 38309888 | tf_op jit(solution)/shard_map/dot_general | solution.py:154
  229.1 3.5 %all-to-all-start.12 = ((f32[4,128,256]{2,1,0:T(8,128)}), f32[4,128,256]{2,1,0:T(8,128)S(1)}, u32[]{:S(2)}, u32[]{:S(2)}) async-start(f32[4,128,256]{2,1,0:T(8,128)} %bitcast.13), calls=%async_computation.12 | async-start | bytes 1048576 | tf_op jit(solution)/shard_map/all_to_all | solution.py:75
  232.6 1.5 constant_dynamic-slice_fusion.c_ref
  234.8 6.6 %all-to-all-done.12 = f32[4,128,256]{2,1,0:T(8,128)S(1)} async-done(((f32[4,128,256]{2,1,0:T(8,128)}), f32[4,128,256]{2,1,0:T(8,128)S(1)}, u32[]{:S(2)}, u32[]{:S(2)}) %all-to-all-start.12) | async-done | bytes 524320 | tf_op jit(solution)/shard_map/all_to_all | solution.py:75
  242.4 19.1 %shard_map.50 = f32[128,256]{1,0:T(8,128)} custom-call(bf16[32768,512]{1,0:T(8,128)(2,1)} %all-gather.2.cloned.1.call-done.ts_ref, bf16[128,256]{1,0:T(8,128)(2,1)} %constant_dynamic-slice_fusion.c_ref, f32[128,1]{1,0:T(8,128)} %copy.15.col_ref, f32[2,32768]{1,0:T(2,128)} %bitcast.23), custom_call_target="tpu_custom_call" | custom-call | tf_op jit(solution)/shard_map/pallas_call | solution.py:41
  261.5 1.6 broadcast_multiply_fusion
  (47 shorter events, 4.8 us)
Async XLA Ops:
  7.2 235.2 %all-gather.2.cloned.1.call-start = ((), (), s32[]{:S(2)}) async-start(), calls=%async_computation.13 | async-start | bytes 34078720 | tf_op jit(solution)/shard_map/all_gather | solution.py:162
  29.3 2.0 copy-start
  128.4 43.4 %copy-start.1 = (bf16[4,128,512]{2,1,0:T(8,128)(2,1)S(1)}, bf16[4,128,512]{2,1,0:T(8,128)(2,1)}, u32[]{:S(2)}) copy-start(bf16[4,128,512]{2,1,0:T(8,128)(2,1)} %all_to_all.84) | copy-start | bytes 1572868
  167.2 14.0 %all-to-all-start.9 = ((f32[64,1,128]{2,1,0:T(1,128)}), f32[64,1,128]{2,1,0:T(1,128)S(1)}, u32[]{:S(2)}, u32[]{:S(2)}) async-start(f32[64,1,128]{2,1,0:T(1,128)} %broadcast_in_dim.44), calls=%async_computation.9 | async-start | bytes 65536 | tf_op jit(solution)/shard_map/all_to_all | solution.py:87
  181.7 10.3 %all-to-all-start.1 = ((f32[4,1,512]{2,1,0:T(1,128)}), f32[4,1,512]{2,1,0:T(1,128)S(1)}, u32[]{:S(2)}, u32[]{:S(2)}) async-start(f32[4,1,512]{2,1,0:T(1,128)} %broadcast_in_dim.39), calls=%async_computation.1 | async-start | bytes 16384 | tf_op jit(solution)/shard_map/all_to_all | solution.py:87
  192.6 8.4 %all-to-all-start.10 = ((f32[4,1,512]{2,1,0:T(1,128)}), f32[4,1,512]{2,1,0:T(1,128)S(1)}, u32[]{:S(2)}, u32[]{:S(2)}) async-start(f32[4,1,512]{2,1,0:T(1,128)} %broadcast_in_dim.45), calls=%async_computation.10 | async-start | bytes 16384 | tf_op jit(solution)/shard_map/all_to_all | solution.py:87
  201.8 27.2 %all-to-all-start.11 = ((f32[64,512,2]{1,2,0:T(2,128)}), f32[64,512,2]{1,2,0:T(2,128)S(1)}, u32[]{:S(2)}, u32[]{:S(2)}) async-start(f32[64,512,2]{1,2,0:T(2,128)} %broadcast_in_dim.46), calls=%async_computation.11 | async-start | bytes 524288 | tf_op jit(solution)/shard_map/all_to_all | solution.py:87
  214.0 27.5 %copy-start.3 = (bf16[128,256]{1,0:T(8,128)(2,1)S(1)}, bf16[128,256]{1,0:T(8,128)(2,1)}, u32[]{:S(2)}) copy-start(bf16[128,256]{1,0:T(8,128)(2,1)} %param.4) | copy-start | bytes 196612
  229.1 13.3 %copy-start.2 = (f32[64,512,2]{1,2,0:T(2,128)}, f32[64,512,2]{1,2,0:T(2,128)S(1)}, u32[]{:S(2)}) copy-start(f32[64,512,2]{1,2,0:T(2,128)S(1)} %all-to-all-done.11) | copy-start | bytes 786436
  229.1 12.4 %all-to-all-start.12 = ((f32[4,128,256]{2,1,0:T(8,128)}), f32[4,128,256]{2,1,0:T(8,128)S(1)}, u32[]{:S(2)}, u32[]{:S(2)}) async-start(f32[4,128,256]{2,1,0:T(8,128)} %bitcast.13), calls=%async_computation.12 | async-start | bytes 1048576 | tf_op jit(solution)/shard_map/all_to_all | solution.py:75
Sparse Core Ops, SparseCore 0:
  23.2 147.4 all-gather.1

commit v7 on v6

--- a/solution.py
+++ b/solution.py
@@ -33,7 +33,62 @@
     out_ref[...] += jnp.dot(g, s, preferred_element_type=jnp.float32)
 
 
-def protos_grad(ts, c_mine, col_mine, al, rows_all, scale, block=4096, interpret=False):
+def _col_kernel(t_ref, c_ref, a_ref, out_ref):
+    dims = (((1,), (1,)), ((), ()))
+    w = jnp.exp(
+        lax.dot_general(t_ref[...], c_ref[...], dims, preferred_element_type=jnp.float32)
+        / teacher_temp
+    )
+    out_ref[...] = jnp.sum(w * a_ref[...], axis=0, keepdims=True)
+
+
+def _row_kernel(t_ref, c_ref, col_ref, out_ref):
+    @pl.when(pl.program_id(0) == 0)
+    def _():
+        out_ref[...] = jnp.zeros_like(out_ref)
+
+    dims = (((1,), (1,)), ((), ()))
+    w = jnp.exp(
+        lax.dot_general(t_ref[...], c_ref[...], dims, preferred_element_type=jnp.float32)
+        / teacher_temp
+    )
+    out_ref[...] += jnp.sum(w * col_ref[...], axis=1, keepdims=True)
+
+
+def sweep(tn_group, cn, vec, by_column, block=2048):
+    rows, width = tn_group.shape
+    count = cn.shape[0]
+    specs = [
+        pl.BlockSpec((rows, width), lambda j: (0, 0)),
+        pl.BlockSpec((block, width), lambda j: (j, 0)),
+    ]
+    if by_column:
+        kern, vec = _col_kernel, vec.reshape(rows, 1)
+        specs.append(pl.BlockSpec((rows, 1), lambda j: (0, 0)))
+        out_spec = pl.BlockSpec((1, block), lambda j: (0, j))
+        out_shape = jax.ShapeDtypeStruct((1, count), jnp.float32)
+    else:
+        kern, vec = _row_kernel, vec.reshape(1, count)
+        specs.append(pl.BlockSpec((1, block), lambda j: (0, j)))
+        out_spec = pl.BlockSpec((rows, 1), lambda j: (0, 0))
+        out_shape = jax.ShapeDtypeStruct((rows, 1), jnp.float32)
+    out = pl.pallas_call(
+        kern,
+        grid=(count // block,),
+        in_specs=specs,
+        out_specs=out_spec,
+        out_shape=out_shape,
+        compiler_params=pltpu.CompilerParams(dimension_semantics=("arbitrary",)),
+        cost_estimate=pl.CostEstimate(
+            flops=2 * rows * count * width,
+            transcendentals=rows * count,
+            bytes_accessed=2 * (rows + count) * width,
+        ),
+    )(tn_group, cn, vec)
+    return out.reshape(-1)
+
+
+def protos_grad(ts, c_mine, col_mine, al, rows_all, scale, block=8192, interpret=False):
     n, w2 = ts.shape
     width = w2 // 2
     m = c_mine.shape[0]
@@ -49,7 +104,14 @@
         ],
         out_specs=pl.BlockSpec((m, width), lambda i: (0, 0)),
         out_shape=jax.ShapeDtypeStruct((m, width), jnp.float32),
-        compiler_params=pltpu.CompilerParams(dimension_semantics=("arbitrary",)),
+        compiler_params=pltpu.CompilerParams(
+            dimension_semantics=("arbitrary",), vmem_limit_bytes=56 * 1024 * 1024
+        ),
+        cost_estimate=pl.CostEstimate(
+            flops=6 * n * m * width,
+            transcendentals=2 * n * m,
+            bytes_accessed=2 * n * w2 + 4 * m * width,
+        ),
         interpret=interpret,
     )(ts, c_mine, col_mine.reshape(m, 1), al)
     return out / student_temp
@@ -140,10 +202,13 @@
     row_scale = jnp.ones((tn_group.shape[0],), jnp.float32)
     col_scale = None
     for step in range(ITERS):
-        mass_local = jnp.sum(weight * row_scale[:, None], axis=0)
+        if step == 0:
+            mass_local = jnp.sum(weight * row_scale[:, None], axis=0)
+        else:
+            mass_local = sweep(tn_group, cn, row_scale, True)
         share = summed_on_arrival(mass_local, "batch", 0)
         col_scale = gather_directly(1.0 / (count_all * share), "batch", 0)
-        sample_local = jnp.sum(weight * col_scale[None, :], axis=1)
+        sample_local = sweep(tn_group, cn, col_scale, False)
         row_scale = 1.0 / (rows_all * over_copies(sample_local, "proto"))
     targets = rows_all * weight * row_scale[:, None] * col_scale[None, :]
     logits = against(sn_group, cn) / student_temp

time: 271 us -> 271 us (level)
  other arithmetic: 53.4 us -> 15.3 us
  Pallas kernels: 19.1 us -> 49.6 us
  blocking collectives: 105 us -> 94 us
  waiting for transfers between devices: 10.8 us -> 18.7 us
  starting transfers between devices: 27.7 us -> 32.6 us
  local copies, waits for them, and re-layouts: 6.99 us -> 11.3 us
    reduce_sum x5 -> x0, other arithmetic: 41.5 us -> none  [the longest x3 24.2 us: per_device(): sample_local = jnp.sum(weight * col_scale[None, :], axis=1)]
    pallas_call x0 -> x5, Pallas kernels: none -> 31.4 us  [sweep(): pl.pallas_call(kern, grid=(count // block,), in_specs=specs, out_specs=ou...]
    all_to_all x5 -> x4, blocking collectives: 53.1 us -> 40.4 us  [copy_for_each(): return lax.all_to_all(copies, axis, split_axis=0, concat_axis=0, tiled=True)]
    all_to_all x4 -> x5, waiting for transfers between devices: 4.17 us -> 12.8 us  [copy_for_each(): return lax.all_to_all(copies, axis, split_axis=0, concat_axis=0, tiled=True)]
    all_to_all x4 -> x5, starting transfers between devices: 24.2 us -> 28.9 us  [copy_for_each(): return lax.all_to_all(copies, axis, split_axis=0, concat_axis=0, tiled=True)]
    pallas_call x0 -> x3, other arithmetic: none -> 3.27 us  [sweep(): pl.pallas_call(kern, grid=(count // block,), in_specs=specs, out_specs=ou...]
  transfers between devices with their start and end apart: 6 -> 7, of which waited for: 2 -> 3; matrix products, arithmetic and copies ran while one was open for 32% -> 20% of each run, Pallas kernels for 0% -> 12%
where the time goes in v7:
time: 271 us; the launch traced here: 269 us
  blocking collectives  94 us (35%)
  Pallas kernels  49.6 us (18%)
  matrix products  33.4 us (12%)
  starting transfers between devices  32.6 us (12%)
  waiting for transfers between devices  18.7 us (7%)
  other arithmetic  15.3 us (6%)
  between operations  14.3 us (5%)
  local copies, waits for them, and re-layouts  11.3 us (4%)
    all_to_all x3, blocking collectives, summed_on_arrival(): lax.all_to_all(parts, axis, split_axis=0, concat_axis=0, tiled=True)  53.6 us
    all_to_all x4, blocking collectives, copy_for_each(): return lax.all_to_all(copies, axis, split_axis=0, concat_axis=0, tiled=True)  40.4 us
    pallas_call x5, Pallas kernels, sweep(): pl.pallas_call(kern, grid=(count // block,), in_specs=specs, out_specs=ou...  31.4 us
    all_to_all x5, starting transfers between devices, copy_for_each(): return lax.all_to_all(copies, axis, split_axis=0, concat_axis=0, tiled=True)  28.9 us
    pallas_call x1, Pallas kernels, protos_grad(): pl.pallas_call(kern, grid=(n // block,), in_specs=[pl.BlockSpec((block, w...  18.2 us
    dot_general x2, matrix products, against(): lax.dot_general(left, right, (((1,), (1,)), ((), ())), preferred_element_...  17.5 us
    dot_general x1, matrix products, per_device(): jnp.dot(grads, cn, preferred_element_type=jnp.float32) / student_temp  15.9 us
    all_to_all x5, waiting for transfers between devices, copy_for_each(): return lax.all_to_all(copies, axis, split_axis=0, concat_axis=0, tiled=True)  12.8 us
  transfers between devices with their start and end apart: 7, of which 3 were waited for; matrix products, arithmetic and copies ran while one was open for 20% of the time, Pallas kernels for 12%

profile of v7, /device:TPU:1, one launch (start us, length us, event | category | flops | bytes accessed | tf_op | source)
XLA Modules:
  0.0 269.3 jit_solution(9911440765539668313)
XLA Ops:
  10.2 12.8 %all_to_all.84 = bf16[4,128,512]{2,1,0:T(8,128)(2,1)} all-to-all(bf16[4,128,512]{2,1,0:T(8,128)(2,1)S(1)} %broadcast_in_dim.42), channel_id=1, replica_groups=mesh['proto'=4,'batch'=64] {'proto'}, dimensions={0} | all-to-all | bytes 1048576 | tf_op jit(solution)/shard_map/all_to_all | solution.py:149
  23.0 3.4 %fusion.1 = f32[8192]{0:T(1024)S(1)} fusion(bf16[8192,256]{1,0:T(8,128)(2,1)} %param.5), kind=kLoop, calls=%fused_computation.6 | loop fusion | flops 6283264 | bytes 4227072 | tf_op jit(solution)/shard_map/reduce_sum | solution.py:178
  26.5 2.9 %fusion.3.c_ref = bf16[8192,256]{1,0:T(8,128)(2,1)S(1)} fusion(bf16[8192,256]{1,0:T(8,128)(2,1)} %param.5, f32[8192]{0:T(1024)S(1)} %add_rsqrt_fusion), kind=kLoop, calls=%fused_computation.8 | loop fusion | flops 8388608 | bytes 8421376 | tf_op jit(solution)/shard_map/convert_element_type | solution.py:197
  29.4 2.0 copy-done
  31.3 8.2 %fusion = (f32[8192]{0:T(1024)S(1)}, f32[512,8192]{1,0:T(8,128)}) fusion(bf16[8192,256]{1,0:T(8,128)(2,1)S(1)} %fusion.3.c_ref, bf16[512,512]{1,0:T(8,128)(2,1)} %bitcast.26), kind=kOutput, calls=%fused_computation.3 | convolution fusion | flops 2155864064 | bytes 21266432 | tf_op jit(solution)/shard_map/dot_general | solution.py:184
  39.5 23.1 %all_to_all.85 = f32[64,1,128]{2,1,0:T(1,128)S(1)} all-to-all(f32[64,1,128]{2,1,0:T(1,128)S(1)} %bitcast.30), channel_id=1, replica_groups=mesh['proto'=4,'batch'=64] {'batch'}, dimensions={0} | all-to-all | bytes 65536 | tf_op jit(solution)/shard_map/all_to_all | solution.py:137
  63.3 4.7 %all-to-all-start.3 = ((f32[64,1,128]{2,1,0:T(1,128)}), f32[64,1,128]{2,1,0:T(1,128)S(1)}, u32[]{:S(2)}, u32[]{:S(2)}) async-start(f32[64,1,128]{2,1,0:T(1,128)} %broadcast_in_dim.44), calls=%async_computation.3 | async-start | bytes 65536 | tf_op jit(solution)/shard_map/all_to_all | solution.py:149
  68.7 8.6 %all-to-all-done.3 = f32[64,1,128]{2,1,0:T(1,128)S(1)} async-done(((f32[64,1,128]{2,1,0:T(1,128)}), f32[64,1,128]{2,1,0:T(1,128)S(1)}, u32[]{:S(2)}, u32[]{:S(2)}) %all-to-all-start.3) | async-done | bytes 32800 | tf_op jit(solution)/shard_map/all_to_all | solution.py:149
  78.0 6.5 %shard_map.50 = f32[512,1]{1,0:T(8,128)} custom-call(bf16[512,256]{1,0:T(8,128)(2,1)} %slice.10.t_ref, bf16[8192,256]{1,0:T(8,128)(2,1)} %copy-done, f32[1,8192]{1,0:T(1,128)} %bitcast.35), custom_call_target="tpu_custom_call" | custom-call | flops 2147483648 | bytes 4456448 | tf_op jit(solution)/shard_map/pallas_call | solution.py:75
  84.5 1.1 reduce.7
  85.6 6.6 %all_to_all.86 = f32[4,1,512]{2,1,0:T(1,128)S(1)} all-to-all(f32[4,1,512]{2,1,0:T(1,128)S(1)} %broadcast_in_dim.46), channel_id=1, replica_groups=mesh['proto'=4,'batch'=64] {'proto'}, dimensions={0} | all-to-all | bytes 16384 | tf_op jit(solution)/shard_map/all_to_all | solution.py:149
  93.1 6.1 %shard_map.51 = f32[1,8192]{1,0:T(1,128)} custom-call(bf16[512,256]{1,0:T(8,128)(2,1)} %slice.10.t_ref, bf16[8192,256]{1,0:T(8,128)(2,1)} %copy-done, f32[512,1]{1,0:T(8,128)} %copy.22.a_ref), custom_call_target="tpu_custom_call" | custom-call | flops 2147483648 | bytes 4456448 | tf_op jit(solution)/shard_map/pallas_call | solution.py:75
  99.2 15.2 %all_to_all.87 = f32[64,1,128]{2,1,0:T(1,128)S(1)} all-to-all(f32[64,1,128]{2,1,0:T(1,128)} %bitcast.36), channel_id=1, replica_groups=mesh['proto'=4,'batch'=64] {'batch'}, dimensions={0} | all-to-all | bytes 65536 | tf_op jit(solution)/shard_map/all_to_all | solution.py:137
  114.5 14.3 %all_to_all.88 = f32[64,1,128]{2,1,0:T(1,128)} all-to-all(f32[64,1,128]{2,1,0:T(1,128)S(1)} %broadcast_in_dim.47), channel_id=1, replica_groups=mesh['proto'=4,'batch'=64] {'batch'}, dimensions={0} | all-to-all | bytes 65536 | tf_op jit(solution)/shard_map/all_to_all | solution.py:149
  128.9 6.5 %shard_map.52 = f32[512,1]{1,0:T(8,128)} custom-call(bf16[512,256]{1,0:T(8,128)(2,1)} %slice.10.t_ref, bf16[8192,256]{1,0:T(8,128)(2,1)} %copy-done, f32[1,8192]{1,0:T(1,128)} %bitcast.37), custom_call_target="tpu_custom_call" | custom-call | flops 2147483648 | bytes 4456448 | tf_op jit(solution)/shard_map/pallas_call | solution.py:75
  135.4 1.1 reduce.8
  136.5 6.6 %all_to_all.89 = f32[4,1,512]{2,1,0:T(1,128)S(1)} all-to-all(f32[4,1,512]{2,1,0:T(1,128)S(1)} %broadcast_in_dim.49), channel_id=1, replica_groups=mesh['proto'=4,'batch'=64] {'proto'}, dimensions={0} | all-to-all | bytes 16384 | tf_op jit(solution)/shard_map/all_to_all | solution.py:149
  144.0 6.1 %shard_map.53 = f32[1,8192]{1,0:T(1,128)} custom-call(bf16[512,256]{1,0:T(8,128)(2,1)} %slice.10.t_ref, bf16[8192,256]{1,0:T(8,128)(2,1)} %copy-done, f32[512,1]{1,0:T(8,128)} %copy.25.a_ref), custom_call_target="tpu_custom_call" | custom-call | flops 2147483648 | bytes 4456448 | tf_op jit(solution)/shard_map/pallas_call | solution.py:75
  150.0 15.3 %all_to_all.90 = f32[64,1,128]{2,1,0:T(1,128)S(1)} all-to-all(f32[64,1,128]{2,1,0:T(1,128)} %bitcast.38), channel_id=1, replica_groups=mesh['proto'=4,'batch'=64] {'batch'}, dimensions={0} | all-to-all | bytes 65536 | tf_op jit(solution)/shard_map/all_to_all | solution.py:137
  166.1 4.6 %all-to-all-start.9 = ((f32[64,1,128]{2,1,0:T(1,128)}), f32[64,1,128]{2,1,0:T(1,128)S(1)}, u32[]{:S(2)}, u32[]{:S(2)}) async-start(f32[64,1,128]{2,1,0:T(1,128)} %broadcast_in_dim.50), calls=%async_computation.9 | async-start | bytes 65536 | tf_op jit(solution)/shard_map/all_to_all | solution.py:149
  170.7 9.3 %exponential_reduce_fusion = (f32[512]{0:T(512)S(1)}, f32[512,8192]{1,0:T(8,128)}) fusion(bf16[8192,256]{1,0:T(8,128)(2,1)} %copy-done, bf16[512,512]{1,0:T(8,128)(2,1)S(1)} %bitcast.28), kind=kOutput, calls=%fused_computation.2 | convolution fusion | flops 2155871744 | bytes 21235712 | tf_op jit(solution)/shard_map/dot_general | solution.py:184
  180.7 3.2 %all-to-all-start.1 = ((f32[4,1,512]{2,1,0:T(1,128)}), f32[4,1,512]{2,1,0:T(1,128)S(1)}, u32[]{:S(2)}, u32[]{:S(2)}) async-start(f32[4,1,512]{2,1,0:T(1,128)} %broadcast_in_dim.43), calls=%async_computation.1 | async-start | bytes 16384 | tf_op jit(solution)/shard_map/all_to_all | solution.py:149
  183.9 6.3 %shard_map.54 = f32[512,1]{1,0:T(8,128)} custom-call(bf16[512,256]{1,0:T(8,128)(2,1)} %slice.10.t_ref, bf16[8192,256]{1,0:T(8,128)(2,1)} %copy-done, f32[1,8192]{1,0:T(1,128)} %bitcast.32), custom_call_target="tpu_custom_call" | custom-call | flops 2147483648 | bytes 4456448 | tf_op jit(solution)/shard_map/pallas_call | solution.py:75
  191.9 4.2 %all-to-all-start.10 = ((f32[4,1,512]{2,1,0:T(1,128)}), f32[4,1,512]{2,1,0:T(1,128)S(1)}, u32[]{:S(2)}, u32[]{:S(2)}) async-start(f32[4,1,512]{2,1,0:T(1,128)} %broadcast_in_dim.52), calls=%async_computation.10 | async-start | bytes 16384 | tf_op jit(solution)/shard_map/all_to_all | solution.py:149
  196.1 4.1 %all-to-all-done.10 = f32[4,1,512]{2,1,0:T(1,128)S(1)} async-done(((f32[4,1,512]{2,1,0:T(1,128)}), f32[4,1,512]{2,1,0:T(1,128)S(1)}, u32[]{:S(2)}, u32[]{:S(2)}) %all-to-all-start.10) | async-done | bytes 8224 | tf_op jit(solution)/shard_map/all_to_all | solution.py:149
  201.1 12.1 %all-to-all-start.11 = ((f32[64,512,2]{1,2,0:T(2,128)}), f32[64,512,2]{1,2,0:T(2,128)S(1)}, u32[]{:S(2)}, u32[]{:S(2)}) async-start(f32[64,512,2]{1,2,0:T(2,128)} %broadcast_in_dim.53), calls=%async_computation.11 | async-start | bytes 524288 | tf_op jit(solution)/shard_map/all_to_all | solution.py:149
  213.2 15.9 %fusion.5 = f32[512,256]{1,0:T(8,128)} fusion(bf16[8192,256]{1,0:T(8,128)(2,1)} %copy-done, f32[512,8192]{1,0:T(8,128)} %get-tuple-element.13, f32[512,8192]{1,0:T(8,128)} %get-tuple-element.11, f32[8192]{0:T(1024)} %bitcast.33, f32[512]{0:T(512)S(1)} %get-tuple-element.6, f32[512]{0:T(512)S(1)} %log.14), kind=kOutput, calls=%fused_computation.10 | convolution fusion | flops 2181169152 | bytes 38309888 | tf_op jit(solution)/shard_map/dot_general | solution.py:219
  229.2 3.7 %all-to-all-start.12 = ((f32[4,128,256]{2,1,0:T(8,128)}), f32[4,128,256]{2,1,0:T(8,128)S(1)}, u32[]{:S(2)}, u32[]{:S(2)}) async-start(f32[4,128,256]{2,1,0:T(8,128)} %bitcast.16), calls=%async_computation.12 | async-start | bytes 1048576 | tf_op jit(solution)/shard_map/all_to_all | solution.py:137
  232.9 1.5 constant_dynamic-slice_fusion.c_ref
  235.8 5.9 %all-to-all-done.12 = f32[4,128,256]{2,1,0:T(8,128)S(1)} async-done(((f32[4,128,256]{2,1,0:T(8,128)}), f32[4,128,256]{2,1,0:T(8,128)S(1)}, u32[]{:S(2)}, u32[]{:S(2)}) %all-to-all-start.12) | async-done | bytes 524320 | tf_op jit(solution)/shard_map/all_to_all | solution.py:137
  242.7 18.2 %shard_map.55 = f32[128,256]{1,0:T(8,128)} custom-call(bf16[32768,512]{1,0:T(8,128)(2,1)} %all-gather.2.cloned.1.call-done.ts_ref, bf16[128,256]{1,0:T(8,128)(2,1)} %constant_dynamic-slice_fusion.c_ref, f32[128,1]{1,0:T(8,128)} %copy.28.col_ref, f32[2,32768]{1,0:T(2,128)} %bitcast.29), custom_call_target="tpu_custom_call" | custom-call | flops 6442450944 | bytes 33685504 | tf_op jit(solution)/shard_map/pallas_call | solution.py:96
  260.9 1.6 broadcast_multiply_fusion
  (58 shorter events, 13.3 us)
Async XLA Ops:
  7.2 235.5 %all-gather.2.cloned.1.call-start = ((), (), s32[]{:S(2)}) async-start(), calls=%async_computation.13 | async-start | bytes 34078720 | tf_op jit(solution)/shard_map/all_gather | solution.py:227
  23.0 45.0 %copy-start.1 = (bf16[4,128,512]{2,1,0:T(8,128)(2,1)S(1)}, bf16[4,128,512]{2,1,0:T(8,128)(2,1)}, u32[]{:S(2)}) copy-start(bf16[4,128,512]{2,1,0:T(8,128)(2,1)} %all_to_all.84) | copy-start | bytes 1572868
  29.3 2.0 copy-start
  63.3 14.1 %all-to-all-start.3 = ((f32[64,1,128]{2,1,0:T(1,128)}), f32[64,1,128]{2,1,0:T(1,128)S(1)}, u32[]{:S(2)}, u32[]{:S(2)}) async-start(f32[64,1,128]{2,1,0:T(1,128)} %broadcast_in_dim.44), calls=%async_computation.3 | async-start | bytes 65536 | tf_op jit(solution)/shard_map/all_to_all | solution.py:149
  77.4 0.6 copy-start.5
  166.1 14.0 %all-to-all-start.9 = ((f32[64,1,128]{2,1,0:T(1,128)}), f32[64,1,128]{2,1,0:T(1,128)S(1)}, u32[]{:S(2)}, u32[]{:S(2)}) async-start(f32[64,1,128]{2,1,0:T(1,128)} %broadcast_in_dim.50), calls=%async_computation.9 | async-start | bytes 65536 | tf_op jit(solution)/shard_map/all_to_all | solution.py:149
  180.1 3.9 %copy-start.4 = (f32[64,1,128]{2,1,0:T(1,128)}, f32[64,1,128]{2,1,0:T(1,128)S(1)}, u32[]{:S(2)}) copy-start(f32[64,1,128]{2,1,0:T(1,128)S(1)} %all-to-all-done.9) | copy-start | bytes 98308
  180.7 10.6 %all-to-all-start.1 = ((f32[4,1,512]{2,1,0:T(1,128)}), f32[4,1,512]{2,1,0:T(1,128)S(1)}, u32[]{:S(2)}, u32[]{:S(2)}) async-start(f32[4,1,512]{2,1,0:T(1,128)} %broadcast_in_dim.43), calls=%async_computation.1 | async-start | bytes 16384 | tf_op jit(solution)/shard_map/all_to_all | solution.py:149
  191.9 8.3 %all-to-all-start.10 = ((f32[4,1,512]{2,1,0:T(1,128)}), f32[4,1,512]{2,1,0:T(1,128)S(1)}, u32[]{:S(2)}, u32[]{:S(2)}) async-start(f32[4,1,512]{2,1,0:T(1,128)} %broadcast_in_dim.52), calls=%async_computation.10 | async-start | bytes 16384 | tf_op jit(solution)/shard_map/all_to_all | solution.py:149
  201.1 28.1 %all-to-all-start.11 = ((f32[64,512,2]{1,2,0:T(2,128)}), f32[64,512,2]{1,2,0:T(2,128)S(1)}, u32[]{:S(2)}, u32[]{:S(2)}) async-start(f32[64,512,2]{1,2,0:T(2,128)} %broadcast_in_dim.53), calls=%async_computation.11 | async-start | bytes 524288 | tf_op jit(solution)/shard_map/all_to_all | solution.py:149
  213.2 28.6 %copy-start.3 = (bf16[128,256]{1,0:T(8,128)(2,1)S(1)}, bf16[128,256]{1,0:T(8,128)(2,1)}, u32[]{:S(2)}) copy-start(bf16[128,256]{1,0:T(8,128)(2,1)} %param.4) | copy-start | bytes 196612
  229.2 13.5 %copy-start.2 = (f32[64,512,2]{1,2,0:T(2,128)}, f32[64,512,2]{1,2,0:T(2,128)S(1)}, u32[]{:S(2)}) copy-start(f32[64,512,2]{1,2,0:T(2,128)S(1)} %all-to-all-done.11) | copy-start | bytes 786436
  229.2 12.6 %all-to-all-start.12 = ((f32[4,128,256]{2,1,0:T(8,128)}), f32[4,128,256]{2,1,0:T(8,128)S(1)}, u32[]{:S(2)}, u32[]{:S(2)}) async-start(f32[4,128,256]{2,1,0:T(8,128)} %bitcast.16), calls=%async_computation.12 | async-start | bytes 1048576 | tf_op jit(solution)/shard_map/all_to_all | solution.py:137
Sparse Core Ops, SparseCore 0:
  23.2 147.2 all-gather.1

commit v8 on v7

--- a/solution.py
+++ b/solution.py
@@ -78,7 +78,9 @@
         in_specs=specs,
         out_specs=out_spec,
         out_shape=out_shape,
-        compiler_params=pltpu.CompilerParams(dimension_semantics=("arbitrary",)),
+        compiler_params=pltpu.CompilerParams(
+            dimension_semantics=("arbitrary",), vmem_limit_bytes=56 * 1024 * 1024
+        ),
         cost_estimate=pl.CostEstimate(
             flops=2 * rows * count * width,
             transcendentals=rows * count,
@@ -202,10 +204,7 @@
     row_scale = jnp.ones((tn_group.shape[0],), jnp.float32)
     col_scale = None
     for step in range(ITERS):
-        if step == 0:
-            mass_local = jnp.sum(weight * row_scale[:, None], axis=0)
-        else:
-            mass_local = sweep(tn_group, cn, row_scale, True)
+        mass_local = sweep(tn_group, cn, row_scale, True)
         share = summed_on_arrival(mass_local, "batch", 0)
         col_scale = gather_directly(1.0 / (count_all * share), "batch", 0)
         sample_local = sweep(tn_group, cn, col_scale, False)

time: 271 us -> 270 us (level)
  blocking collectives: 94 us -> 108 us
  matrix products: 33.4 us -> 24.9 us
  waiting for transfers between devices: 18.7 us -> 10.3 us
  Pallas kernels: 49.6 us -> 55.7 us
  starting transfers between devices: 32.6 us -> 27.7 us
    all_to_all x4 -> x5, blocking collectives: 40.4 us -> 54.3 us  [copy_for_each(): return lax.all_to_all(copies, axis, split_axis=0, concat_axis=0, tiled=True)]
    all_to_all x5 -> x4, waiting for transfers between devices: 12.8 us -> 4.17 us  [copy_for_each(): return lax.all_to_all(copies, axis, split_axis=0, concat_axis=0, tiled=True)]
    dot_general x2 -> x1, matrix products: 17.5 us -> 9.31 us  [against(): lax.dot_general(left, right, (((1,), (1,)), ((), ())), preferred_element_...]
    pallas_call x5 -> x6, Pallas kernels: 31.4 us -> 37.6 us  [sweep(): pl.pallas_call(kern, grid=(count // block,), in_specs=specs, out_specs=ou...]
    all_to_all x5 -> x4, starting transfers between devices: 28.9 us -> 24.2 us  [copy_for_each(): return lax.all_to_all(copies, axis, split_axis=0, concat_axis=0, tiled=True)]
  transfers between devices with their start and end apart: 7 -> 6, of which waited for: 3 -> 2; matrix products, arithmetic and copies ran while one was open for 20% -> 18% of each run, Pallas kernels for 12% -> 14%
where the time goes in v8:
time: 270 us; the launch traced here: 268 us
  blocking collectives  108 us (40%)
  Pallas kernels  55.7 us (21%)
  starting transfers between devices  27.7 us (10%)
  matrix products  24.9 us (9%)
  other arithmetic  16.7 us (6%)
  between operations  14.2 us (5%)
  waiting for transfers between devices  10.3 us (4%)
  local copies, waits for them, and re-layouts  9.79 us (4%)
    all_to_all x5, blocking collectives, copy_for_each(): return lax.all_to_all(copies, axis, split_axis=0, concat_axis=0, tiled=True)  54.3 us
    all_to_all x3, blocking collectives, summed_on_arrival(): lax.all_to_all(parts, axis, split_axis=0, concat_axis=0, tiled=True)  54.1 us
    pallas_call x6, Pallas kernels, sweep(): pl.pallas_call(kern, grid=(count // block,), in_specs=specs, out_specs=ou...  37.6 us
    all_to_all x4, starting transfers between devices, copy_for_each(): return lax.all_to_all(copies, axis, split_axis=0, concat_axis=0, tiled=True)  24.2 us
    pallas_call x1, Pallas kernels, protos_grad(): pl.pallas_call(kern, grid=(n // block,), in_specs=[pl.BlockSpec((block, w...  18.2 us
    dot_general x1, matrix products, per_device(): jnp.dot(grads, cn, preferred_element_type=jnp.float32) / student_temp  15.6 us
    dot_general x1, matrix products, against(): lax.dot_general(left, right, (((1,), (1,)), ((), ())), preferred_element_...  9.31 us
    all_to_all x1, waiting for transfers between devices, summed_on_arrival(): lax.all_to_all(parts, axis, split_axis=0, concat_axis=0, tiled=True)  6.12 us
  transfers between devices with their start and end apart: 6, of which 2 were waited for; matrix products, arithmetic and copies ran while one was open for 18% of the time, Pallas kernels for 14%

profile of v8, /device:TPU:1, one launch (start us, length us, event | category | flops | bytes accessed | tf_op | source)
XLA Modules:
  0.0 267.8 jit_solution(429222202860586972)
XLA Ops:
  10.2 12.8 %all_to_all.84 = bf16[4,128,512]{2,1,0:T(8,128)(2,1)} all-to-all(bf16[4,128,512]{2,1,0:T(8,128)(2,1)S(1)} %broadcast_in_dim.42), channel_id=1, replica_groups=mesh['proto'=4,'batch'=64] {'proto'}, dimensions={0} | all-to-all | bytes 1048576 | tf_op jit(solution)/shard_map/all_to_all | solution.py:151
  23.0 3.3 %fusion = f32[8192]{0:T(1024)S(1)} fusion(bf16[8192,256]{1,0:T(8,128)(2,1)} %param.5), kind=kLoop, calls=%fused_computation.4 | loop fusion | flops 6283264 | bytes 4227072 | tf_op jit(solution)/shard_map/reduce_sum | solution.py:180
  26.4 4.2 %fusion.2.c_ref = bf16[8192,256]{1,0:T(8,128)(2,1)} fusion(bf16[8192,256]{1,0:T(8,128)(2,1)} %param.5, f32[8192]{0:T(1024)S(1)} %add_rsqrt_fusion), kind=kLoop, calls=%fused_computation.6 | loop fusion | flops 8388608 | bytes 8421376 | tf_op jit(solution)/shard_map/convert_element_type | solution.py:199
  30.6 1.7 slice.10.t_ref
  33.0 6.1 %shard_map.50 = f32[1,8192]{1,0:T(1,128)} custom-call(bf16[512,256]{1,0:T(8,128)(2,1)} %slice.10.t_ref, bf16[8192,256]{1,0:T(8,128)(2,1)} %fusion.2.c_ref, f32[512,1]{1,0:T(8,128)} %broadcast.157.a_ref), custom_call_target="tpu_custom_call" | custom-call | flops 2147483648 | bytes 4456448 | tf_op jit(solution)/shard_map/pallas_call | solution.py:75
  39.1 23.4 %all_to_all.85 = f32[64,1,128]{2,1,0:T(1,128)S(1)} all-to-all(f32[64,1,128]{2,1,0:T(1,128)} %bitcast.34), channel_id=1, replica_groups=mesh['proto'=4,'batch'=64] {'batch'}, dimensions={0} | all-to-all | bytes 65536 | tf_op jit(solution)/shard_map/all_to_all | solution.py:139
  62.6 14.0 %all_to_all.86 = f32[64,1,128]{2,1,0:T(1,128)} all-to-all(f32[64,1,128]{2,1,0:T(1,128)S(1)} %broadcast_in_dim.44), channel_id=1, replica_groups=mesh['proto'=4,'batch'=64] {'batch'}, dimensions={0} | all-to-all | bytes 65536 | tf_op jit(solution)/shard_map/all_to_all | solution.py:151
  76.6 6.6 %shard_map.51 = f32[512,1]{1,0:T(8,128)} custom-call(bf16[512,256]{1,0:T(8,128)(2,1)} %slice.10.t_ref, bf16[8192,256]{1,0:T(8,128)(2,1)} %fusion.2.c_ref, f32[1,8192]{1,0:T(1,128)} %bitcast.35), custom_call_target="tpu_custom_call" | custom-call | flops 2147483648 | bytes 4456448 | tf_op jit(solution)/shard_map/pallas_call | solution.py:75
  83.2 1.1 reduce.7
  84.3 6.6 %all_to_all.87 = f32[4,1,512]{2,1,0:T(1,128)S(1)} all-to-all(f32[4,1,512]{2,1,0:T(1,128)S(1)} %broadcast_in_dim.46), channel_id=1, replica_groups=mesh['proto'=4,'batch'=64] {'proto'}, dimensions={0} | all-to-all | bytes 16384 | tf_op jit(solution)/shard_map/all_to_all | solution.py:151
  91.8 6.1 %shard_map.52 = f32[1,8192]{1,0:T(1,128)} custom-call(bf16[512,256]{1,0:T(8,128)(2,1)} %slice.10.t_ref, bf16[8192,256]{1,0:T(8,128)(2,1)} %fusion.2.c_ref, f32[512,1]{1,0:T(8,128)} %copy.24.a_ref), custom_call_target="tpu_custom_call" | custom-call | flops 2147483648 | bytes 4456448 | tf_op jit(solution)/shard_map/pallas_call | solution.py:75
  97.9 15.1 %all_to_all.88 = f32[64,1,128]{2,1,0:T(1,128)S(1)} all-to-all(f32[64,1,128]{2,1,0:T(1,128)} %bitcast.36), channel_id=1, replica_groups=mesh['proto'=4,'batch'=64] {'batch'}, dimensions={0} | all-to-all | bytes 65536 | tf_op jit(solution)/shard_map/all_to_all | solution.py:139
  113.2 14.3 %all_to_all.89 = f32[64,1,128]{2,1,0:T(1,128)} all-to-all(f32[64,1,128]{2,1,0:T(1,128)S(1)} %broadcast_in_dim.47), channel_id=1, replica_groups=mesh['proto'=4,'batch'=64] {'batch'}, dimensions={0} | all-to-all | bytes 65536 | tf_op jit(solution)/shard_map/all_to_all | solution.py:151
  127.5 6.4 %shard_map.53 = f32[512,1]{1,0:T(8,128)} custom-call(bf16[512,256]{1,0:T(8,128)(2,1)} %slice.10.t_ref, bf16[8192,256]{1,0:T(8,128)(2,1)} %fusion.2.c_ref, f32[1,8192]{1,0:T(1,128)} %bitcast.37), custom_call_target="tpu_custom_call" | custom-call | flops 2147483648 | bytes 4456448 | tf_op jit(solution)/shard_map/pallas_call | solution.py:75
  133.9 1.1 reduce.8
  135.0 6.6 %all_to_all.90 = f32[4,1,512]{2,1,0:T(1,128)S(1)} all-to-all(f32[4,1,512]{2,1,0:T(1,128)S(1)} %broadcast_in_dim.49), channel_id=1, replica_groups=mesh['proto'=4,'batch'=64] {'proto'}, dimensions={0} | all-to-all | bytes 16384 | tf_op jit(solution)/shard_map/all_to_all | solution.py:151
  142.5 6.1 %shard_map.54 = f32[1,8192]{1,0:T(1,128)} custom-call(bf16[512,256]{1,0:T(8,128)(2,1)} %slice.10.t_ref, bf16[8192,256]{1,0:T(8,128)(2,1)} %fusion.2.c_ref, f32[512,1]{1,0:T(8,128)} %copy.27.a_ref), custom_call_target="tpu_custom_call" | custom-call | flops 2147483648 | bytes 4456448 | tf_op jit(solution)/shard_map/pallas_call | solution.py:75
  148.6 15.6 %all_to_all.91 = f32[64,1,128]{2,1,0:T(1,128)S(1)} all-to-all(f32[64,1,128]{2,1,0:T(1,128)} %bitcast.38), channel_id=1, replica_groups=mesh['proto'=4,'batch'=64] {'batch'}, dimensions={0} | all-to-all | bytes 65536 | tf_op jit(solution)/shard_map/all_to_all | solution.py:139
  164.9 4.6 %all-to-all-start.9 = ((f32[64,1,128]{2,1,0:T(1,128)}), f32[64,1,128]{2,1,0:T(1,128)S(1)}, u32[]{:S(2)}, u32[]{:S(2)}) async-start(f32[64,1,128]{2,1,0:T(1,128)} %broadcast_in_dim.50), calls=%async_computation.9 | async-start | bytes 65536 | tf_op jit(solution)/shard_map/all_to_all | solution.py:151
  169.5 9.3 %exponential_reduce_fusion = (f32[512]{0:T(512)S(1)}, f32[512,8192]{1,0:T(8,128)}) fusion(bf16[8192,256]{1,0:T(8,128)(2,1)} %fusion.2.c_ref, bf16[512,512]{1,0:T(8,128)(2,1)S(1)} %bitcast.28), kind=kOutput, calls=%fused_computation.1 | convolution fusion | flops 2155871744 | bytes 21235712 | tf_op jit(solution)/shard_map/dot_general | solution.py:186
  179.5 3.2 %all-to-all-start.1 = ((f32[4,1,512]{2,1,0:T(1,128)}), f32[4,1,512]{2,1,0:T(1,128)S(1)}, u32[]{:S(2)}, u32[]{:S(2)}) async-start(f32[4,1,512]{2,1,0:T(1,128)} %broadcast_in_dim.43), calls=%async_computation.1 | async-start | bytes 16384 | tf_op jit(solution)/shard_map/all_to_all | solution.py:151
  182.8 6.3 %shard_map.55 = f32[512,1]{1,0:T(8,128)} custom-call(bf16[512,256]{1,0:T(8,128)(2,1)} %slice.10.t_ref, bf16[8192,256]{1,0:T(8,128)(2,1)} %fusion.2.c_ref, f32[1,8192]{1,0:T(1,128)} %bitcast.31), custom_call_target="tpu_custom_call" | custom-call | flops 2147483648 | bytes 4456448 | tf_op jit(solution)/shard_map/pallas_call | solution.py:75
  189.1 1.1 reduce.9
  190.8 4.2 %all-to-all-start.10 = ((f32[4,1,512]{2,1,0:T(1,128)}), f32[4,1,512]{2,1,0:T(1,128)S(1)}, u32[]{:S(2)}, u32[]{:S(2)}) async-start(f32[4,1,512]{2,1,0:T(1,128)} %broadcast_in_dim.52), calls=%async_computation.10 | async-start | bytes 16384 | tf_op jit(solution)/shard_map/all_to_all | solution.py:151
  195.0 4.1 %all-to-all-done.10 = f32[4,1,512]{2,1,0:T(1,128)S(1)} async-done(((f32[4,1,512]{2,1,0:T(1,128)}), f32[4,1,512]{2,1,0:T(1,128)S(1)}, u32[]{:S(2)}, u32[]{:S(2)}) %all-to-all-start.10) | async-done | bytes 8224 | tf_op jit(solution)/shard_map/all_to_all | solution.py:151
  199.9 12.1 %all-to-all-start.11 = ((f32[64,512,2]{1,2,0:T(2,128)}), f32[64,512,2]{1,2,0:T(2,128)S(1)}, u32[]{:S(2)}, u32[]{:S(2)}) async-start(f32[64,512,2]{1,2,0:T(2,128)} %broadcast_in_dim.53), calls=%async_computation.11 | async-start | bytes 524288 | tf_op jit(solution)/shard_map/all_to_all | solution.py:151
  212.1 15.6 %fusion.4 = f32[512,256]{1,0:T(8,128)} fusion(bf16[8192,256]{1,0:T(8,128)(2,1)} %fusion.2.c_ref, f32[512,8192]{1,0:T(8,128)} %get-tuple-element.11, f32[8192]{0:T(1024)} %bitcast.32, f32[512]{0:T(512)S(1)} %get-tuple-element.6, f32[512]{0:T(512)S(1)} %log.14, bf16[512,512]{1,0:T(8,128)(2,1)S(1)} %bitcast.29), kind=kOutput, calls=%fused_computation.8 | convolution fusion | flops 4328652800 | bytes 25989120 | tf_op jit(solution)/shard_map/dot_general | solution.py:218
  227.7 3.5 %all-to-all-start.12 = ((f32[4,128,256]{2,1,0:T(8,128)}), f32[4,128,256]{2,1,0:T(8,128)S(1)}, u32[]{:S(2)}, u32[]{:S(2)}) async-start(f32[4,128,256]{2,1,0:T(8,128)} %bitcast.16), calls=%async_computation.12 | async-start | bytes 1048576 | tf_op jit(solution)/shard_map/all_to_all | solution.py:139
  231.2 1.5 constant_dynamic-slice_fusion.c_ref
  234.2 6.1 %all-to-all-done.12 = f32[4,128,256]{2,1,0:T(8,128)S(1)} async-done(((f32[4,128,256]{2,1,0:T(8,128)}), f32[4,128,256]{2,1,0:T(8,128)S(1)}, u32[]{:S(2)}, u32[]{:S(2)}) %all-to-all-start.12) | async-done | bytes 524320 | tf_op jit(solution)/shard_map/all_to_all | solution.py:139
  241.2 18.2 %shard_map.56 = f32[128,256]{1,0:T(8,128)} custom-call(bf16[32768,512]{1,0:T(8,128)(2,1)} %all-gather.2.cloned.1.call-done.ts_ref, bf16[128,256]{1,0:T(8,128)(2,1)} %constant_dynamic-slice_fusion.c_ref, f32[128,1]{1,0:T(8,128)} %copy.30.col_ref, f32[2,32768]{1,0:T(2,128)} %bitcast.30), custom_call_target="tpu_custom_call" | custom-call | flops 6442450944 | bytes 33685504 | tf_op jit(solution)/shard_map/pallas_call | solution.py:98
  259.4 1.6 broadcast_multiply_fusion
  (54 shorter events, 11.0 us)
Async XLA Ops:
  7.2 234.1 %all-gather.2.cloned.1.call-start = ((), (), s32[]{:S(2)}) async-start(), calls=%async_computation.13 | async-start | bytes 34078720 | tf_op jit(solution)/shard_map/all_gather | solution.py:226
  39.1 130.5 %copy-start = (bf16[4,128,512]{2,1,0:T(8,128)(2,1)S(1)}, bf16[4,128,512]{2,1,0:T(8,128)(2,1)}, u32[]{:S(2)}) copy-start(bf16[4,128,512]{2,1,0:T(8,128)(2,1)} %all_to_all.84) | copy-start | bytes 1572868
  164.9 14.0 %all-to-all-start.9 = ((f32[64,1,128]{2,1,0:T(1,128)}), f32[64,1,128]{2,1,0:T(1,128)S(1)}, u32[]{:S(2)}, u32[]{:S(2)}) async-start(f32[64,1,128]{2,1,0:T(1,128)} %broadcast_in_dim.50), calls=%async_computation.9 | async-start | bytes 65536 | tf_op jit(solution)/shard_map/all_to_all | solution.py:151
  178.9 3.9 %copy-start.3 = (f32[64,1,128]{2,1,0:T(1,128)}, f32[64,1,128]{2,1,0:T(1,128)S(1)}, u32[]{:S(2)}) copy-start(f32[64,1,128]{2,1,0:T(1,128)S(1)} %all-to-all-done.9) | copy-start | bytes 98308
  179.5 10.7 %all-to-all-start.1 = ((f32[4,1,512]{2,1,0:T(1,128)}), f32[4,1,512]{2,1,0:T(1,128)S(1)}, u32[]{:S(2)}, u32[]{:S(2)}) async-start(f32[4,1,512]{2,1,0:T(1,128)} %broadcast_in_dim.43), calls=%async_computation.1 | async-start | bytes 16384 | tf_op jit(solution)/shard_map/all_to_all | solution.py:151
  190.8 8.4 %all-to-all-start.10 = ((f32[4,1,512]{2,1,0:T(1,128)}), f32[4,1,512]{2,1,0:T(1,128)S(1)}, u32[]{:S(2)}, u32[]{:S(2)}) async-start(f32[4,1,512]{2,1,0:T(1,128)} %broadcast_in_dim.52), calls=%async_computation.10 | async-start | bytes 16384 | tf_op jit(solution)/shard_map/all_to_all | solution.py:151
  199.9 27.8 %all-to-all-start.11 = ((f32[64,512,2]{1,2,0:T(2,128)}), f32[64,512,2]{1,2,0:T(2,128)S(1)}, u32[]{:S(2)}, u32[]{:S(2)}) async-start(f32[64,512,2]{1,2,0:T(2,128)} %broadcast_in_dim.53), calls=%async_computation.11 | async-start | bytes 524288 | tf_op jit(solution)/shard_map/all_to_all | solution.py:151
  212.1 28.2 %copy-start.2 = (bf16[128,256]{1,0:T(8,128)(2,1)S(1)}, bf16[128,256]{1,0:T(8,128)(2,1)}, u32[]{:S(2)}) copy-start(bf16[128,256]{1,0:T(8,128)(2,1)} %param.4) | copy-start | bytes 196612
  227.7 13.5 %copy-start.1 = (f32[64,512,2]{1,2,0:T(2,128)}, f32[64,512,2]{1,2,0:T(2,128)S(1)}, u32[]{:S(2)}) copy-start(f32[64,512,2]{1,2,0:T(2,128)S(1)} %all-to-all-done.11) | copy-start | bytes 786436
  227.7 12.6 %all-to-all-start.12 = ((f32[4,128,256]{2,1,0:T(8,128)}), f32[4,128,256]{2,1,0:T(8,128)S(1)}, u32[]{:S(2)}, u32[]{:S(2)}) async-start(f32[4,128,256]{2,1,0:T(8,128)} %bitcast.16), calls=%async_computation.12 | async-start | bytes 1048576 | tf_op jit(solution)/shard_map/all_to_all | solution.py:139
Sparse Core Ops, SparseCore 0:
  23.2 147.4 all-gather.1

commit v9 on v8

--- a/solution.py
+++ b/solution.py
@@ -55,7 +55,7 @@
     out_ref[...] += jnp.sum(w * col_ref[...], axis=1, keepdims=True)
 
 
-def sweep(tn_group, cn, vec, by_column, block=2048):
+def sweep(tn_group, cn, vec, by_column, block=4096):
     rows, width = tn_group.shape
     count = cn.shape[0]
     specs = [
@@ -90,7 +90,7 @@
     return out.reshape(-1)
 
 
-def protos_grad(ts, c_mine, col_mine, al, rows_all, scale, block=8192, interpret=False):
+def protos_grad(ts, c_mine, col_mine, al, rows_all, scale, block=4096, interpret=False):
     n, w2 = ts.shape
     width = w2 // 2
     m = c_mine.shape[0]

time: 270 us -> 268 us (level)
  transfers between devices with their start and end apart: 6 -> 6, of which waited for: 2 -> 2; matrix products, arithmetic and copies ran while one was open for 18% -> 18% of each run, Pallas kernels for 14% -> 13%
where the time goes in v9:
time: 268 us; the launch traced here: 267 us
  blocking collectives  108 us (40%)
  Pallas kernels  54.8 us (20%)
  starting transfers between devices  27.7 us (10%)
  matrix products  24.9 us (9%)
  other arithmetic  16.7 us (6%)
  between operations  14.2 us (5%)
  waiting for transfers between devices  10.1 us (4%)
  local copies, waits for them, and re-layouts  9.79 us (4%)
    all_to_all x5, blocking collectives, copy_for_each(): return lax.all_to_all(copies, axis, split_axis=0, concat_axis=0, tiled=True)  54.3 us
    all_to_all x3, blocking collectives, summed_on_arrival(): lax.all_to_all(parts, axis, split_axis=0, concat_axis=0, tiled=True)  54.1 us
    pallas_call x6, Pallas kernels, sweep(): pl.pallas_call(kern, grid=(count // block,), in_specs=specs, out_specs=ou...  35.7 us
    all_to_all x4, starting transfers between devices, copy_for_each(): return lax.all_to_all(copies, axis, split_axis=0, concat_axis=0, tiled=True)  24.2 us
    pallas_call x1, Pallas kernels, protos_grad(): pl.pallas_call(kern, grid=(n // block,), in_specs=[pl.BlockSpec((block, w...  19.1 us
    dot_general x1, matrix products, per_device(): jnp.dot(grads, cn, preferred_element_type=jnp.float32) / student_temp  15.6 us
    dot_general x1, matrix products, against(): lax.dot_general(left, right, (((1,), (1,)), ((), ())), preferred_element_...  9.31 us
    all_to_all x1, waiting for transfers between devices, summed_on_arrival(): lax.all_to_all(parts, axis, split_axis=0, concat_axis=0, tiled=True)  5.91 us
  transfers between devices with their start and end apart: 6, of which 2 were waited for; matrix products, arithmetic and copies ran while one was open for 18% of the time, Pallas kernels for 13%

profile of v9, /device:TPU:1, one launch (start us, length us, event | category | flops | bytes accessed | tf_op | source)
XLA Modules:
  0.0 266.6 jit_solution(5178263755144156976)
XLA Ops:
  10.2 12.8 %all_to_all.84 = bf16[4,128,512]{2,1,0:T(8,128)(2,1)} all-to-all(bf16[4,128,512]{2,1,0:T(8,128)(2,1)S(1)} %broadcast_in_dim.42), channel_id=1, replica_groups=mesh['proto'=4,'batch'=64] {'proto'}, dimensions={0} | all-to-all | bytes 1048576 | tf_op jit(solution)/shard_map/all_to_all | solution.py:151
  23.0 3.3 %fusion = f32[8192]{0:T(1024)S(1)} fusion(bf16[8192,256]{1,0:T(8,128)(2,1)} %param.5), kind=kLoop, calls=%fused_computation.4 | loop fusion | flops 6283264 | bytes 4227072 | tf_op jit(solution)/shard_map/reduce_sum | solution.py:180
  26.4 4.2 %fusion.2.c_ref = bf16[8192,256]{1,0:T(8,128)(2,1)} fusion(bf16[8192,256]{1,0:T(8,128)(2,1)} %param.5, f32[8192]{0:T(1024)S(1)} %add_rsqrt_fusion), kind=kLoop, calls=%fused_computation.6 | loop fusion | flops 8388608 | bytes 8421376 | tf_op jit(solution)/shard_map/convert_element_type | solution.py:199
  30.6 1.7 slice.10.t_ref
  33.0 5.9 %shard_map.50 = f32[1,8192]{1,0:T(1,128)} custom-call(bf16[512,256]{1,0:T(8,128)(2,1)} %slice.10.t_ref, bf16[8192,256]{1,0:T(8,128)(2,1)} %fusion.2.c_ref, f32[512,1]{1,0:T(8,128)} %broadcast.157.a_ref), custom_call_target="tpu_custom_call" | custom-call | flops 2147483648 | bytes 4456448 | tf_op jit(solution)/shard_map/pallas_call | solution.py:75
  38.9 23.6 %all_to_all.85 = f32[64,1,128]{2,1,0:T(1,128)S(1)} all-to-all(f32[64,1,128]{2,1,0:T(1,128)} %bitcast.34), channel_id=1, replica_groups=mesh['proto'=4,'batch'=64] {'batch'}, dimensions={0} | all-to-all | bytes 65536 | tf_op jit(solution)/shard_map/all_to_all | solution.py:139
  62.7 14.0 %all_to_all.86 = f32[64,1,128]{2,1,0:T(1,128)} all-to-all(f32[64,1,128]{2,1,0:T(1,128)S(1)} %broadcast_in_dim.44), channel_id=1, replica_groups=mesh['proto'=4,'batch'=64] {'batch'}, dimensions={0} | all-to-all | bytes 65536 | tf_op jit(solution)/shard_map/all_to_all | solution.py:151
  76.6 6.0 %shard_map.51 = f32[512,1]{1,0:T(8,128)} custom-call(bf16[512,256]{1,0:T(8,128)(2,1)} %slice.10.t_ref, bf16[8192,256]{1,0:T(8,128)(2,1)} %fusion.2.c_ref, f32[1,8192]{1,0:T(1,128)} %bitcast.35), custom_call_target="tpu_custom_call" | custom-call | flops 2147483648 | bytes 4456448 | tf_op jit(solution)/shard_map/pallas_call | solution.py:75
  82.6 1.1 reduce.7
  83.7 6.6 %all_to_all.87 = f32[4,1,512]{2,1,0:T(1,128)S(1)} all-to-all(f32[4,1,512]{2,1,0:T(1,128)S(1)} %broadcast_in_dim.46), channel_id=1, replica_groups=mesh['proto'=4,'batch'=64] {'proto'}, dimensions={0} | all-to-all | bytes 16384 | tf_op jit(solution)/shard_map/all_to_all | solution.py:151
  91.2 5.9 %shard_map.52 = f32[1,8192]{1,0:T(1,128)} custom-call(bf16[512,256]{1,0:T(8,128)(2,1)} %slice.10.t_ref, bf16[8192,256]{1,0:T(8,128)(2,1)} %fusion.2.c_ref, f32[512,1]{1,0:T(8,128)} %copy.24.a_ref), custom_call_target="tpu_custom_call" | custom-call | flops 2147483648 | bytes 4456448 | tf_op jit(solution)/shard_map/pallas_call | solution.py:75
  97.1 15.0 %all_to_all.88 = f32[64,1,128]{2,1,0:T(1,128)S(1)} all-to-all(f32[64,1,128]{2,1,0:T(1,128)} %bitcast.36), channel_id=1, replica_groups=mesh['proto'=4,'batch'=64] {'batch'}, dimensions={0} | all-to-all | bytes 65536 | tf_op jit(solution)/shard_map/all_to_all | solution.py:139
  112.2 14.3 %all_to_all.89 = f32[64,1,128]{2,1,0:T(1,128)} all-to-all(f32[64,1,128]{2,1,0:T(1,128)S(1)} %broadcast_in_dim.47), channel_id=1, replica_groups=mesh['proto'=4,'batch'=64] {'batch'}, dimensions={0} | all-to-all | bytes 65536 | tf_op jit(solution)/shard_map/all_to_all | solution.py:151
  126.6 6.0 %shard_map.53 = f32[512,1]{1,0:T(8,128)} custom-call(bf16[512,256]{1,0:T(8,128)(2,1)} %slice.10.t_ref, bf16[8192,256]{1,0:T(8,128)(2,1)} %fusion.2.c_ref, f32[1,8192]{1,0:T(1,128)} %bitcast.37), custom_call_target="tpu_custom_call" | custom-call | flops 2147483648 | bytes 4456448 | tf_op jit(solution)/shard_map/pallas_call | solution.py:75
  132.5 1.1 reduce.8
  133.6 6.6 %all_to_all.90 = f32[4,1,512]{2,1,0:T(1,128)S(1)} all-to-all(f32[4,1,512]{2,1,0:T(1,128)S(1)} %broadcast_in_dim.49), channel_id=1, replica_groups=mesh['proto'=4,'batch'=64] {'proto'}, dimensions={0} | all-to-all | bytes 16384 | tf_op jit(solution)/shard_map/all_to_all | solution.py:151
  141.1 5.9 %shard_map.54 = f32[1,8192]{1,0:T(1,128)} custom-call(bf16[512,256]{1,0:T(8,128)(2,1)} %slice.10.t_ref, bf16[8192,256]{1,0:T(8,128)(2,1)} %fusion.2.c_ref, f32[512,1]{1,0:T(8,128)} %copy.27.a_ref), custom_call_target="tpu_custom_call" | custom-call | flops 2147483648 | bytes 4456448 | tf_op jit(solution)/shard_map/pallas_call | solution.py:75
  147.1 15.5 %all_to_all.91 = f32[64,1,128]{2,1,0:T(1,128)S(1)} all-to-all(f32[64,1,128]{2,1,0:T(1,128)} %bitcast.38), channel_id=1, replica_groups=mesh['proto'=4,'batch'=64] {'batch'}, dimensions={0} | all-to-all | bytes 65536 | tf_op jit(solution)/shard_map/all_to_all | solution.py:139
  163.3 4.6 %all-to-all-start.9 = ((f32[64,1,128]{2,1,0:T(1,128)}), f32[64,1,128]{2,1,0:T(1,128)S(1)}, u32[]{:S(2)}, u32[]{:S(2)}) async-start(f32[64,1,128]{2,1,0:T(1,128)} %broadcast_in_dim.50), calls=%async_computation.9 | async-start | bytes 65536 | tf_op jit(solution)/shard_map/all_to_all | solution.py:151
  167.9 9.3 %exponential_reduce_fusion = (f32[512]{0:T(512)S(1)}, f32[512,8192]{1,0:T(8,128)}) fusion(bf16[8192,256]{1,0:T(8,128)(2,1)} %fusion.2.c_ref, bf16[512,512]{1,0:T(8,128)(2,1)S(1)} %bitcast.28), kind=kOutput, calls=%fused_computation.1 | convolution fusion | flops 2155871744 | bytes 21235712 | tf_op jit(solution)/shard_map/dot_general | solution.py:186
  177.9 3.2 %all-to-all-start.1 = ((f32[4,1,512]{2,1,0:T(1,128)}), f32[4,1,512]{2,1,0:T(1,128)S(1)}, u32[]{:S(2)}, u32[]{:S(2)}) async-start(f32[4,1,512]{2,1,0:T(1,128)} %broadcast_in_dim.43), calls=%async_computation.1 | async-start | bytes 16384 | tf_op jit(solution)/shard_map/all_to_all | solution.py:151
  181.1 6.0 %shard_map.55 = f32[512,1]{1,0:T(8,128)} custom-call(bf16[512,256]{1,0:T(8,128)(2,1)} %slice.10.t_ref, bf16[8192,256]{1,0:T(8,128)(2,1)} %fusion.2.c_ref, f32[1,8192]{1,0:T(1,128)} %bitcast.31), custom_call_target="tpu_custom_call" | custom-call | flops 2147483648 | bytes 4456448 | tf_op jit(solution)/shard_map/pallas_call | solution.py:75
  187.2 1.1 reduce.9
  188.9 4.2 %all-to-all-start.10 = ((f32[4,1,512]{2,1,0:T(1,128)}), f32[4,1,512]{2,1,0:T(1,128)S(1)}, u32[]{:S(2)}, u32[]{:S(2)}) async-start(f32[4,1,512]{2,1,0:T(1,128)} %broadcast_in_dim.52), calls=%async_computation.10 | async-start | bytes 16384 | tf_op jit(solution)/shard_map/all_to_all | solution.py:151
  193.1 4.1 %all-to-all-done.10 = f32[4,1,512]{2,1,0:T(1,128)S(1)} async-done(((f32[4,1,512]{2,1,0:T(1,128)}), f32[4,1,512]{2,1,0:T(1,128)S(1)}, u32[]{:S(2)}, u32[]{:S(2)}) %all-to-all-start.10) | async-done | bytes 8224 | tf_op jit(solution)/shard_map/all_to_all | solution.py:151
  198.0 12.1 %all-to-all-start.11 = ((f32[64,512,2]{1,2,0:T(2,128)}), f32[64,512,2]{1,2,0:T(2,128)S(1)}, u32[]{:S(2)}, u32[]{:S(2)}) async-start(f32[64,512,2]{1,2,0:T(2,128)} %broadcast_in_dim.53), calls=%async_computation.11 | async-start | bytes 524288 | tf_op jit(solution)/shard_map/all_to_all | solution.py:151
  210.2 15.6 %fusion.4 = f32[512,256]{1,0:T(8,128)} fusion(bf16[8192,256]{1,0:T(8,128)(2,1)} %fusion.2.c_ref, f32[512,8192]{1,0:T(8,128)} %get-tuple-element.11, f32[8192]{0:T(1024)} %bitcast.32, f32[512]{0:T(512)S(1)} %get-tuple-element.6, f32[512]{0:T(512)S(1)} %log.14, bf16[512,512]{1,0:T(8,128)(2,1)S(1)} %bitcast.29), kind=kOutput, calls=%fused_computation.8 | convolution fusion | flops 4328652800 | bytes 25989120 | tf_op jit(solution)/shard_map/dot_general | solution.py:218
  225.8 3.5 %all-to-all-start.12 = ((f32[4,128,256]{2,1,0:T(8,128)}), f32[4,128,256]{2,1,0:T(8,128)S(1)}, u32[]{:S(2)}, u32[]{:S(2)}) async-start(f32[4,128,256]{2,1,0:T(8,128)} %bitcast.16), calls=%async_computation.12 | async-start | bytes 1048576 | tf_op jit(solution)/shard_map/all_to_all | solution.py:139
  229.3 1.5 constant_dynamic-slice_fusion.c_ref
  232.2 5.9 %all-to-all-done.12 = f32[4,128,256]{2,1,0:T(8,128)S(1)} async-done(((f32[4,128,256]{2,1,0:T(8,128)}), f32[4,128,256]{2,1,0:T(8,128)S(1)}, u32[]{:S(2)}, u32[]{:S(2)}) %all-to-all-start.12) | async-done | bytes 524320 | tf_op jit(solution)/shard_map/all_to_all | solution.py:139
  239.1 19.1 %shard_map.56 = f32[128,256]{1,0:T(8,128)} custom-call(bf16[32768,512]{1,0:T(8,128)(2,1)} %all-gather.2.cloned.1.call-done.ts_ref, bf16[128,256]{1,0:T(8,128)(2,1)} %constant_dynamic-slice_fusion.c_ref, f32[128,1]{1,0:T(8,128)} %copy.30.col_ref, f32[2,32768]{1,0:T(2,128)} %bitcast.30), custom_call_target="tpu_custom_call" | custom-call | flops 6442450944 | bytes 33685504 | tf_op jit(solution)/shard_map/pallas_call | solution.py:98
  258.2 1.6 broadcast_multiply_fusion
  (54 shorter events, 11.0 us)
Async XLA Ops:
  7.2 231.9 %all-gather.2.cloned.1.call-start = ((), (), s32[]{:S(2)}) async-start(), calls=%async_computation.13 | async-start | bytes 34078720 | tf_op jit(solution)/shard_map/all_gather | solution.py:226
  38.9 129.0 %copy-start = (bf16[4,128,512]{2,1,0:T(8,128)(2,1)S(1)}, bf16[4,128,512]{2,1,0:T(8,128)(2,1)}, u32[]{:S(2)}) copy-start(bf16[4,128,512]{2,1,0:T(8,128)(2,1)} %all_to_all.84) | copy-start | bytes 1572868
  163.3 14.0 %all-to-all-start.9 = ((f32[64,1,128]{2,1,0:T(1,128)}), f32[64,1,128]{2,1,0:T(1,128)S(1)}, u32[]{:S(2)}, u32[]{:S(2)}) async-start(f32[64,1,128]{2,1,0:T(1,128)} %broadcast_in_dim.50), calls=%async_computation.9 | async-start | bytes 65536 | tf_op jit(solution)/shard_map/all_to_all | solution.py:151
  177.3 3.9 %copy-start.3 = (f32[64,1,128]{2,1,0:T(1,128)}, f32[64,1,128]{2,1,0:T(1,128)S(1)}, u32[]{:S(2)}) copy-start(f32[64,1,128]{2,1,0:T(1,128)S(1)} %all-to-all-done.9) | copy-start | bytes 98308
  177.9 10.4 %all-to-all-start.1 = ((f32[4,1,512]{2,1,0:T(1,128)}), f32[4,1,512]{2,1,0:T(1,128)S(1)}, u32[]{:S(2)}, u32[]{:S(2)}) async-start(f32[4,1,512]{2,1,0:T(1,128)} %broadcast_in_dim.43), calls=%async_computation.1 | async-start | bytes 16384 | tf_op jit(solution)/shard_map/all_to_all | solution.py:151
  188.9 8.3 %all-to-all-start.10 = ((f32[4,1,512]{2,1,0:T(1,128)}), f32[4,1,512]{2,1,0:T(1,128)S(1)}, u32[]{:S(2)}, u32[]{:S(2)}) async-start(f32[4,1,512]{2,1,0:T(1,128)} %broadcast_in_dim.52), calls=%async_computation.10 | async-start | bytes 16384 | tf_op jit(solution)/shard_map/all_to_all | solution.py:151
  198.0 27.8 %all-to-all-start.11 = ((f32[64,512,2]{1,2,0:T(2,128)}), f32[64,512,2]{1,2,0:T(2,128)S(1)}, u32[]{:S(2)}, u32[]{:S(2)}) async-start(f32[64,512,2]{1,2,0:T(2,128)} %broadcast_in_dim.53), calls=%async_computation.11 | async-start | bytes 524288 | tf_op jit(solution)/shard_map/all_to_all | solution.py:151
  210.2 28.0 %copy-start.2 = (bf16[128,256]{1,0:T(8,128)(2,1)S(1)}, bf16[128,256]{1,0:T(8,128)(2,1)}, u32[]{:S(2)}) copy-start(bf16[128,256]{1,0:T(8,128)(2,1)} %param.4) | copy-start | bytes 196612
  225.8 13.3 %copy-start.1 = (f32[64,512,2]{1,2,0:T(2,128)}, f32[64,512,2]{1,2,0:T(2,128)S(1)}, u32[]{:S(2)}) copy-start(f32[64,512,2]{1,2,0:T(2,128)S(1)} %all-to-all-done.11) | copy-start | bytes 786436
  225.8 12.3 %all-to-all-start.12 = ((f32[4,128,256]{2,1,0:T(8,128)}), f32[4,128,256]{2,1,0:T(8,128)S(1)}, u32[]{:S(2)}, u32[]{:S(2)}) async-start(f32[4,128,256]{2,1,0:T(8,128)} %bitcast.16), calls=%async_computation.12 | async-start | bytes 1048576 | tf_op jit(solution)/shard_map/all_to_all | solution.py:139
Sparse Core Ops, SparseCore 0:
  23.2 147.2 all-gather.1

commit v10 on v9

--- a/solution.py
+++ b/solution.py
@@ -222,10 +222,11 @@
     col_mine = lax.dynamic_slice_in_dim(col_scale, offset, mine_rows, 0)
     both = gather_directly(jnp.stack([row_scale, logz], axis=1), "batch", 0)
     sn_partial, both = lax.optimization_barrier((sn_partial, both))
-    grad_sn = summed_on_arrival(sn_partial, "proto", 0)
     pieces = lax.all_gather(
         jnp.concatenate((tn_group, sn_group), axis=1), "batch", axis=0, tiled=True
     )
+    sn_partial, pieces = lax.optimization_barrier((sn_partial, pieces))
+    grad_sn = lax.psum_scatter(sn_partial, "proto", scatter_dimension=0, tiled=True)
     grad_protos = protos_grad(pieces, c_mine, col_mine, both.T, rows_all, scale)
     _, pull = jax.vjp(unit_rows, student.astype(jnp.float32))
     grad_student = pull(grad_sn)[0]

time: 268 us -> 261 us (0.974)
  waiting for transfers between devices: 10.1 us -> 4.22 us
  starting transfers between devices: 27.7 us -> 24.5 us
    all_to_all x1 -> x0, waiting for transfers between devices: 5.91 us -> none  [summed_on_arrival(): lax.all_to_all(parts, axis, split_axis=0, concat_axis=0, tiled=True)]
    all_to_all x1 -> x0, starting transfers between devices: 3.47 us -> none  [summed_on_arrival(): lax.all_to_all(parts, axis, split_axis=0, concat_axis=0, tiled=True)]
  transfers between devices with their start and end apart: 6 -> 6, of which waited for: 2 -> 1; matrix products, arithmetic and copies ran while one was open for 18% -> 18% of each run, Pallas kernels for 13% -> 21%
where the time goes in v10:
time: 261 us; the launch traced here: 259 us
  blocking collectives  108 us (41%)
  Pallas kernels  54.9 us (21%)
  matrix products  24.9 us (10%)
  starting transfers between devices  24.5 us (9%)
  other arithmetic  18.4 us (7%)
  between operations  14.2 us (5%)
  local copies, waits for them, and re-layouts  9.87 us (4%)
  waiting for transfers between devices  4.22 us (2%)
    all_to_all x5, blocking collectives, copy_for_each(): return lax.all_to_all(copies, axis, split_axis=0, concat_axis=0, tiled=True)  54.3 us
    all_to_all x3, blocking collectives, summed_on_arrival(): lax.all_to_all(parts, axis, split_axis=0, concat_axis=0, tiled=True)  54.1 us
    pallas_call x6, Pallas kernels, sweep(): pl.pallas_call(kern, grid=(count // block,), in_specs=specs, out_specs=ou...  35.7 us
    all_to_all x4, starting transfers between devices, copy_for_each(): return lax.all_to_all(copies, axis, split_axis=0, concat_axis=0, tiled=True)  24.2 us
    pallas_call x1, Pallas kernels, protos_grad(): pl.pallas_call(kern, grid=(n // block,), in_specs=[pl.BlockSpec((block, w...  19.2 us
    dot_general x1, matrix products, per_device(): jnp.dot(grads, cn, preferred_element_type=jnp.float32) / student_temp  15.6 us
    dot_general x1, matrix products, against(): lax.dot_general(left, right, (((1,), (1,)), ((), ())), preferred_element_...  9.31 us
    reduce_sum x3, other arithmetic, unit_rows(): jnp.mean(full * full, axis=1, keepdims=True) + 1e-06  5.24 us
  transfers between devices with their start and end apart: 6, of which 1 were waited for; matrix products, arithmetic and copies ran while one was open for 18% of the time, Pallas kernels for 21%

profile of v10, /device:TPU:1, one launch (start us, length us, event | category | flops | bytes accessed | tf_op | source)
XLA Modules:
  0.0 259.5 jit_solution(14361707136194336129)
XLA Ops:
  10.2 12.8 %all_to_all.79 = bf16[4,128,512]{2,1,0:T(8,128)(2,1)} all-to-all(bf16[4,128,512]{2,1,0:T(8,128)(2,1)S(1)} %broadcast_in_dim.42), channel_id=1, replica_groups=mesh['proto'=4,'batch'=64] {'proto'}, dimensions={0} | all-to-all | bytes 1048576 | tf_op jit(solution)/shard_map/all_to_all | solution.py:151
  23.0 3.3 %fusion = f32[8192]{0:T(1024)S(1)} fusion(bf16[8192,256]{1,0:T(8,128)(2,1)} %param.5), kind=kLoop, calls=%fused_computation.4 | loop fusion | flops 6283264 | bytes 4227072 | tf_op jit(solution)/shard_map/reduce_sum | solution.py:180
  26.4 4.2 %fusion.2.c_ref = bf16[8192,256]{1,0:T(8,128)(2,1)} fusion(bf16[8192,256]{1,0:T(8,128)(2,1)} %param.5, f32[8192]{0:T(1024)S(1)} %add_rsqrt_fusion), kind=kLoop, calls=%fused_computation.6 | loop fusion | flops 8388608 | bytes 8421376 | tf_op jit(solution)/shard_map/convert_element_type | solution.py:199
  30.6 1.7 slice.10.t_ref
  33.0 5.9 %shard_map.50 = f32[1,8192]{1,0:T(1,128)} custom-call(bf16[512,256]{1,0:T(8,128)(2,1)} %slice.10.t_ref, bf16[8192,256]{1,0:T(8,128)(2,1)} %fusion.2.c_ref, f32[512,1]{1,0:T(8,128)} %broadcast.157.a_ref), custom_call_target="tpu_custom_call" | custom-call | flops 2147483648 | bytes 4456448 | tf_op jit(solution)/shard_map/pallas_call | solution.py:75
  38.9 23.6 %all_to_all.80 = f32[64,1,128]{2,1,0:T(1,128)S(1)} all-to-all(f32[64,1,128]{2,1,0:T(1,128)} %bitcast.33), channel_id=1, replica_groups=mesh['proto'=4,'batch'=64] {'batch'}, dimensions={0} | all-to-all | bytes 65536 | tf_op jit(solution)/shard_map/all_to_all | solution.py:139
  62.7 14.0 %all_to_all.81 = f32[64,1,128]{2,1,0:T(1,128)} all-to-all(f32[64,1,128]{2,1,0:T(1,128)S(1)} %broadcast_in_dim.44), channel_id=1, replica_groups=mesh['proto'=4,'batch'=64] {'batch'}, dimensions={0} | all-to-all | bytes 65536 | tf_op jit(solution)/shard_map/all_to_all | solution.py:151
  76.6 6.0 %shard_map.51 = f32[512,1]{1,0:T(8,128)} custom-call(bf16[512,256]{1,0:T(8,128)(2,1)} %slice.10.t_ref, bf16[8192,256]{1,0:T(8,128)(2,1)} %fusion.2.c_ref, f32[1,8192]{1,0:T(1,128)} %bitcast.34), custom_call_target="tpu_custom_call" | custom-call | flops 2147483648 | bytes 4456448 | tf_op jit(solution)/shard_map/pallas_call | solution.py:75
  82.6 1.1 reduce.7
  83.7 6.6 %all_to_all.82 = f32[4,1,512]{2,1,0:T(1,128)S(1)} all-to-all(f32[4,1,512]{2,1,0:T(1,128)S(1)} %broadcast_in_dim.46), channel_id=1, replica_groups=mesh['proto'=4,'batch'=64] {'proto'}, dimensions={0} | all-to-all | bytes 16384 | tf_op jit(solution)/shard_map/all_to_all | solution.py:151
  91.2 5.9 %shard_map.52 = f32[1,8192]{1,0:T(1,128)} custom-call(bf16[512,256]{1,0:T(8,128)(2,1)} %slice.10.t_ref, bf16[8192,256]{1,0:T(8,128)(2,1)} %fusion.2.c_ref, f32[512,1]{1,0:T(8,128)} %copy.24.a_ref), custom_call_target="tpu_custom_call" | custom-call | flops 2147483648 | bytes 4456448 | tf_op jit(solution)/shard_map/pallas_call | solution.py:75
  97.1 15.0 %all_to_all.83 = f32[64,1,128]{2,1,0:T(1,128)S(1)} all-to-all(f32[64,1,128]{2,1,0:T(1,128)} %bitcast.35), channel_id=1, replica_groups=mesh['proto'=4,'batch'=64] {'batch'}, dimensions={0} | all-to-all | bytes 65536 | tf_op jit(solution)/shard_map/all_to_all | solution.py:139
  112.2 14.3 %all_to_all.84 = f32[64,1,128]{2,1,0:T(1,128)} all-to-all(f32[64,1,128]{2,1,0:T(1,128)S(1)} %broadcast_in_dim.47), channel_id=1, replica_groups=mesh['proto'=4,'batch'=64] {'batch'}, dimensions={0} | all-to-all | bytes 65536 | tf_op jit(solution)/shard_map/all_to_all | solution.py:151
  126.6 6.0 %shard_map.53 = f32[512,1]{1,0:T(8,128)} custom-call(bf16[512,256]{1,0:T(8,128)(2,1)} %slice.10.t_ref, bf16[8192,256]{1,0:T(8,128)(2,1)} %fusion.2.c_ref, f32[1,8192]{1,0:T(1,128)} %bitcast.36), custom_call_target="tpu_custom_call" | custom-call | flops 2147483648 | bytes 4456448 | tf_op jit(solution)/shard_map/pallas_call | solution.py:75
  132.5 1.1 reduce.8
  133.6 6.6 %all_to_all.85 = f32[4,1,512]{2,1,0:T(1,128)S(1)} all-to-all(f32[4,1,512]{2,1,0:T(1,128)S(1)} %broadcast_in_dim.49), channel_id=1, replica_groups=mesh['proto'=4,'batch'=64] {'proto'}, dimensions={0} | all-to-all | bytes 16384 | tf_op jit(solution)/shard_map/all_to_all | solution.py:151
  141.1 5.9 %shard_map.54 = f32[1,8192]{1,0:T(1,128)} custom-call(bf16[512,256]{1,0:T(8,128)(2,1)} %slice.10.t_ref, bf16[8192,256]{1,0:T(8,128)(2,1)} %fusion.2.c_ref, f32[512,1]{1,0:T(8,128)} %copy.27.a_ref), custom_call_target="tpu_custom_call" | custom-call | flops 2147483648 | bytes 4456448 | tf_op jit(solution)/shard_map/pallas_call | solution.py:75
  147.1 15.5 %all_to_all.86 = f32[64,1,128]{2,1,0:T(1,128)S(1)} all-to-all(f32[64,1,128]{2,1,0:T(1,128)} %bitcast.37), channel_id=1, replica_groups=mesh['proto'=4,'batch'=64] {'batch'}, dimensions={0} | all-to-all | bytes 65536 | tf_op jit(solution)/shard_map/all_to_all | solution.py:139
  163.3 4.6 %all-to-all-start.9 = ((f32[64,1,128]{2,1,0:T(1,128)}), f32[64,1,128]{2,1,0:T(1,128)S(1)}, u32[]{:S(2)}, u32[]{:S(2)}) async-start(f32[64,1,128]{2,1,0:T(1,128)} %broadcast_in_dim.50), calls=%async_computation.9 | async-start | bytes 65536 | tf_op jit(solution)/shard_map/all_to_all | solution.py:151
  167.9 9.3 %exponential_reduce_fusion = (f32[512]{0:T(512)S(1)}, f32[512,8192]{1,0:T(8,128)}) fusion(bf16[8192,256]{1,0:T(8,128)(2,1)} %fusion.2.c_ref, bf16[512,512]{1,0:T(8,128)(2,1)S(1)} %bitcast.27), kind=kOutput, calls=%fused_computation.1 | convolution fusion | flops 2155871744 | bytes 21235712 | tf_op jit(solution)/shard_map/dot_general | solution.py:186
  177.9 3.2 %all-to-all-start.1 = ((f32[4,1,512]{2,1,0:T(1,128)}), f32[4,1,512]{2,1,0:T(1,128)S(1)}, u32[]{:S(2)}, u32[]{:S(2)}) async-start(f32[4,1,512]{2,1,0:T(1,128)} %broadcast_in_dim.43), calls=%async_computation.1 | async-start | bytes 16384 | tf_op jit(solution)/shard_map/all_to_all | solution.py:151
  181.1 6.0 %shard_map.55 = f32[512,1]{1,0:T(8,128)} custom-call(bf16[512,256]{1,0:T(8,128)(2,1)} %slice.10.t_ref, bf16[8192,256]{1,0:T(8,128)(2,1)} %fusion.2.c_ref, f32[1,8192]{1,0:T(1,128)} %bitcast.30), custom_call_target="tpu_custom_call" | custom-call | flops 2147483648 | bytes 4456448 | tf_op jit(solution)/shard_map/pallas_call | solution.py:75
  187.2 1.1 reduce.9
  188.9 4.2 %all-to-all-start.10 = ((f32[4,1,512]{2,1,0:T(1,128)}), f32[4,1,512]{2,1,0:T(1,128)S(1)}, u32[]{:S(2)}, u32[]{:S(2)}) async-start(f32[4,1,512]{2,1,0:T(1,128)} %broadcast_in_dim.52), calls=%async_computation.10 | async-start | bytes 16384 | tf_op jit(solution)/shard_map/all_to_all | solution.py:151
  193.1 4.1 %all-to-all-done.10 = f32[4,1,512]{2,1,0:T(1,128)S(1)} async-done(((f32[4,1,512]{2,1,0:T(1,128)}), f32[4,1,512]{2,1,0:T(1,128)S(1)}, u32[]{:S(2)}, u32[]{:S(2)}) %all-to-all-start.10) | async-done | bytes 8224 | tf_op jit(solution)/shard_map/all_to_all | solution.py:151
  198.0 12.1 %all-to-all-start.11 = ((f32[64,512,2]{1,2,0:T(2,128)}), f32[64,512,2]{1,2,0:T(2,128)S(1)}, u32[]{:S(2)}, u32[]{:S(2)}) async-start(f32[64,512,2]{1,2,0:T(2,128)} %broadcast_in_dim.53), calls=%async_computation.11 | async-start | bytes 524288 | tf_op jit(solution)/shard_map/all_to_all | solution.py:151
  210.4 15.6 %fusion.4 = f32[512,256]{1,0:T(8,128)} fusion(bf16[8192,256]{1,0:T(8,128)(2,1)} %fusion.2.c_ref, f32[512,8192]{1,0:T(8,128)} %get-tuple-element.15, f32[8192]{0:T(1024)} %bitcast.31, f32[512]{0:T(512)S(1)} %get-tuple-element.10, f32[512]{0:T(512)S(1)} %log.14, bf16[512,512]{1,0:T(8,128)(2,1)S(1)} %bitcast.28), kind=kOutput, calls=%fused_computation.8 | convolution fusion | flops 4328652800 | bytes 25989120 | tf_op jit(solution)/shard_map/dot_general | solution.py:218
  226.1 1.5 constant_dynamic-slice_fusion.c_ref
  229.1 19.2 %shard_map.56 = f32[128,256]{1,0:T(8,128)} custom-call(bf16[32768,512]{1,0:T(8,128)(2,1)} %all-gather.2.cloned.1.call-done.ts_ref, bf16[128,256]{1,0:T(8,128)(2,1)} %constant_dynamic-slice_fusion.c_ref, f32[128,1]{1,0:T(8,128)} %copy.30.col_ref, f32[2,32768]{1,0:T(2,128)} %bitcast.29), custom_call_target="tpu_custom_call" | custom-call | flops 6442450944 | bytes 33685504 | tf_op jit(solution)/shard_map/pallas_call | solution.py:98
  248.4 1.6 broadcast_multiply_fusion
  249.9 1.0 fusion.13
  251.0 1.7 add_add_fusion
  (54 shorter events, 10.4 us)
Async XLA Ops:
  7.2 218.9 %all-gather.2.cloned.1.call-start = ((), (), s32[]{:S(2)}) async-start(), calls=%async_computation.13 | async-start | bytes 34078720 | tf_op jit(solution)/shard_map/all_gather | solution.py:225
  38.9 129.0 %copy-start = (bf16[4,128,512]{2,1,0:T(8,128)(2,1)S(1)}, bf16[4,128,512]{2,1,0:T(8,128)(2,1)}, u32[]{:S(2)}) copy-start(bf16[4,128,512]{2,1,0:T(8,128)(2,1)} %all_to_all.79) | copy-start | bytes 1572868
  163.3 14.0 %all-to-all-start.9 = ((f32[64,1,128]{2,1,0:T(1,128)}), f32[64,1,128]{2,1,0:T(1,128)S(1)}, u32[]{:S(2)}, u32[]{:S(2)}) async-start(f32[64,1,128]{2,1,0:T(1,128)} %broadcast_in_dim.50), calls=%async_computation.9 | async-start | bytes 65536 | tf_op jit(solution)/shard_map/all_to_all | solution.py:151
  177.3 3.9 %copy-start.3 = (f32[64,1,128]{2,1,0:T(1,128)}, f32[64,1,128]{2,1,0:T(1,128)S(1)}, u32[]{:S(2)}) copy-start(f32[64,1,128]{2,1,0:T(1,128)S(1)} %all-to-all-done.9) | copy-start | bytes 98308
  177.9 10.4 %all-to-all-start.1 = ((f32[4,1,512]{2,1,0:T(1,128)}), f32[4,1,512]{2,1,0:T(1,128)S(1)}, u32[]{:S(2)}, u32[]{:S(2)}) async-start(f32[4,1,512]{2,1,0:T(1,128)} %broadcast_in_dim.43), calls=%async_computation.1 | async-start | bytes 16384 | tf_op jit(solution)/shard_map/all_to_all | solution.py:151
  188.9 8.3 %all-to-all-start.10 = ((f32[4,1,512]{2,1,0:T(1,128)}), f32[4,1,512]{2,1,0:T(1,128)S(1)}, u32[]{:S(2)}, u32[]{:S(2)}) async-start(f32[4,1,512]{2,1,0:T(1,128)} %broadcast_in_dim.52), calls=%async_computation.10 | async-start | bytes 16384 | tf_op jit(solution)/shard_map/all_to_all | solution.py:151
  198.0 28.0 %all-to-all-start.11 = ((f32[64,512,2]{1,2,0:T(2,128)}), f32[64,512,2]{1,2,0:T(2,128)S(1)}, u32[]{:S(2)}, u32[]{:S(2)}) async-start(f32[64,512,2]{1,2,0:T(2,128)} %broadcast_in_dim.53), calls=%async_computation.11 | async-start | bytes 524288 | tf_op jit(solution)/shard_map/all_to_all | solution.py:151
  210.2 39.8 %reduce-scatter.2.cloned.1.call-start = ((), (), s32[]{:S(2)}) async-start(), calls=%async_computation.14 | async-start | bytes 655360 | tf_op jit(solution)/shard_map/reduce_scatter | solution.py:229
  226.1 3.1 %copy-start.1 = (f32[64,512,2]{1,2,0:T(2,128)}, f32[64,512,2]{1,2,0:T(2,128)S(1)}, u32[]{:S(2)}) copy-start(f32[64,512,2]{1,2,0:T(2,128)S(1)} %all-to-all-done.11) | copy-start | bytes 786436
  229.1 20.8 %copy-start.2 = (bf16[128,256]{1,0:T(8,128)(2,1)S(1)}, bf16[128,256]{1,0:T(8,128)(2,1)}, u32[]{:S(2)}) copy-start(bf16[128,256]{1,0:T(8,128)(2,1)} %param.4) | copy-start | bytes 196612
Sparse Core Ops, SparseCore 0:
  23.2 147.2 all-gather.1
  226.2 20.9 reduce-scatter.1

commit v11 on v10

--- a/solution.py
+++ b/solution.py
@@ -55,7 +55,7 @@
     out_ref[...] += jnp.sum(w * col_ref[...], axis=1, keepdims=True)
 
 
-def sweep(tn_group, cn, vec, by_column, block=4096):
+def sweep(tn_group, cn, vec, by_column, block=2048):
     rows, width = tn_group.shape
     count = cn.shape[0]
     specs = [

time: 261 us -> 263 us (level)
  transfers between devices with their start and end apart: 6 -> 6, of which waited for: 1 -> 1; matrix products, arithmetic and copies ran while one was open for 18% -> 18% of each run, Pallas kernels for 21% -> 22%
where the time goes in v11:
time: 263 us; the launch traced here: 261 us
  blocking collectives  108 us (41%)
  Pallas kernels  56.8 us (22%)
  matrix products  24.9 us (9%)
  starting transfers between devices  24.3 us (9%)
  other arithmetic  18.4 us (7%)
  between operations  14.2 us (5%)
  local copies, waits for them, and re-layouts  9.87 us (4%)
  waiting for transfers between devices  4.22 us (2%)
    all_to_all x5, blocking collectives, copy_for_each(): return lax.all_to_all(copies, axis, split_axis=0, concat_axis=0, tiled=True)  54.3 us
    all_to_all x3, blocking collectives, summed_on_arrival(): lax.all_to_all(parts, axis, split_axis=0, concat_axis=0, tiled=True)  54.1 us
    pallas_call x6, Pallas kernels, sweep(): pl.pallas_call(kern, grid=(count // block,), in_specs=specs, out_specs=ou...  37.6 us
    all_to_all x4, starting transfers between devices, copy_for_each(): return lax.all_to_all(copies, axis, split_axis=0, concat_axis=0, tiled=True)  24.2 us
    pallas_call x1, Pallas kernels, protos_grad(): pl.pallas_call(kern, grid=(n // block,), in_specs=[pl.BlockSpec((block, w...  19.2 us
    dot_general x1, matrix products, per_device(): jnp.dot(grads, cn, preferred_element_type=jnp.float32) / student_temp  15.6 us
    dot_general x1, matrix products, against(): lax.dot_general(left, right, (((1,), (1,)), ((), ())), preferred_element_...  9.31 us
  transfers between devices with their start and end apart: 6, of which 1 were waited for; matrix products, arithmetic and copies ran while one was open for 18% of the time, Pallas kernels for 22%

profile of v11, /device:TPU:1, one launch (start us, length us, event | category | flops | bytes accessed | tf_op | source)
XLA Modules:
  0.0 261.2 jit_solution(10710673633848033499)
XLA Ops:
  10.2 12.8 %all_to_all.79 = bf16[4,128,512]{2,1,0:T(8,128)(2,1)} all-to-all(bf16[4,128,512]{2,1,0:T(8,128)(2,1)S(1)} %broadcast_in_dim.42), channel_id=1, replica_groups=mesh['proto'=4,'batch'=64] {'proto'}, dimensions={0} | all-to-all | bytes 1048576 | tf_op jit(solution)/shard_map/all_to_all | solution.py:151
  23.0 3.3 %fusion = f32[8192]{0:T(1024)S(1)} fusion(bf16[8192,256]{1,0:T(8,128)(2,1)} %param.5), kind=kLoop, calls=%fused_computation.4 | loop fusion | flops 6283264 | bytes 4227072 | tf_op jit(solution)/shard_map/reduce_sum | solution.py:180
  26.4 4.2 %fusion.2.c_ref = bf16[8192,256]{1,0:T(8,128)(2,1)} fusion(bf16[8192,256]{1,0:T(8,128)(2,1)} %param.5, f32[8192]{0:T(1024)S(1)} %add_rsqrt_fusion), kind=kLoop, calls=%fused_computation.6 | loop fusion | flops 8388608 | bytes 8421376 | tf_op jit(solution)/shard_map/convert_element_type | solution.py:199
  30.6 1.7 slice.10.t_ref
  33.0 6.1 %shard_map.50 = f32[1,8192]{1,0:T(1,128)} custom-call(bf16[512,256]{1,0:T(8,128)(2,1)} %slice.10.t_ref, bf16[8192,256]{1,0:T(8,128)(2,1)} %fusion.2.c_ref, f32[512,1]{1,0:T(8,128)} %broadcast.157.a_ref), custom_call_target="tpu_custom_call" | custom-call | flops 2147483648 | bytes 4456448 | tf_op jit(solution)/shard_map/pallas_call | solution.py:75
  39.1 23.4 %all_to_all.80 = f32[64,1,128]{2,1,0:T(1,128)S(1)} all-to-all(f32[64,1,128]{2,1,0:T(1,128)} %bitcast.33), channel_id=1, replica_groups=mesh['proto'=4,'batch'=64] {'batch'}, dimensions={0} | all-to-all | bytes 65536 | tf_op jit(solution)/shard_map/all_to_all | solution.py:139
  62.6 14.0 %all_to_all.81 = f32[64,1,128]{2,1,0:T(1,128)} all-to-all(f32[64,1,128]{2,1,0:T(1,128)S(1)} %broadcast_in_dim.44), channel_id=1, replica_groups=mesh['proto'=4,'batch'=64] {'batch'}, dimensions={0} | all-to-all | bytes 65536 | tf_op jit(solution)/shard_map/all_to_all | solution.py:151
  76.6 6.6 %shard_map.51 = f32[512,1]{1,0:T(8,128)} custom-call(bf16[512,256]{1,0:T(8,128)(2,1)} %slice.10.t_ref, bf16[8192,256]{1,0:T(8,128)(2,1)} %fusion.2.c_ref, f32[1,8192]{1,0:T(1,128)} %bitcast.34), custom_call_target="tpu_custom_call" | custom-call | flops 2147483648 | bytes 4456448 | tf_op jit(solution)/shard_map/pallas_call | solution.py:75
  83.2 1.1 reduce.7
  84.3 6.6 %all_to_all.82 = f32[4,1,512]{2,1,0:T(1,128)S(1)} all-to-all(f32[4,1,512]{2,1,0:T(1,128)S(1)} %broadcast_in_dim.46), channel_id=1, replica_groups=mesh['proto'=4,'batch'=64] {'proto'}, dimensions={0} | all-to-all | bytes 16384 | tf_op jit(solution)/shard_map/all_to_all | solution.py:151
  91.8 6.1 %shard_map.52 = f32[1,8192]{1,0:T(1,128)} custom-call(bf16[512,256]{1,0:T(8,128)(2,1)} %slice.10.t_ref, bf16[8192,256]{1,0:T(8,128)(2,1)} %fusion.2.c_ref, f32[512,1]{1,0:T(8,128)} %copy.24.a_ref), custom_call_target="tpu_custom_call" | custom-call | flops 2147483648 | bytes 4456448 | tf_op jit(solution)/shard_map/pallas_call | solution.py:75
  97.9 15.1 %all_to_all.83 = f32[64,1,128]{2,1,0:T(1,128)S(1)} all-to-all(f32[64,1,128]{2,1,0:T(1,128)} %bitcast.35), channel_id=1, replica_groups=mesh['proto'=4,'batch'=64] {'batch'}, dimensions={0} | all-to-all | bytes 65536 | tf_op jit(solution)/shard_map/all_to_all | solution.py:139
  113.2 14.3 %all_to_all.84 = f32[64,1,128]{2,1,0:T(1,128)} all-to-all(f32[64,1,128]{2,1,0:T(1,128)S(1)} %broadcast_in_dim.47), channel_id=1, replica_groups=mesh['proto'=4,'batch'=64] {'batch'}, dimensions={0} | all-to-all | bytes 65536 | tf_op jit(solution)/shard_map/all_to_all | solution.py:151
  127.5 6.4 %shard_map.53 = f32[512,1]{1,0:T(8,128)} custom-call(bf16[512,256]{1,0:T(8,128)(2,1)} %slice.10.t_ref, bf16[8192,256]{1,0:T(8,128)(2,1)} %fusion.2.c_ref, f32[1,8192]{1,0:T(1,128)} %bitcast.36), custom_call_target="tpu_custom_call" | custom-call | flops 2147483648 | bytes 4456448 | tf_op jit(solution)/shard_map/pallas_call | solution.py:75
  133.9 1.1 reduce.8
  135.0 6.6 %all_to_all.85 = f32[4,1,512]{2,1,0:T(1,128)S(1)} all-to-all(f32[4,1,512]{2,1,0:T(1,128)S(1)} %broadcast_in_dim.49), channel_id=1, replica_groups=mesh['proto'=4,'batch'=64] {'proto'}, dimensions={0} | all-to-all | bytes 16384 | tf_op jit(solution)/shard_map/all_to_all | solution.py:151
  142.5 6.1 %shard_map.54 = f32[1,8192]{1,0:T(1,128)} custom-call(bf16[512,256]{1,0:T(8,128)(2,1)} %slice.10.t_ref, bf16[8192,256]{1,0:T(8,128)(2,1)} %fusion.2.c_ref, f32[512,1]{1,0:T(8,128)} %copy.27.a_ref), custom_call_target="tpu_custom_call" | custom-call | flops 2147483648 | bytes 4456448 | tf_op jit(solution)/shard_map/pallas_call | solution.py:75
  148.6 15.6 %all_to_all.86 = f32[64,1,128]{2,1,0:T(1,128)S(1)} all-to-all(f32[64,1,128]{2,1,0:T(1,128)} %bitcast.37), channel_id=1, replica_groups=mesh['proto'=4,'batch'=64] {'batch'}, dimensions={0} | all-to-all | bytes 65536 | tf_op jit(solution)/shard_map/all_to_all | solution.py:139
  164.9 4.6 %all-to-all-start.9 = ((f32[64,1,128]{2,1,0:T(1,128)}), f32[64,1,128]{2,1,0:T(1,128)S(1)}, u32[]{:S(2)}, u32[]{:S(2)}) async-start(f32[64,1,128]{2,1,0:T(1,128)} %broadcast_in_dim.50), calls=%async_computation.9 | async-start | bytes 65536 | tf_op jit(solution)/shard_map/all_to_all | solution.py:151
  169.5 9.3 %exponential_reduce_fusion = (f32[512]{0:T(512)S(1)}, f32[512,8192]{1,0:T(8,128)}) fusion(bf16[8192,256]{1,0:T(8,128)(2,1)} %fusion.2.c_ref, bf16[512,512]{1,0:T(8,128)(2,1)S(1)} %bitcast.27), kind=kOutput, calls=%fused_computation.1 | convolution fusion | flops 2155871744 | bytes 21235712 | tf_op jit(solution)/shard_map/dot_general | solution.py:186
  179.5 3.2 %all-to-all-start.1 = ((f32[4,1,512]{2,1,0:T(1,128)}), f32[4,1,512]{2,1,0:T(1,128)S(1)}, u32[]{:S(2)}, u32[]{:S(2)}) async-start(f32[4,1,512]{2,1,0:T(1,128)} %broadcast_in_dim.43), calls=%async_computation.1 | async-start | bytes 16384 | tf_op jit(solution)/shard_map/all_to_all | solution.py:151
  182.8 6.3 %shard_map.55 = f32[512,1]{1,0:T(8,128)} custom-call(bf16[512,256]{1,0:T(8,128)(2,1)} %slice.10.t_ref, bf16[8192,256]{1,0:T(8,128)(2,1)} %fusion.2.c_ref, f32[1,8192]{1,0:T(1,128)} %bitcast.30), custom_call_target="tpu_custom_call" | custom-call | flops 2147483648 | bytes 4456448 | tf_op jit(solution)/shard_map/pallas_call | solution.py:75
  189.1 1.1 reduce.9
  190.8 4.2 %all-to-all-start.10 = ((f32[4,1,512]{2,1,0:T(1,128)}), f32[4,1,512]{2,1,0:T(1,128)S(1)}, u32[]{:S(2)}, u32[]{:S(2)}) async-start(f32[4,1,512]{2,1,0:T(1,128)} %broadcast_in_dim.52), calls=%async_computation.10 | async-start | bytes 16384 | tf_op jit(solution)/shard_map/all_to_all | solution.py:151
  195.0 4.1 %all-to-all-done.10 = f32[4,1,512]{2,1,0:T(1,128)S(1)} async-done(((f32[4,1,512]{2,1,0:T(1,128)}), f32[4,1,512]{2,1,0:T(1,128)S(1)}, u32[]{:S(2)}, u32[]{:S(2)}) %all-to-all-start.10) | async-done | bytes 8224 | tf_op jit(solution)/shard_map/all_to_all | solution.py:151
  199.9 12.1 %all-to-all-start.11 = ((f32[64,512,2]{1,2,0:T(2,128)}), f32[64,512,2]{1,2,0:T(2,128)S(1)}, u32[]{:S(2)}, u32[]{:S(2)}) async-start(f32[64,512,2]{1,2,0:T(2,128)} %broadcast_in_dim.53), calls=%async_computation.11 | async-start | bytes 524288 | tf_op jit(solution)/shard_map/all_to_all | solution.py:151
  212.1 15.6 %fusion.4 = f32[512,256]{1,0:T(8,128)} fusion(bf16[8192,256]{1,0:T(8,128)(2,1)} %fusion.2.c_ref, f32[512,8192]{1,0:T(8,128)} %get-tuple-element.15, f32[8192]{0:T(1024)} %bitcast.31, f32[512]{0:T(512)S(1)} %get-tuple-element.10, f32[512]{0:T(512)S(1)} %log.14, bf16[512,512]{1,0:T(8,128)(2,1)S(1)} %bitcast.28), kind=kOutput, calls=%fused_computation.8 | convolution fusion | flops 4328652800 | bytes 25989120 | tf_op jit(solution)/shard_map/dot_general | solution.py:218
  227.8 1.5 constant_dynamic-slice_fusion.c_ref
  230.8 19.2 %shard_map.56 = f32[128,256]{1,0:T(8,128)} custom-call(bf16[32768,512]{1,0:T(8,128)(2,1)} %all-gather.2.cloned.1.call-done.ts_ref, bf16[128,256]{1,0:T(8,128)(2,1)} %constant_dynamic-slice_fusion.c_ref, f32[128,1]{1,0:T(8,128)} %copy.30.col_ref, f32[2,32768]{1,0:T(2,128)} %bitcast.29), custom_call_target="tpu_custom_call" | custom-call | flops 6442450944 | bytes 33685504 | tf_op jit(solution)/shard_map/pallas_call | solution.py:98
  250.1 1.6 broadcast_multiply_fusion
  251.6 1.0 fusion.13
  252.7 1.7 add_add_fusion
  (54 shorter events, 10.2 us)
Async XLA Ops:
  7.2 220.6 %all-gather.2.cloned.1.call-start = ((), (), s32[]{:S(2)}) async-start(), calls=%async_computation.13 | async-start | bytes 34078720 | tf_op jit(solution)/shard_map/all_gather | solution.py:225
  39.1 130.5 %copy-start = (bf16[4,128,512]{2,1,0:T(8,128)(2,1)S(1)}, bf16[4,128,512]{2,1,0:T(8,128)(2,1)}, u32[]{:S(2)}) copy-start(bf16[4,128,512]{2,1,0:T(8,128)(2,1)} %all_to_all.79) | copy-start | bytes 1572868
  164.9 14.0 %all-to-all-start.9 = ((f32[64,1,128]{2,1,0:T(1,128)}), f32[64,1,128]{2,1,0:T(1,128)S(1)}, u32[]{:S(2)}, u32[]{:S(2)}) async-start(f32[64,1,128]{2,1,0:T(1,128)} %broadcast_in_dim.50), calls=%async_computation.9 | async-start | bytes 65536 | tf_op jit(solution)/shard_map/all_to_all | solution.py:151
  178.9 3.9 %copy-start.3 = (f32[64,1,128]{2,1,0:T(1,128)}, f32[64,1,128]{2,1,0:T(1,128)S(1)}, u32[]{:S(2)}) copy-start(f32[64,1,128]{2,1,0:T(1,128)S(1)} %all-to-all-done.9) | copy-start | bytes 98308
  179.5 10.7 %all-to-all-start.1 = ((f32[4,1,512]{2,1,0:T(1,128)}), f32[4,1,512]{2,1,0:T(1,128)S(1)}, u32[]{:S(2)}, u32[]{:S(2)}) async-start(f32[4,1,512]{2,1,0:T(1,128)} %broadcast_in_dim.43), calls=%async_computation.1 | async-start | bytes 16384 | tf_op jit(solution)/shard_map/all_to_all | solution.py:151
  190.8 8.4 %all-to-all-start.10 = ((f32[4,1,512]{2,1,0:T(1,128)}), f32[4,1,512]{2,1,0:T(1,128)S(1)}, u32[]{:S(2)}, u32[]{:S(2)}) async-start(f32[4,1,512]{2,1,0:T(1,128)} %broadcast_in_dim.52), calls=%async_computation.10 | async-start | bytes 16384 | tf_op jit(solution)/shard_map/all_to_all | solution.py:151
  199.9 27.8 %all-to-all-start.11 = ((f32[64,512,2]{1,2,0:T(2,128)}), f32[64,512,2]{1,2,0:T(2,128)S(1)}, u32[]{:S(2)}, u32[]{:S(2)}) async-start(f32[64,512,2]{1,2,0:T(2,128)} %broadcast_in_dim.53), calls=%async_computation.11 | async-start | bytes 524288 | tf_op jit(solution)/shard_map/all_to_all | solution.py:151
  212.1 39.6 %reduce-scatter.2.cloned.1.call-start = ((), (), s32[]{:S(2)}) async-start(), calls=%async_computation.14 | async-start | bytes 655360 | tf_op jit(solution)/shard_map/reduce_scatter | solution.py:229
  227.8 3.1 %copy-start.1 = (f32[64,512,2]{1,2,0:T(2,128)}, f32[64,512,2]{1,2,0:T(2,128)S(1)}, u32[]{:S(2)}) copy-start(f32[64,512,2]{1,2,0:T(2,128)S(1)} %all-to-all-done.11) | copy-start | bytes 786436
  230.8 20.8 %copy-start.2 = (bf16[128,256]{1,0:T(8,128)(2,1)S(1)}, bf16[128,256]{1,0:T(8,128)(2,1)}, u32[]{:S(2)}) copy-start(bf16[128,256]{1,0:T(8,128)(2,1)} %param.4) | copy-start | bytes 196612
Sparse Core Ops, SparseCore 0:
  23.2 147.4 all-gather.1
  227.9 20.9 reduce-scatter.1

commit v12 on v10

--- a/solution.py
+++ b/solution.py
@@ -90,7 +90,7 @@
     return out.reshape(-1)
 
 
-def protos_grad(ts, c_mine, col_mine, al, rows_all, scale, block=4096, interpret=False):
+def protos_grad(ts, c_mine, col_mine, al, rows_all, scale, block=8192, interpret=False):
     n, w2 = ts.shape
     width = w2 // 2
     m = c_mine.shape[0]

time: 261 us -> 260 us (level)
  no operation moved by 1% of the time
where the time goes in v12:
time: 260 us; the launch traced here: 258 us
  blocking collectives  108 us (42%)
  Pallas kernels  53.9 us (21%)
  matrix products  24.9 us (10%)
  starting transfers between devices  24.5 us (9%)
  other arithmetic  18.4 us (7%)
  between operations  14.2 us (5%)
  local copies, waits for them, and re-layouts  9.87 us (4%)
  waiting for transfers between devices  4.22 us (2%)
    all_to_all x5, blocking collectives, copy_for_each(): return lax.all_to_all(copies, axis, split_axis=0, concat_axis=0, tiled=True)  54.3 us
    all_to_all x3, blocking collectives, summed_on_arrival(): lax.all_to_all(parts, axis, split_axis=0, concat_axis=0, tiled=True)  54.1 us
    pallas_call x6, Pallas kernels, sweep(): pl.pallas_call(kern, grid=(count // block,), in_specs=specs, out_specs=ou...  35.7 us
    all_to_all x4, starting transfers between devices, copy_for_each(): return lax.all_to_all(copies, axis, split_axis=0, concat_axis=0, tiled=True)  24.2 us
    pallas_call x1, Pallas kernels, protos_grad(): pl.pallas_call(kern, grid=(n // block,), in_specs=[pl.BlockSpec((block, w...  18.2 us
    dot_general x1, matrix products, per_device(): jnp.dot(grads, cn, preferred_element_type=jnp.float32) / student_temp  15.6 us
    dot_general x1, matrix products, against(): lax.dot_general(left, right, (((1,), (1,)), ((), ())), preferred_element_...  9.31 us
    reduce_sum x3, other arithmetic, unit_rows(): jnp.mean(full * full, axis=1, keepdims=True) + 1e-06  5.24 us
  transfers between devices with their start and end apart: 6, of which 1 were waited for; matrix products, arithmetic and copies ran while one was open for 18% of the time, Pallas kernels for 21%

profile of v12, /device:TPU:1, one launch (start us, length us, event | category | flops | bytes accessed | tf_op | source)
XLA Modules:
  0.0 258.5 jit_solution(9264192918238511506)
XLA Ops:
  10.2 12.8 %all_to_all.79 = bf16[4,128,512]{2,1,0:T(8,128)(2,1)} all-to-all(bf16[4,128,512]{2,1,0:T(8,128)(2,1)S(1)} %broadcast_in_dim.42), channel_id=1, replica_groups=mesh['proto'=4,'batch'=64] {'proto'}, dimensions={0} | all-to-all | bytes 1048576 | tf_op jit(solution)/shard_map/all_to_all | solution.py:151
  23.0 3.3 %fusion = f32[8192]{0:T(1024)S(1)} fusion(bf16[8192,256]{1,0:T(8,128)(2,1)} %param.5), kind=kLoop, calls=%fused_computation.4 | loop fusion | flops 6283264 | bytes 4227072 | tf_op jit(solution)/shard_map/reduce_sum | solution.py:180
  26.4 4.2 %fusion.2.c_ref = bf16[8192,256]{1,0:T(8,128)(2,1)} fusion(bf16[8192,256]{1,0:T(8,128)(2,1)} %param.5, f32[8192]{0:T(1024)S(1)} %add_rsqrt_fusion), kind=kLoop, calls=%fused_computation.6 | loop fusion | flops 8388608 | bytes 8421376 | tf_op jit(solution)/shard_map/convert_element_type | solution.py:199
  30.6 1.7 slice.10.t_ref
  33.0 5.9 %shard_map.50 = f32[1,8192]{1,0:T(1,128)} custom-call(bf16[512,256]{1,0:T(8,128)(2,1)} %slice.10.t_ref, bf16[8192,256]{1,0:T(8,128)(2,1)} %fusion.2.c_ref, f32[512,1]{1,0:T(8,128)} %broadcast.157.a_ref), custom_call_target="tpu_custom_call" | custom-call | flops 2147483648 | bytes 4456448 | tf_op jit(solution)/shard_map/pallas_call | solution.py:75
  38.9 23.6 %all_to_all.80 = f32[64,1,128]{2,1,0:T(1,128)S(1)} all-to-all(f32[64,1,128]{2,1,0:T(1,128)} %bitcast.33), channel_id=1, replica_groups=mesh['proto'=4,'batch'=64] {'batch'}, dimensions={0} | all-to-all | bytes 65536 | tf_op jit(solution)/shard_map/all_to_all | solution.py:139
  62.7 14.0 %all_to_all.81 = f32[64,1,128]{2,1,0:T(1,128)} all-to-all(f32[64,1,128]{2,1,0:T(1,128)S(1)} %broadcast_in_dim.44), channel_id=1, replica_groups=mesh['proto'=4,'batch'=64] {'batch'}, dimensions={0} | all-to-all | bytes 65536 | tf_op jit(solution)/shard_map/all_to_all | solution.py:151
  76.6 6.0 %shard_map.51 = f32[512,1]{1,0:T(8,128)} custom-call(bf16[512,256]{1,0:T(8,128)(2,1)} %slice.10.t_ref, bf16[8192,256]{1,0:T(8,128)(2,1)} %fusion.2.c_ref, f32[1,8192]{1,0:T(1,128)} %bitcast.34), custom_call_target="tpu_custom_call" | custom-call | flops 2147483648 | bytes 4456448 | tf_op jit(solution)/shard_map/pallas_call | solution.py:75
  82.6 1.1 reduce.7
  83.7 6.6 %all_to_all.82 = f32[4,1,512]{2,1,0:T(1,128)S(1)} all-to-all(f32[4,1,512]{2,1,0:T(1,128)S(1)} %broadcast_in_dim.46), channel_id=1, replica_groups=mesh['proto'=4,'batch'=64] {'proto'}, dimensions={0} | all-to-all | bytes 16384 | tf_op jit(solution)/shard_map/all_to_all | solution.py:151
  91.2 5.9 %shard_map.52 = f32[1,8192]{1,0:T(1,128)} custom-call(bf16[512,256]{1,0:T(8,128)(2,1)} %slice.10.t_ref, bf16[8192,256]{1,0:T(8,128)(2,1)} %fusion.2.c_ref, f32[512,1]{1,0:T(8,128)} %copy.24.a_ref), custom_call_target="tpu_custom_call" | custom-call | flops 2147483648 | bytes 4456448 | tf_op jit(solution)/shard_map/pallas_call | solution.py:75
  97.1 15.0 %all_to_all.83 = f32[64,1,128]{2,1,0:T(1,128)S(1)} all-to-all(f32[64,1,128]{2,1,0:T(1,128)} %bitcast.35), channel_id=1, replica_groups=mesh['proto'=4,'batch'=64] {'batch'}, dimensions={0} | all-to-all | bytes 65536 | tf_op jit(solution)/shard_map/all_to_all | solution.py:139
  112.2 14.3 %all_to_all.84 = f32[64,1,128]{2,1,0:T(1,128)} all-to-all(f32[64,1,128]{2,1,0:T(1,128)S(1)} %broadcast_in_dim.47), channel_id=1, replica_groups=mesh['proto'=4,'batch'=64] {'batch'}, dimensions={0} | all-to-all | bytes 65536 | tf_op jit(solution)/shard_map/all_to_all | solution.py:151
  126.6 6.0 %shard_map.53 = f32[512,1]{1,0:T(8,128)} custom-call(bf16[512,256]{1,0:T(8,128)(2,1)} %slice.10.t_ref, bf16[8192,256]{1,0:T(8,128)(2,1)} %fusion.2.c_ref, f32[1,8192]{1,0:T(1,128)} %bitcast.36), custom_call_target="tpu_custom_call" | custom-call | flops 2147483648 | bytes 4456448 | tf_op jit(solution)/shard_map/pallas_call | solution.py:75
  132.5 1.1 reduce.8
  133.6 6.6 %all_to_all.85 = f32[4,1,512]{2,1,0:T(1,128)S(1)} all-to-all(f32[4,1,512]{2,1,0:T(1,128)S(1)} %broadcast_in_dim.49), channel_id=1, replica_groups=mesh['proto'=4,'batch'=64] {'proto'}, dimensions={0} | all-to-all | bytes 16384 | tf_op jit(solution)/shard_map/all_to_all | solution.py:151
  141.1 5.9 %shard_map.54 = f32[1,8192]{1,0:T(1,128)} custom-call(bf16[512,256]{1,0:T(8,128)(2,1)} %slice.10.t_ref, bf16[8192,256]{1,0:T(8,128)(2,1)} %fusion.2.c_ref, f32[512,1]{1,0:T(8,128)} %copy.27.a_ref), custom_call_target="tpu_custom_call" | custom-call | flops 2147483648 | bytes 4456448 | tf_op jit(solution)/shard_map/pallas_call | solution.py:75
  147.1 15.5 %all_to_all.86 = f32[64,1,128]{2,1,0:T(1,128)S(1)} all-to-all(f32[64,1,128]{2,1,0:T(1,128)} %bitcast.37), channel_id=1, replica_groups=mesh['proto'=4,'batch'=64] {'batch'}, dimensions={0} | all-to-all | bytes 65536 | tf_op jit(solution)/shard_map/all_to_all | solution.py:139
  163.3 4.6 %all-to-all-start.9 = ((f32[64,1,128]{2,1,0:T(1,128)}), f32[64,1,128]{2,1,0:T(1,128)S(1)}, u32[]{:S(2)}, u32[]{:S(2)}) async-start(f32[64,1,128]{2,1,0:T(1,128)} %broadcast_in_dim.50), calls=%async_computation.9 | async-start | bytes 65536 | tf_op jit(solution)/shard_map/all_to_all | solution.py:151
  167.9 9.3 %exponential_reduce_fusion = (f32[512]{0:T(512)S(1)}, f32[512,8192]{1,0:T(8,128)}) fusion(bf16[8192,256]{1,0:T(8,128)(2,1)} %fusion.2.c_ref, bf16[512,512]{1,0:T(8,128)(2,1)S(1)} %bitcast.27), kind=kOutput, calls=%fused_computation.1 | convolution fusion | flops 2155871744 | bytes 21235712 | tf_op jit(solution)/shard_map/dot_general | solution.py:186
  177.9 3.2 %all-to-all-start.1 = ((f32[4,1,512]{2,1,0:T(1,128)}), f32[4,1,512]{2,1,0:T(1,128)S(1)}, u32[]{:S(2)}, u32[]{:S(2)}) async-start(f32[4,1,512]{2,1,0:T(1,128)} %broadcast_in_dim.43), calls=%async_computation.1 | async-start | bytes 16384 | tf_op jit(solution)/shard_map/all_to_all | solution.py:151
  181.1 6.0 %shard_map.55 = f32[512,1]{1,0:T(8,128)} custom-call(bf16[512,256]{1,0:T(8,128)(2,1)} %slice.10.t_ref, bf16[8192,256]{1,0:T(8,128)(2,1)} %fusion.2.c_ref, f32[1,8192]{1,0:T(1,128)} %bitcast.30), custom_call_target="tpu_custom_call" | custom-call | flops 2147483648 | bytes 4456448 | tf_op jit(solution)/shard_map/pallas_call | solution.py:75
  187.2 1.1 reduce.9
  188.9 4.2 %all-to-all-start.10 = ((f32[4,1,512]{2,1,0:T(1,128)}), f32[4,1,512]{2,1,0:T(1,128)S(1)}, u32[]{:S(2)}, u32[]{:S(2)}) async-start(f32[4,1,512]{2,1,0:T(1,128)} %broadcast_in_dim.52), calls=%async_computation.10 | async-start | bytes 16384 | tf_op jit(solution)/shard_map/all_to_all | solution.py:151
  193.1 4.1 %all-to-all-done.10 = f32[4,1,512]{2,1,0:T(1,128)S(1)} async-done(((f32[4,1,512]{2,1,0:T(1,128)}), f32[4,1,512]{2,1,0:T(1,128)S(1)}, u32[]{:S(2)}, u32[]{:S(2)}) %all-to-all-start.10) | async-done | bytes 8224 | tf_op jit(solution)/shard_map/all_to_all | solution.py:151
  198.0 12.1 %all-to-all-start.11 = ((f32[64,512,2]{1,2,0:T(2,128)}), f32[64,512,2]{1,2,0:T(2,128)S(1)}, u32[]{:S(2)}, u32[]{:S(2)}) async-start(f32[64,512,2]{1,2,0:T(2,128)} %broadcast_in_dim.53), calls=%async_computation.11 | async-start | bytes 524288 | tf_op jit(solution)/shard_map/all_to_all | solution.py:151
  210.4 15.6 %fusion.4 = f32[512,256]{1,0:T(8,128)} fusion(bf16[8192,256]{1,0:T(8,128)(2,1)} %fusion.2.c_ref, f32[512,8192]{1,0:T(8,128)} %get-tuple-element.15, f32[8192]{0:T(1024)} %bitcast.31, f32[512]{0:T(512)S(1)} %get-tuple-element.10, f32[512]{0:T(512)S(1)} %log.14, bf16[512,512]{1,0:T(8,128)(2,1)S(1)} %bitcast.28), kind=kOutput, calls=%fused_computation.8 | convolution fusion | flops 4328652800 | bytes 25989120 | tf_op jit(solution)/shard_map/dot_general | solution.py:218
  226.1 1.5 constant_dynamic-slice_fusion.c_ref
  229.1 18.2 %shard_map.56 = f32[128,256]{1,0:T(8,128)} custom-call(bf16[32768,512]{1,0:T(8,128)(2,1)} %all-gather.2.cloned.1.call-done.ts_ref, bf16[128,256]{1,0:T(8,128)(2,1)} %constant_dynamic-slice_fusion.c_ref, f32[128,1]{1,0:T(8,128)} %copy.30.col_ref, f32[2,32768]{1,0:T(2,128)} %bitcast.29), custom_call_target="tpu_custom_call" | custom-call | flops 6442450944 | bytes 33685504 | tf_op jit(solution)/shard_map/pallas_call | solution.py:98
  247.4 1.6 broadcast_multiply_fusion
  248.9 1.0 fusion.13
  250.0 1.7 add_add_fusion
  (54 shorter events, 10.4 us)
Async XLA Ops:
  7.2 218.9 %all-gather.2.cloned.1.call-start = ((), (), s32[]{:S(2)}) async-start(), calls=%async_computation.13 | async-start | bytes 34078720 | tf_op jit(solution)/shard_map/all_gather | solution.py:225
  38.9 129.0 %copy-start = (bf16[4,128,512]{2,1,0:T(8,128)(2,1)S(1)}, bf16[4,128,512]{2,1,0:T(8,128)(2,1)}, u32[]{:S(2)}) copy-start(bf16[4,128,512]{2,1,0:T(8,128)(2,1)} %all_to_all.79) | copy-start | bytes 1572868
  163.3 14.0 %all-to-all-start.9 = ((f32[64,1,128]{2,1,0:T(1,128)}), f32[64,1,128]{2,1,0:T(1,128)S(1)}, u32[]{:S(2)}, u32[]{:S(2)}) async-start(f32[64,1,128]{2,1,0:T(1,128)} %broadcast_in_dim.50), calls=%async_computation.9 | async-start | bytes 65536 | tf_op jit(solution)/shard_map/all_to_all | solution.py:151
  177.3 3.9 %copy-start.3 = (f32[64,1,128]{2,1,0:T(1,128)}, f32[64,1,128]{2,1,0:T(1,128)S(1)}, u32[]{:S(2)}) copy-start(f32[64,1,128]{2,1,0:T(1,128)S(1)} %all-to-all-done.9) | copy-start | bytes 98308
  177.9 10.4 %all-to-all-start.1 = ((f32[4,1,512]{2,1,0:T(1,128)}), f32[4,1,512]{2,1,0:T(1,128)S(1)}, u32[]{:S(2)}, u32[]{:S(2)}) async-start(f32[4,1,512]{2,1,0:T(1,128)} %broadcast_in_dim.43), calls=%async_computation.1 | async-start | bytes 16384 | tf_op jit(solution)/shard_map/all_to_all | solution.py:151
  188.9 8.3 %all-to-all-start.10 = ((f32[4,1,512]{2,1,0:T(1,128)}), f32[4,1,512]{2,1,0:T(1,128)S(1)}, u32[]{:S(2)}, u32[]{:S(2)}) async-start(f32[4,1,512]{2,1,0:T(1,128)} %broadcast_in_dim.52), calls=%async_computation.10 | async-start | bytes 16384 | tf_op jit(solution)/shard_map/all_to_all | solution.py:151
  198.0 28.0 %all-to-all-start.11 = ((f32[64,512,2]{1,2,0:T(2,128)}), f32[64,512,2]{1,2,0:T(2,128)S(1)}, u32[]{:S(2)}, u32[]{:S(2)}) async-start(f32[64,512,2]{1,2,0:T(2,128)} %broadcast_in_dim.53), calls=%async_computation.11 | async-start | bytes 524288 | tf_op jit(solution)/shard_map/all_to_all | solution.py:151
  210.2 38.8 %reduce-scatter.2.cloned.1.call-start = ((), (), s32[]{:S(2)}) async-start(), calls=%async_computation.14 | async-start | bytes 655360 | tf_op jit(solution)/shard_map/reduce_scatter | solution.py:229
  226.1 3.1 %copy-start.1 = (f32[64,512,2]{1,2,0:T(2,128)}, f32[64,512,2]{1,2,0:T(2,128)S(1)}, u32[]{:S(2)}) copy-start(f32[64,512,2]{1,2,0:T(2,128)S(1)} %all-to-all-done.11) | copy-start | bytes 786436
  229.1 19.8 %copy-start.2 = (bf16[128,256]{1,0:T(8,128)(2,1)S(1)}, bf16[128,256]{1,0:T(8,128)(2,1)}, u32[]{:S(2)}) copy-start(bf16[128,256]{1,0:T(8,128)(2,1)} %param.4) | copy-start | bytes 196612
Sparse Core Ops, SparseCore 0:
  23.2 147.2 all-gather.1
  226.2 20.9 reduce-scatter.1
